TPU v7x, 256 devices: a whole 4x4x8 slice. The times are simulated.
256 devices in a mesh: rows: 64 (over z, y, x_hi), cent: 4 (over x_lo, core).
Axes of the slice: x: 4 (x_hi: 2, x_lo: 2; x = x_hi * 2 + x_lo), y: 4, z: 8, core: 2. Of those that a mesh axis runs over, the one named last changes fastest.
Arguments:
- embeddings: bfloat16 [131072, 4096], P('rows', 'cent'), may hold values from -6 to 6
- basis: bfloat16 [4096, 512], P('cent'), may hold values from -0.09375 to 0.09375
- start_centroids: float32 [4096, 512], P('cent'), as said below
Outputs:
- centroids: float32 [4096, 512], P('cent')
- log_total: float32 [131072], P('rows')
Inputs may be any that keep to these rules, and one draw needn't show every extreme that they name: `start_centroids`: initial centroids, real-valued; some may lie far from the others.
All inputs are finite; a program needn't handle non-finite values.
Results may differ from a plain program's by a relative error of at most 0.0024.
The roundings to bfloat16 on the way count: a program that leaves them out, or rounds other values in their place, can miss the bound.
Values may be sent and summed in bfloat16 or wider, within the bound.
No kernel may reach another device: no remote copies, remote signals or barrier semaphores. Data moves between devices by JAX's collectives and lax.ppermute only.
A program may use at most 64 MiB of HBM per device.

v0:
```python
import jax
import jax.numpy as jnp
from jax import lax
from jax.sharding import PartitionSpec as P

ITERS = 2


TEMPER = 8.0


def on_device(embeddings, basis, start_centroids):
    row_count = embeddings.shape[0]
    proj_share = lax.psum_scatter(
        jnp.dot(embeddings, basis, preferred_element_type=jnp.float32),
        "cent",
        scatter_dimension=0,
        tiled=True,
    )
    projected = lax.all_gather(proj_share.astype(jnp.bfloat16), "cent", axis=0, tiled=True)
    centroids = start_centroids
    log_total = jnp.zeros((row_count,), jnp.float32)
    for step in range(ITERS):
        cent_bf = centroids.astype(jnp.bfloat16)
        scores = (
            lax.dot_general(
                projected, cent_bf, (((1,), (1,)), ((), ())), preferred_element_type=jnp.float32
            )
            / TEMPER
        )
        local_top = jnp.max(scores, axis=1)
        top = lax.pmax(local_top, "cent")
        total = lax.psum(jnp.sum(jnp.exp(scores - top[:, None]), axis=1), "cent")
        log_total = top + jnp.log(total)
        weights = jnp.exp(scores - log_total[:, None])
        local_mass = jnp.sum(weights, axis=0)
        local_numer = lax.dot_general(
            weights.astype(jnp.bfloat16),
            projected,
            (((0,), (0,)), ((), ())),
            preferred_element_type=jnp.float32,
        )
        numer, mass = lax.psum((local_numer, local_mass), "rows")
        centroids = (numer + centroids) / (mass[:, None] + 1.0)
    return (centroids, log_total)


def solution(mesh):
    return jax.shard_map(
        on_device,
        mesh=mesh,
        in_specs=(P("rows", "cent"), P("cent", None), P("cent", None)),
        out_specs=(P("cent", None), P("rows")),
        check_vma=False,
    )
```

profile of v0, /device:TPU:2, one launch (start us, length us, event | category | flops | bytes accessed | tf_op | source)
XLA Modules:
  0.0 1584.5 jit_solution(6299140008386346362)
XLA Ops:
  7.2 0.0 copy-start
  7.2 0.0 reduce-scatter.2.cloned.1.call-start
  7.2 1.2 copy-done
  8.4 6.5 fusion.18
  14.9 0.0 copy-start.1
  14.9 0.0 reduce-scatter.2.cloned.1.call-update
  14.9 0.0 all-gather.2.cloned.1.call-start
  14.9 49.2 %reduce-scatter.2.cloned.1.call-done = f32[512,512]{1,0:T(8,128)} async-done(((f32[2048,512]{1,0:T(8,128)}), f32[512,512]{1,0:T(8,128)}) %reduce-scatter.2.cloned.1.call-update) | async-done | bytes 1048592 | tf_op jit(solution)/shard_map/reduce_scatter | solution.py:14
  64.2 2.1 convert_element_type.15
  66.3 0.0 all-gather.2.cloned.1.call-update
  66.3 0.0 all-reduce.3.cloned.1.call-start
  66.3 32.8 %all-gather.2.cloned.1.call-done = bf16[2048,512]{1,0:T(8,128)(2,1)} async-done(((bf16[512,512]{1,0:T(8,128)(2,1)}), bf16[2048,512]{1,0:T(8,128)(2,1)}) %all-gather.2.cloned.1.call-update) | async-done | bytes 2097168 | tf_op jit(solution)/shard_map/all_gather | solution.py:20
  99.1 0.0 copy-done.1
  99.1 7.2 multiply_reduce_fusion.1
  106.3 7.8 pmax.14
  114.2 4.8 exponential_reduce_fusion.1
  118.9 5.9 psum.42
  124.8 7.6 fusion.6
  132.5 0.0 all-reduce.3.cloned.1.call-update
  132.5 0.0 all-reduce.5.cloned.1.call-start
  132.6 4.8 fusion
  137.4 183.6 %psum.44 = f32[1024]{0:T(1024)S(1)} all-reduce(f32[1024]{0:T(1024)S(1)} %fusion), channel_id=1, replica_groups=mesh['rows'=64,'cent'=4] {'rows'}, use_global_device_ids=true, to_apply=%region_7.0 | all-reduce | flops 1024 | bytes 8192 | tf_op jit(solution)/shard_map/psum | solution.py:43
  321.0 517.9 %all-reduce.3.cloned.1.call-done = f32[1024,512]{1,0:T(8,128)} async-done(((f32[1024,512]{1,0:T(8,128)}), f32[1024,512]{1,0:T(8,128)}) %all-reduce.3.cloned.1.call-update) | async-done | bytes 2097168 | tf_op jit(solution)/shard_map/psum | solution.py:43
  838.9 7.9 multiply_reduce_fusion
  846.7 5.9 pmax.15
  852.7 4.8 exponential_reduce_fusion
  857.5 6.6 psum.45
  864.1 0.0 copy-start.2
  864.1 7.6 fusion.4
  871.7 0.0 all-reduce.5.cloned.1.call-update
  871.8 0.0 copy-done.2
  871.8 4.8 fusion.2
  876.6 181.1 %psum.47 = f32[1024]{0:T(1024)S(1)} all-reduce(f32[1024]{0:T(1024)S(1)} %fusion.2), channel_id=1, replica_groups=mesh['rows'=64,'cent'=4] {'rows'}, use_global_device_ids=true, to_apply=%region_14.0 | all-reduce | flops 1024 | bytes 8192 | tf_op jit(solution)/shard_map/psum | solution.py:43
  1057.7 516.3 %all-reduce.5.cloned.1.call-done = f32[1024,512]{1,0:T(8,128)} async-done(((f32[1024,512]{1,0:T(8,128)}), f32[1024,512]{1,0:T(8,128)}) %all-reduce.5.cloned.1.call-update) | async-done | bytes 2097168 | tf_op jit(solution)/shard_map/psum | solution.py:43
  1574.0 4.0 add_divide_fusion
  (4 shorter events, 0.0 us)
Async XLA Ops:
  7.2 1.2 copy-start
  7.2 57.0 %reduce-scatter.2.cloned.1.call-start = ((), (), s32[]{:S(2)}) async-start(), calls=%async_computation.1 | async-start | bytes 5242880 | tf_op jit(solution)/shard_map/reduce_scatter | solution.py:14
  14.9 84.3 %copy-start.1 = (f32[1024,512]{1,0:T(8,128)S(1)}, f32[1024,512]{1,0:T(8,128)}, u32[]{:S(2)}) copy-start(f32[1024,512]{1,0:T(8,128)} %param.5) | copy-start | bytes 6291460
  14.9 84.2 %all-gather.2.cloned.1.call-start = ((), (), s32[]{:S(2)}) async-start(), calls=%async_computation.2 | async-start | bytes 2621440 | tf_op jit(solution)/shard_map/all_gather | solution.py:20
  66.3 772.6 %all-reduce.3.cloned.1.call-start = ((), (), s32[]{:S(2)}) async-start(), calls=%async_computation.3 | async-start | bytes 4194304 | tf_op jit(solution)/shard_map/psum | solution.py:43
  132.5 1441.5 %all-reduce.5.cloned.1.call-start = ((), (), s32[]{:S(2)}) async-start(), calls=%async_computation.4 | async-start | bytes 4194304 | tf_op jit(solution)/shard_map/psum | solution.py:43
  864.1 7.7 copy-start.2
Sparse Core Ops, SparseCore 0:
  15.0 49.1 reduce-scatter.1
  66.6 32.5 all-gather.1
  132.6 706.2 all-reduce.2
  871.9 702.0 all-reduce.4
where the time goes:
time: 1590 us; the launch traced here: 1580 us
  waiting for transfers between devices  1120 us (70%)
  blocking collectives  391 us (25%)
  matrix products  36.8 us (2%)
  other arithmetic  25.3 us (2%)
    psum x2, waiting for transfers between devices, on_device(): numer, mass = lax.psum((local_numer, local_mass), 'rows')  1030 us
    psum x2, blocking collectives, on_device(): numer, mass = lax.psum((local_numer, local_mass), 'rows')  365 us
    reduce_scatter x1, waiting for transfers between devices, on_device(): lax.psum_scatter(jnp.dot(embeddings, basis, preferred_element_type=jnp.fl...  49.2 us
    all_gather x1, waiting for transfers between devices, on_device(): lax.all_gather(proj_share.astype(jnp.bfloat16), 'cent', axis=0, tiled=True)  32.8 us
  transfers between devices with their start and end apart: 4, of which 4 were waited for; matrix products, arithmetic and copies ran while one was open for 1% of the time, Pallas kernels for 0%

commit v1 on v0

v1 whole, which is shorter than its diff:
```python
import jax
import jax.numpy as jnp
from jax import lax
from jax.sharding import Mesh
from jax.sharding import PartitionSpec as P

ITERS = 2


TEMPER = 8.0

ROW_AXES = ("z", "y", "xh")
CENT_AXES = ("xl", "core")


def _reduce_rows(numer, mass):
    count, width = numer.shape
    blocks = 8
    per = count // blocks
    mass_rows = jnp.zeros((blocks, 8, width), jnp.float32).at[:, 0, :per].set(mass.reshape(blocks, per))
    payload = jnp.concatenate([numer.reshape(blocks, per, width), mass_rows], axis=1)
    payload = payload.reshape(blocks * (per + 8), width)
    payload = lax.psum_scatter(payload, "z", scatter_dimension=0, tiled=True)
    payload = lax.psum(payload, "y")
    payload = lax.psum(payload, "xh")
    return payload[:per], payload[per, :per]


def _gather_rows(block):
    return lax.all_gather(block, "z", axis=0, tiled=True)


def _row_index():
    return lax.axis_index("z")


def on_device(embeddings, basis, start_centroids):
    row_count = embeddings.shape[0]
    count = start_centroids.shape[0]
    per = count // 8
    proj_share = lax.psum_scatter(
        jnp.dot(embeddings, basis, preferred_element_type=jnp.float32),
        CENT_AXES,
        scatter_dimension=0,
        tiled=True,
    )
    projected = lax.all_gather(proj_share.astype(jnp.bfloat16), CENT_AXES, axis=0, tiled=True)
    start = _row_index() * per
    block = lax.dynamic_slice_in_dim(start_centroids, start, per, axis=0)
    cent_bf = start_centroids.astype(jnp.bfloat16)
    log_total = jnp.zeros((row_count,), jnp.float32)
    for step in range(ITERS):
        scores = (
            lax.dot_general(
                projected, cent_bf, (((1,), (1,)), ((), ())), preferred_element_type=jnp.float32
            )
            / TEMPER
        )
        local_top = jnp.max(scores, axis=1)
        top = lax.pmax(local_top, CENT_AXES)
        total = lax.psum(jnp.sum(jnp.exp(scores - top[:, None]), axis=1), CENT_AXES)
        log_total = top + jnp.log(total)
        weights = jnp.exp(scores - log_total[:, None])
        local_mass = jnp.sum(weights, axis=0)
        local_numer = lax.dot_general(
            weights.astype(jnp.bfloat16),
            projected,
            (((0,), (0,)), ((), ())),
            preferred_element_type=jnp.float32,
        )
        numer, mass = _reduce_rows(local_numer, local_mass)
        block = (numer + block) / (mass[:, None] + 1.0)
        if step + 1 < ITERS:
            cent_bf = _gather_rows(block.astype(jnp.bfloat16))
    centroids = _gather_rows(block)
    return (centroids, log_total)


def solution(mesh):
    fine = Mesh(mesh.devices.reshape(8, 4, 2, 2, 2), ROW_AXES + CENT_AXES)
    return jax.shard_map(
        on_device,
        mesh=fine,
        in_specs=(P(ROW_AXES, CENT_AXES), P(CENT_AXES, None), P(CENT_AXES, None)),
        out_specs=(P(CENT_AXES, None), P(ROW_AXES)),
        check_vma=False,
    )
```

time: 1590 us -> 528 us (0.33)
  waiting for transfers between devices: 1120 us -> 422 us
  blocking collectives: 391 us -> 25.6 us
    psum x2 -> x4, waiting for transfers between devices: 1030 us -> 174 us  [the longest x2 96.4 us: _reduce_rows(): payload = lax.psum(payload, 'y')]
    psum x4 -> x2, blocking collectives: 377 us -> 11.7 us  [on_device(): total = lax.psum(jnp.sum(jnp.exp(scores - top[:, None]), axis=1), CENT_AXES)]
    reduce_scatter x0 -> x2, waiting for transfers between devices: none -> 86.4 us  [_reduce_rows(): payload = lax.psum_scatter(payload, 'z', scatter_dimension=0, tiled=True)]
    all_gather x1 -> x3, waiting for transfers between devices: 32.8 us -> 113 us  [the longest x2 80.1 us: _gather_rows(): return lax.all_gather(block, 'z', axis=0, tiled=True)]
  transfers between devices with their start and end apart: 4 -> 10, of which waited for: 4 -> 10; matrix products, arithmetic and copies ran while one was open for 1% -> 0% of each run, Pallas kernels for 0% -> 0%
where the time goes in v1:
time: 528 us; the launch traced here: 527 us
  waiting for transfers between devices  422 us (80%)
  other arithmetic  29.7 us (6%)
  matrix products  29 us (5%)
  blocking collectives  25.6 us (5%)
  between operations  14.3 us (3%)
  local copies, waits for them, and re-layouts  5.83 us (1%)
    psum x2, waiting for transfers between devices, _reduce_rows(): payload = lax.psum(payload, 'y')  96.4 us
    reduce_scatter x2, waiting for transfers between devices, _reduce_rows(): payload = lax.psum_scatter(payload, 'z', scatter_dimension=0, tiled=True)  86.4 us
    all_gather x2, waiting for transfers between devices, _gather_rows(): return lax.all_gather(block, 'z', axis=0, tiled=True)  80.1 us
    psum x2, waiting for transfers between devices, _reduce_rows(): payload = lax.psum(payload, 'xh')  77.2 us
    reduce_scatter x1, waiting for transfers between devices, on_device(): lax.psum_scatter(jnp.dot(embeddings, basis, preferred_element_type=jnp.fl...  49.2 us
    all_gather x1, waiting for transfers between devices, on_device(): lax.all_gather(proj_share.astype(jnp.bfloat16), CENT_AXES, axis=0, tiled=...  32.8 us
    dot_general x2, matrix products, on_device(): lax.dot_general(projected, cent_bf, (((1,), (1,)), ((), ())), preferred_e...  14.6 us
    pmax x2, blocking collectives, on_device(): top = lax.pmax(local_top, CENT_AXES)  13.9 us
  transfers between devices with their start and end apart: 10, of which 10 were waited for; matrix products, arithmetic and copies ran while one was open for 0% of the time, Pallas kernels for 0%

profile of v1, /device:TPU:2, one launch (start us, length us, event | category | flops | bytes accessed | tf_op | source)
XLA Modules:
  0.0 527.2 jit_solution(15643615945442049934)
XLA Ops:
  7.2 0.0 reduce-scatter.4.cloned.1.call-start
  7.2 1.2 copy-done
  8.4 6.5 %fusion.21 = f32[2048,512]{1,0:T(8,128)} fusion(bf16[2048,1024]{1,0:T(8,128)(2,1)} %param.7, bf16[1024,512]{1,0:T(8,128)(2,1)S(1)} %copy-done), kind=kOutput, calls=%fused_computation.34 | convolution fusion | flops 2147483648 | bytes 9437184 | tf_op jit(solution)/shard_map/dot_general | solution.py:42
  14.9 0.0 reduce-scatter.4.cloned.1.call-update
  14.9 0.0 all-gather.4.cloned.1.call-start
  14.9 49.2 %reduce-scatter.4.cloned.1.call-done = f32[512,512]{1,0:T(8,128)} async-done(((f32[2048,512]{1,0:T(8,128)}), f32[512,512]{1,0:T(8,128)}) %reduce-scatter.4.cloned.1.call-update) | async-done | bytes 1048592 | tf_op jit(solution)/shard_map/reduce_scatter | solution.py:41
  64.2 2.1 convert_element_type.15
  66.3 0.0 all-gather.4.cloned.1.call-update
  66.3 0.0 reduce-scatter.6.cloned.1.call-start
  66.3 32.8 %all-gather.4.cloned.1.call-done = bf16[2048,512]{1,0:T(8,128)(2,1)} async-done(((bf16[512,512]{1,0:T(8,128)(2,1)}), bf16[2048,512]{1,0:T(8,128)(2,1)}) %all-gather.4.cloned.1.call-update) | async-done | bytes 2097168 | tf_op jit(solution)/shard_map/all_gather | solution.py:47
  99.1 7.2 %multiply_reduce_fusion.1 = (f32[2048]{0:T(1024)S(1)}, f32[2048,1024]{0,1:T(8,128)}) fusion(bf16[2048,512]{1,0:T(8,128)(2,1)} %all-gather.4.cloned.1.call-done, f32[1024,512]{1,0:T(8,128)S(1)} %copy-done.3), kind=kOutput, calls=%fused_computation.9 | convolution fusion | flops 2152200192 | bytes 12591104 | tf_op jit(solution)/shard_map/dot_general | solution.py:54
  106.3 7.8 %pmax.14 = f32[2048]{0:T(1024)S(1)} all-reduce(f32[2048]{0:T(1024)S(1)} %get-tuple-element.26), channel_id=1, replica_groups=mesh['z'=8,'y'=4,'xh'=2,'xl'=2,'core'=2] {'xl','core'}, use_global_device_ids=true, to_apply=%region_2.0 | all-reduce | flops 2048 | bytes 16384 | tf_op jit(solution)/shard_map/pmax | solution.py:60
  114.2 4.8 exponential_reduce_fusion.1
  118.9 5.9 %psum.42 = f32[2048]{0:T(1024)S(1)} all-reduce(f32[2048]{0:T(1024)S(1)} %exponential_reduce_fusion.1), channel_id=1, replica_groups=mesh['z'=8,'y'=4,'xh'=2,'xl'=2,'core'=2] {'xl','core'}, use_global_device_ids=true, to_apply=%region_4.0 | all-reduce | flops 2048 | bytes 16384 | tf_op jit(solution)/shard_map/psum | solution.py:61
  124.8 5.0 fusion
  129.8 0.8 copy-done.1
  130.6 4.0 fusion.6
  134.6 1.6 select_maximum_fusion.1
  136.2 0.0 reduce-scatter.6.cloned.1.call-update
  136.2 0.0 all-reduce.7.cloned.1.call-start
  136.3 44.4 %reduce-scatter.6.cloned.1.call-done = f32[136,512]{1,0:T(8,128)} async-done(((f32[1088,512]{1,0:T(8,128)}), f32[136,512]{1,0:T(8,128)}) %reduce-scatter.6.cloned.1.call-update) | async-done | bytes 278544 | tf_op jit(solution)/shard_map/reduce_scatter | solution.py:23
  180.7 0.0 all-reduce.7.cloned.1.call-update
  180.7 0.0 all-reduce.9.cloned.1.call-start
  180.7 48.0 %all-reduce.7.cloned.1.call-done = f32[136,512]{1,0:T(8,128)} async-done(((f32[136,512]{1,0:T(8,128)}), f32[136,512]{1,0:T(8,128)}) %all-reduce.7.cloned.1.call-update) | async-done | bytes 278544 | tf_op jit(solution)/shard_map/psum | solution.py:24
  228.8 0.0 all-gather.6.cloned.1.call-start
  228.8 38.5 %all-reduce.9.cloned.1.call-done = f32[136,512]{1,0:T(8,128)} async-done(((f32[136,512]{1,0:T(8,128)}), f32[136,512]{1,0:T(8,128)}) %all-reduce.9.cloned.1.call-update) | async-done | bytes 278544 | tf_op jit(solution)/shard_map/psum | solution.py:25
  267.3 0.7 fusion.17
  268.0 1.7 fusion.20
  269.7 0.2 reduce-scatter.8.cloned.1.call-start
  270.0 38.7 %all-gather.6.cloned.1.call-done = bf16[1024,512]{1,0:T(8,128)(2,1)} async-done(((bf16[128,512]{1,0:T(8,128)(2,1)}), bf16[1024,512]{1,0:T(8,128)(2,1)}) %all-gather.6.cloned.1.call-update) | async-done | bytes 1048592 | tf_op jit(solution)/shard_map/all_gather | solution.py:30
  308.7 7.4 %multiply_reduce_fusion = (f32[2048]{0:T(1024)S(1)}, f32[2048,1024]{0,1:T(8,128)}) fusion(bf16[2048,512]{1,0:T(8,128)(2,1)} %all-gather.4.cloned.1.call-done, bf16[1024,512]{1,0:T(8,128)(2,1)} %all-gather.6.cloned.1.call-done), kind=kOutput, calls=%fused_computation.8 | convolution fusion | flops 2151675904 | bytes 11542528 | tf_op jit(solution)/shard_map/dot_general | solution.py:54
  316.1 6.0 %pmax.15 = f32[2048]{0:T(1024)S(1)} all-reduce(f32[2048]{0:T(1024)S(1)} %get-tuple-element.28), channel_id=1, replica_groups=mesh['z'=8,'y'=4,'xh'=2,'xl'=2,'core'=2] {'xl','core'}, use_global_device_ids=true, to_apply=%region_10.0 | all-reduce | flops 2048 | bytes 16384 | tf_op jit(solution)/shard_map/pmax | solution.py:60
  322.2 4.8 exponential_reduce_fusion
  327.0 5.9 %psum.45 = f32[2048]{0:T(1024)S(1)} all-reduce(f32[2048]{0:T(1024)S(1)} %exponential_reduce_fusion), channel_id=1, replica_groups=mesh['z'=8,'y'=4,'xh'=2,'xl'=2,'core'=2] {'xl','core'}, use_global_device_ids=true, to_apply=%region_12.0 | all-reduce | flops 2048 | bytes 16384 | tf_op jit(solution)/shard_map/psum | solution.py:61
  332.9 5.0 fusion.2
  337.8 0.8 copy-done.2
  338.6 4.0 fusion.4
  342.6 1.6 select_maximum_fusion
  344.3 0.0 all-reduce.11.cloned.1.call-start
  344.3 42.0 %reduce-scatter.8.cloned.1.call-done = f32[136,512]{1,0:T(8,128)} async-done(((f32[1088,512]{1,0:T(8,128)}), f32[136,512]{1,0:T(8,128)}) %reduce-scatter.8.cloned.1.call-update) | async-done | bytes 278544 | tf_op jit(solution)/shard_map/reduce_scatter | solution.py:23
  386.4 0.0 all-reduce.13.cloned.1.call-start
  386.4 48.3 %all-reduce.11.cloned.1.call-done = f32[136,512]{1,0:T(8,128)} async-done(((f32[136,512]{1,0:T(8,128)}), f32[136,512]{1,0:T(8,128)}) %all-reduce.11.cloned.1.call-update) | async-done | bytes 278544 | tf_op jit(solution)/shard_map/psum | solution.py:24
  434.8 0.0 all-gather.8.cloned.1.call-start
  434.8 38.7 %all-reduce.13.cloned.1.call-done = f32[136,512]{1,0:T(8,128)} async-done(((f32[136,512]{1,0:T(8,128)}), f32[136,512]{1,0:T(8,128)}) %all-reduce.13.cloned.1.call-update) | async-done | bytes 278544 | tf_op jit(solution)/shard_map/psum | solution.py:25
  473.5 0.7 fusion.16
  474.1 1.8 fusion.14
  475.9 41.4 %all-gather.8.cloned.1.call-done = f32[1024,512]{1,0:T(8,128)} async-done(((f32[128,512]{1,0:T(8,128)}), f32[1024,512]{1,0:T(8,128)}) %all-gather.8.cloned.1.call-update) | async-done | bytes 2097168 | tf_op jit(solution)/shard_map/all_gather | solution.py:30
  517.3 3.1 copy.10
  (17 shorter events, 0.1 us)
Async XLA Ops:
  7.2 1.2 copy-start
  7.2 57.0 %reduce-scatter.4.cloned.1.call-start = ((), (), s32[]{:S(2)}) async-start(), calls=%async_computation.3 | async-start | bytes 5242880 | tf_op jit(solution)/shard_map/reduce_scatter | solution.py:41
  14.9 84.3 %copy-start.3 = (f32[1024,512]{1,0:T(8,128)S(1)}, f32[1024,512]{1,0:T(8,128)}, u32[]{:S(2)}) copy-start(f32[1024,512]{1,0:T(8,128)} %param.9) | copy-start | bytes 6291460
  14.9 84.2 %all-gather.4.cloned.1.call-start = ((), (), s32[]{:S(2)}) async-start(), calls=%async_computation.4 | async-start | bytes 2621440 | tf_op jit(solution)/shard_map/all_gather | solution.py:47
  66.3 114.4 %reduce-scatter.6.cloned.1.call-start = ((), (), s32[]{:S(2)}) async-start(), calls=%async_computation.5 | async-start | bytes 2506752 | tf_op jit(solution)/shard_map/reduce_scatter | solution.py:23
  124.8 5.8 %copy-start.1 = (f32[2048,1024]{0,1:T(8,128)S(1)}, f32[2048,1024]{0,1:T(8,128)}, u32[]{:S(2)}) copy-start(f32[2048,1024]{0,1:T(8,128)} %get-tuple-element.27) | copy-start | bytes 25165828
  136.2 92.5 %all-reduce.7.cloned.1.call-start = ((), (), s32[]{:S(2)}) async-start(), calls=%async_computation.6 | async-start | bytes 557056 | tf_op jit(solution)/shard_map/psum | solution.py:24
  180.7 86.7 %all-reduce.9.cloned.1.call-start = ((), (), s32[]{:S(2)}) async-start(), calls=%async_computation.7 | async-start | bytes 557056 | tf_op jit(solution)/shard_map/psum | solution.py:25
  228.8 79.9 %all-gather.6.cloned.1.call-start = ((), (), s32[]{:S(2)}) async-start(), calls=%async_computation.8 | async-start | bytes 1179648 | tf_op jit(solution)/shard_map/all_gather | solution.py:30
  269.7 116.6 %reduce-scatter.8.cloned.1.call-start = ((), (), s32[]{:S(2)}) async-start(), calls=%async_computation.9 | async-start | bytes 2506752 | tf_op jit(solution)/shard_map/reduce_scatter | solution.py:23
  332.8 5.0 copy-start.5
  332.9 5.8 %copy-start.2 = (f32[2048,1024]{0,1:T(8,128)S(1)}, f32[2048,1024]{0,1:T(8,128)}, u32[]{:S(2)}) copy-start(f32[2048,1024]{0,1:T(8,128)} %get-tuple-element.29) | copy-start | bytes 25165828
  342.6 131.5 %copy-start.4 = (f32[136,512]{1,0:T(8,128)S(1)}, f32[136,512]{1,0:T(8,128)}, u32[]{:S(2)}) copy-start(f32[136,512]{1,0:T(8,128)} %all-reduce.9.cloned.1.call-done) | copy-start | bytes 835588
  344.3 90.5 %all-reduce.11.cloned.1.call-start = ((), (), s32[]{:S(2)}) async-start(), calls=%async_computation.10 | async-start | bytes 557056 | tf_op jit(solution)/shard_map/psum | solution.py:24
  386.4 87.1 %all-reduce.13.cloned.1.call-start = ((), (), s32[]{:S(2)}) async-start(), calls=%async_computation.11 | async-start | bytes 557056 | tf_op jit(solution)/shard_map/psum | solution.py:25
  434.8 82.6 %all-gather.8.cloned.1.call-start = ((), (), s32[]{:S(2)}) async-start(), calls=%async_computation.12 | async-start | bytes 2359296 | tf_op jit(solution)/shard_map/all_gather | solution.py:30
Sparse Core Ops, SparseCore 0:
  15.0 49.1 reduce-scatter.3
  66.6 32.5 all-gather.3
  136.4 44.2 reduce-scatter.5
  182.9 45.8 all-reduce.6
  231.2 36.0 all-reduce.8
  269.9 38.7 all-gather.5
  344.4 41.9 reduce-scatter.7
  388.7 46.0 all-reduce.10
  437.3 36.0 all-reduce.12
  476.1 41.2 all-gather.7

commit v2 on v1

--- a/solution.py
+++ b/solution.py
@@ -15,29 +15,17 @@
 
 def _reduce_rows(numer, mass):
     count, width = numer.shape
-    blocks = 8
-    per = count // blocks
-    mass_rows = jnp.zeros((blocks, 8, width), jnp.float32).at[:, 0, :per].set(mass.reshape(blocks, per))
-    payload = jnp.concatenate([numer.reshape(blocks, per, width), mass_rows], axis=1)
-    payload = payload.reshape(blocks * (per + 8), width)
-    payload = lax.psum_scatter(payload, "z", scatter_dimension=0, tiled=True)
-    payload = lax.psum(payload, "y")
-    payload = lax.psum(payload, "xh")
-    return payload[:per], payload[per, :per]
-
-
-def _gather_rows(block):
-    return lax.all_gather(block, "z", axis=0, tiled=True)
-
-
-def _row_index():
-    return lax.axis_index("z")
+    mass_rows = jnp.zeros((8, width), jnp.float32).at[: count // width].set(mass.reshape(count // width, width))
+    mine = jnp.concatenate([numer, mass_rows], axis=0)
+    xl = lax.axis_index("xl")
+    payload = jnp.stack([jnp.where(xl == slot, mine, 0.0) for slot in range(2)])
+    payload = lax.psum(payload, ROW_AXES + ("xl",))
+    total = lax.dynamic_index_in_dim(payload, xl, axis=0, keepdims=False)
+    return total[:count], total[count : count + count // width].reshape(count)
 
 
 def on_device(embeddings, basis, start_centroids):
     row_count = embeddings.shape[0]
-    count = start_centroids.shape[0]
-    per = count // 8
     proj_share = lax.psum_scatter(
         jnp.dot(embeddings, basis, preferred_element_type=jnp.float32),
         CENT_AXES,
@@ -45,8 +33,7 @@
         tiled=True,
     )
     projected = lax.all_gather(proj_share.astype(jnp.bfloat16), CENT_AXES, axis=0, tiled=True)
-    start = _row_index() * per
-    block = lax.dynamic_slice_in_dim(start_centroids, start, per, axis=0)
+    centroids = start_centroids
     cent_bf = start_centroids.astype(jnp.bfloat16)
     log_total = jnp.zeros((row_count,), jnp.float32)
     for step in range(ITERS):
@@ -69,10 +56,8 @@
             preferred_element_type=jnp.float32,
         )
         numer, mass = _reduce_rows(local_numer, local_mass)
-        block = (numer + block) / (mass[:, None] + 1.0)
-        if step + 1 < ITERS:
-            cent_bf = _gather_rows(block.astype(jnp.bfloat16))
-    centroids = _gather_rows(block)
+        centroids = (numer + centroids) / (mass[:, None] + 1.0)
+        cent_bf = centroids.astype(jnp.bfloat16)
     return (centroids, log_total)
 
 

time: 528 us -> 660 us (1.25)
  waiting for transfers between devices: 422 us -> 551 us
    psum x4 -> x2, waiting for transfers between devices: 174 us -> 469 us  [_reduce_rows(): payload = lax.psum(payload, ROW_AXES + ('xl',))]
    reduce_scatter x2 -> x0, waiting for transfers between devices: 86.4 us -> none  [_reduce_rows(): payload = lax.psum_scatter(payload, 'z', scatter_dimension=0, tiled=True)]
    all_gather x2 -> x0, waiting for transfers between devices: 80.1 us -> none  [_gather_rows(): return lax.all_gather(block, 'z', axis=0, tiled=True)]
  transfers between devices with their start and end apart: 10 -> 4, of which waited for: 10 -> 4; matrix products, arithmetic and copies ran while one was open for 0% -> 0% of each run, Pallas kernels for 0% -> 0%
where the time goes in v2:
time: 660 us; the launch traced here: 659 us
  waiting for transfers between devices  551 us (83%)
  matrix products  34.4 us (5%)
  other arithmetic  32.7 us (5%)
  blocking collectives  25.7 us (4%)
  between operations  13.9 us (2%)
    psum x2, waiting for transfers between devices, _reduce_rows(): payload = lax.psum(payload, ROW_AXES + ('xl',))  469 us
    reduce_scatter x1, waiting for transfers between devices, on_device(): lax.psum_scatter(jnp.dot(embeddings, basis, preferred_element_type=jnp.fl...  49.2 us
    all_gather x1, waiting for transfers between devices, on_device(): lax.all_gather(proj_share.astype(jnp.bfloat16), CENT_AXES, axis=0, tiled=...  32.8 us
    dot_general x2, matrix products, on_device(): lax.dot_general(projected, cent_bf, (((1,), (1,)), ((), ())), preferred_e...  15.2 us
    pmax x2, blocking collectives, on_device(): top = lax.pmax(local_top, CENT_AXES)  13.6 us
  transfers between devices with their start and end apart: 4, of which 4 were waited for; matrix products, arithmetic and copies ran while one was open for 0% of the time, Pallas kernels for 0%

profile of v2, /device:TPU:2, one launch (start us, length us, event | category | flops | bytes accessed | tf_op | source)
XLA Modules:
  0.0 659.3 jit_solution(13476238934799898947)
XLA Ops:
  7.2 0.0 copy-start
  7.2 0.0 reduce-scatter.2.cloned.1.call-start
  7.2 1.2 copy-done
  8.4 6.5 fusion.35
  14.9 0.0 copy-start.1
  14.9 0.0 reduce-scatter.2.cloned.1.call-update
  14.9 0.0 all-gather.2.cloned.1.call-start
  14.9 49.2 %reduce-scatter.2.cloned.1.call-done = f32[512,512]{1,0:T(8,128)} async-done(((f32[2048,512]{1,0:T(8,128)}), f32[512,512]{1,0:T(8,128)}) %reduce-scatter.2.cloned.1.call-update) | async-done | bytes 1048592 | tf_op jit(solution)/shard_map/reduce_scatter | solution.py:29
  64.2 2.1 convert_element_type.15
  66.3 0.0 all-gather.2.cloned.1.call-update
  66.3 0.0 all-reduce.5.cloned.1.call-start
  66.3 32.8 %all-gather.2.cloned.1.call-done = bf16[2048,512]{1,0:T(8,128)(2,1)} async-done(((bf16[512,512]{1,0:T(8,128)(2,1)}), bf16[2048,512]{1,0:T(8,128)(2,1)}) %all-gather.2.cloned.1.call-update) | async-done | bytes 2097168 | tf_op jit(solution)/shard_map/all_gather | solution.py:35
  99.1 0.0 copy-done.1
  99.1 7.3 %multiply_reduce_fusion.1 = (f32[2048]{0:T(1024)S(1)}, f32[2048,1024]{0,1:T(8,128)}) fusion(bf16[2048,512]{1,0:T(8,128)(2,1)} %all-gather.2.cloned.1.call-done, f32[1024,512]{1,0:T(8,128)S(1)} %copy-done.1), kind=kOutput, calls=%fused_computation.9 | convolution fusion | flops 2152200192 | bytes 12591104 | tf_op jit(solution)/shard_map/dot_general | solution.py:41
  106.4 7.8 %pmax.14 = f32[2048]{0:T(1024)S(1)} all-reduce(f32[2048]{0:T(1024)S(1)} %get-tuple-element.30), channel_id=1, replica_groups=mesh['z'=8,'y'=4,'xh'=2,'xl'=2,'core'=2] {'xl','core'}, use_global_device_ids=true, to_apply=%region_2.0 | all-reduce | flops 2048 | bytes 16384 | tf_op jit(solution)/shard_map/pmax | solution.py:47
  114.3 4.8 exponential_reduce_fusion.1
  119.1 5.9 psum.28
  124.9 4.8 fusion
  129.8 6.3 fusion.20
  136.1 0.5 fusion.19
  136.7 2.5 pad_maximum_fusion
  139.2 0.0 all-reduce.5.cloned.1.call-update
  139.2 0.2 all-reduce.7.cloned.1.call-start
  139.4 236.1 %all-reduce.5.cloned.1.call-done = f32[2,1032,512]{2,1,0:T(8,128)} async-done(((f32[2,1032,512]{2,1,0:T(8,128)}), f32[2,1032,512]{2,1,0:T(8,128)}) %all-reduce.5.cloned.1.call-update) | async-done | bytes 4227088 | tf_op jit(solution)/shard_map/psum | solution.py:22
  375.5 0.7 fusion.31
  376.3 8.0 %multiply_reduce_fusion = (f32[2048]{0:T(1024)S(1)}, f32[2048,1024]{0,1:T(8,128)}) fusion(bf16[2048,512]{1,0:T(8,128)(2,1)} %all-gather.2.cloned.1.call-done, f32[1024]{0:T(1024)S(1)} %bitcast.39, f32[1024,512]{1,0:T(8,128)S(1)} %copy-done.1, f32[2,1032,512]{2,1,0:T(8,128)} %all-reduce.5.cloned.1.call-done, s32[]{:T(128)S(6)} %select_n.59), kind=kOutput, calls=%fused_computation.8 | convolution fusion | flops 2153248768 | bytes 14692356 | tf_op jit(solution)/shard_map/dot_general | solution.py:41
  384.2 5.7 pmax.15
  390.0 4.8 exponential_reduce_fusion
  394.8 6.3 psum.30
  401.1 0.0 copy-start.2
  401.1 4.8 fusion.2
  405.9 0.0 copy-done.2
  405.9 6.3 fusion.23
  412.3 0.5 fusion.17
  412.8 2.4 pad_maximum_fusion.1
  415.2 0.0 all-reduce.7.cloned.1.call-update
  415.2 232.8 %all-reduce.7.cloned.1.call-done = f32[2,1032,512]{2,1,0:T(8,128)} async-done(((f32[2,1032,512]{2,1,0:T(8,128)}), f32[2,1032,512]{2,1,0:T(8,128)}) %all-reduce.7.cloned.1.call-update) | async-done | bytes 4227088 | tf_op jit(solution)/shard_map/psum | solution.py:22
  648.0 0.7 fusion.30
  648.8 4.0 fusion.13
  (8 shorter events, 0.1 us)
Async XLA Ops:
  7.2 1.2 copy-start
  7.2 57.0 %reduce-scatter.2.cloned.1.call-start = ((), (), s32[]{:S(2)}) async-start(), calls=%async_computation.1 | async-start | bytes 5242880 | tf_op jit(solution)/shard_map/reduce_scatter | solution.py:29
  14.9 84.3 %copy-start.1 = (f32[1024,512]{1,0:T(8,128)S(1)}, f32[1024,512]{1,0:T(8,128)}, u32[]{:S(2)}) copy-start(f32[1024,512]{1,0:T(8,128)} %param.9) | copy-start | bytes 6291460
  14.9 84.2 %all-gather.2.cloned.1.call-start = ((), (), s32[]{:S(2)}) async-start(), calls=%async_computation.2 | async-start | bytes 2621440 | tf_op jit(solution)/shard_map/all_gather | solution.py:35
  66.3 309.3 %all-reduce.5.cloned.1.call-start = ((), (), s32[]{:S(2)}) async-start(), calls=%async_computation.3 | async-start | bytes 8454144 | tf_op jit(solution)/shard_map/psum | solution.py:22
  139.2 508.9 %all-reduce.7.cloned.1.call-start = ((), (), s32[]{:S(2)}) async-start(), calls=%async_computation.4 | async-start | bytes 8454144 | tf_op jit(solution)/shard_map/psum | solution.py:22
  401.1 4.9 copy-start.2
Sparse Core Ops, SparseCore 0:
  15.0 49.1 reduce-scatter.1
  66.6 32.5 all-gather.1
  139.3 236.2 all-reduce.4
  415.4 232.6 all-reduce.6

commit v3 on v1

--- a/solution.py
+++ b/solution.py
@@ -13,6 +13,16 @@
 CENT_AXES = ("xl", "core")
 
 
+def _swap(x, axis, bit):
+    size = {"y": 4, "xh": 2}[axis]
+    return lax.ppermute(x, axis, [(i, i ^ bit) for i in range(size)])
+
+
+def _bits():
+    y = lax.axis_index("y")
+    return ((y & 1, "y", 1), ((y >> 1) & 1, "y", 2), (lax.axis_index("xh"), "xh", 1))
+
+
 def _reduce_rows(numer, mass):
     count, width = numer.shape
     blocks = 8
@@ -21,23 +31,35 @@
     payload = jnp.concatenate([numer.reshape(blocks, per, width), mass_rows], axis=1)
     payload = payload.reshape(blocks * (per + 8), width)
     payload = lax.psum_scatter(payload, "z", scatter_dimension=0, tiled=True)
-    payload = lax.psum(payload, "y")
-    payload = lax.psum(payload, "xh")
-    return payload[:per], payload[per, :per]
+    numer, mass = payload[:per], payload[per, :per]
+    for bit, axis, mask in _bits():
+        half = numer.shape[0] // 2
+        keep = lax.dynamic_slice_in_dim(numer, bit * half, half, axis=0)
+        send = lax.dynamic_slice_in_dim(numer, (1 - bit) * half, half, axis=0)
+        keep_mass = lax.dynamic_slice_in_dim(mass, bit * half, half, axis=0)
+        send_mass = lax.dynamic_slice_in_dim(mass, (1 - bit) * half, half, axis=0)
+        numer = keep + _swap(send, axis, mask)
+        mass = keep_mass + _swap(send_mass, axis, mask)
+    return numer, mass
 
 
 def _gather_rows(block):
+    for bit, axis, mask in reversed(_bits()):
+        other = _swap(block, axis, mask)
+        block = jnp.where(bit == 0, jnp.concatenate([block, other]), jnp.concatenate([other, block]))
     return lax.all_gather(block, "z", axis=0, tiled=True)
 
 
-def _row_index():
-    return lax.axis_index("z")
+def _row_offset(count):
+    y = lax.axis_index("y")
+    per = count // 64
+    return lax.axis_index("z") * (count // 8) + (y & 1) * (4 * per) + ((y >> 1) & 1) * (2 * per) + lax.axis_index("xh") * per
 
 
 def on_device(embeddings, basis, start_centroids):
     row_count = embeddings.shape[0]
     count = start_centroids.shape[0]
-    per = count // 8
+    per = count // 64
     proj_share = lax.psum_scatter(
         jnp.dot(embeddings, basis, preferred_element_type=jnp.float32),
         CENT_AXES,
@@ -45,7 +67,7 @@
         tiled=True,
     )
     projected = lax.all_gather(proj_share.astype(jnp.bfloat16), CENT_AXES, axis=0, tiled=True)
-    start = _row_index() * per
+    start = _row_offset(count)
     block = lax.dynamic_slice_in_dim(start_centroids, start, per, axis=0)
     cent_bf = start_centroids.astype(jnp.bfloat16)
     log_total = jnp.zeros((row_count,), jnp.float32)

time: 528 us -> 415 us (0.79)
  waiting for transfers between devices: 422 us -> 273 us
  starting transfers between devices: 0.58 us -> 38.6 us
    psum x4 -> x0, waiting for transfers between devices: 174 us -> none  [the longest x2 96.4 us: _reduce_rows(): payload = lax.psum(payload, 'y')]
    ppermute x0 -> x18, starting transfers between devices: none -> 38.4 us  [_swap(): return lax.ppermute(x, axis, [(i, i ^ bit) for i in range(size)])]
    ppermute x0 -> x18, waiting for transfers between devices: none -> 28.3 us  [_swap(): return lax.ppermute(x, axis, [(i, i ^ bit) for i in range(size)])]
  transfers between devices with their start and end apart: 10 -> 24, of which waited for: 10 -> 21; matrix products, arithmetic and copies ran while one was open for 0% -> 1% of each run, Pallas kernels for 0% -> 0%
where the time goes in v3:
time: 415 us
  waiting for transfers between devices  273 us (66%)
  starting transfers between devices  38.6 us (9%)
  other arithmetic  27.9 us (7%)
  blocking collectives  25.6 us (6%)
  matrix products  25.2 us (6%)
  between operations  14.4 us (3%)
  local copies, waits for them, and re-layouts  9.64 us (2%)
    reduce_scatter x2, waiting for transfers between devices, _reduce_rows(): payload = lax.psum_scatter(payload, 'z', scatter_dimension=0, tiled=True)  86.1 us
    all_gather x2, waiting for transfers between devices, _gather_rows(): return lax.all_gather(block, 'z', axis=0, tiled=True)  76.8 us
    reduce_scatter x1, waiting for transfers between devices, on_device(): lax.psum_scatter(jnp.dot(embeddings, basis, preferred_element_type=jnp.fl...  49.2 us
    ppermute x18, starting transfers between devices, _swap(): return lax.ppermute(x, axis, [(i, i ^ bit) for i in range(size)])  38.4 us
    all_gather x1, waiting for transfers between devices, on_device(): lax.all_gather(proj_share.astype(jnp.bfloat16), CENT_AXES, axis=0, tiled=...  32.8 us
    ppermute x18, waiting for transfers between devices, _swap(): return lax.ppermute(x, axis, [(i, i ^ bit) for i in range(size)])  28.3 us
    dot_general x2, matrix products, on_device(): lax.dot_general(projected, cent_bf, (((1,), (1,)), ((), ())), preferred_e...  14 us
    pmax x2, blocking collectives, on_device(): top = lax.pmax(local_top, CENT_AXES)  13.9 us
  transfers between devices with their start and end apart: 24, of which 21 were waited for; matrix products, arithmetic and copies ran while one was open for 1% of the time, Pallas kernels for 0%

profile of v3, /device:TPU:2, one launch (start us, length us, event | category | flops | bytes accessed | tf_op | source)
XLA Modules:
  0.0 414.8 jit_solution(17188950508600034289)
XLA Ops:
  7.2 1.2 copy-done
  8.4 6.5 %fusion.23 = f32[2048,512]{1,0:T(8,128)} fusion(bf16[2048,1024]{1,0:T(8,128)(2,1)} %param.7, bf16[1024,512]{1,0:T(8,128)(2,1)S(1)} %copy-done), kind=kOutput, calls=%fused_computation.58 | convolution fusion | flops 2147483648 | bytes 9437184 | tf_op jit(solution)/shard_map/dot_general | solution.py:64
  14.9 49.2 %reduce-scatter.4.cloned.1.call-done = f32[512,512]{1,0:T(8,128)} async-done(((f32[2048,512]{1,0:T(8,128)}), f32[512,512]{1,0:T(8,128)}) %reduce-scatter.4.cloned.1.call-update) | async-done | bytes 1048592 | tf_op jit(solution)/shard_map/reduce_scatter | solution.py:63
  64.2 2.1 convert_element_type.15
  66.3 32.8 %all-gather.4.cloned.1.call-done = bf16[2048,512]{1,0:T(8,128)(2,1)} async-done(((bf16[512,512]{1,0:T(8,128)(2,1)}), bf16[2048,512]{1,0:T(8,128)(2,1)}) %all-gather.4.cloned.1.call-update) | async-done | bytes 2097168 | tf_op jit(solution)/shard_map/all_gather | solution.py:69
  99.1 7.2 %multiply_reduce_fusion.1 = (f32[2048]{0:T(1024)S(1)}, f32[2048,1024]{0,1:T(8,128)}) fusion(bf16[2048,512]{1,0:T(8,128)(2,1)} %all-gather.4.cloned.1.call-done, f32[1024,512]{1,0:T(8,128)S(1)} %copy-done.4), kind=kOutput, calls=%fused_computation.9 | convolution fusion | flops 2152200192 | bytes 12591104 | tf_op jit(solution)/shard_map/dot_general | solution.py:76
  106.3 7.8 %pmax.14 = f32[2048]{0:T(1024)S(1)} all-reduce(f32[2048]{0:T(1024)S(1)} %get-tuple-element.28), channel_id=1, replica_groups=mesh['z'=8,'y'=4,'xh'=2,'xl'=2,'core'=2] {'xl','core'}, use_global_device_ids=true, to_apply=%region_2.0 | all-reduce | flops 2048 | bytes 16384 | tf_op jit(solution)/shard_map/pmax | solution.py:82
  114.2 4.9 %exponential_reduce_fusion.1 = f32[2048]{0:T(1024)S(1)} fusion(f32[2048,1024]{0,1:T(8,128)} %get-tuple-element.29, f32[2048]{0:T(1024)S(1)} %pmax.14), kind=kLoop, calls=%fused_computation.3 | loop fusion | flops 6289408 | bytes 8404992 | tf_op jit(solution)/shard_map/reduce_sum | solution.py:83
  119.1 5.9 %psum.14 = f32[2048]{0:T(1024)S(1)} all-reduce(f32[2048]{0:T(1024)S(1)} %exponential_reduce_fusion.1), channel_id=1, replica_groups=mesh['z'=8,'y'=4,'xh'=2,'xl'=2,'core'=2] {'xl','core'}, use_global_device_ids=true, to_apply=%region_4.0 | all-reduce | flops 2048 | bytes 16384 | tf_op jit(solution)/shard_map/psum | solution.py:83
  125.0 5.0 %fusion = f32[1024]{0:T(1024)S(1)} fusion(f32[2048,1024]{0,1:T(8,128)} %get-tuple-element.29, f32[2048]{0:T(1024)S(1)} %log_add_fusion.1), kind=kLoop, calls=%fused_computation.4 | loop fusion | flops 6290432 | bytes 8400896 | tf_op jit(solution)/shard_map/reduce_sum | solution.py:86
  130.8 2.4 fusion.6
  133.2 1.6 select_maximum_fusion.1
  134.9 44.2 %reduce-scatter.6.cloned.1.call-done = f32[136,512]{1,0:T(8,128)} async-done(((f32[1088,512]{1,0:T(8,128)}), f32[136,512]{1,0:T(8,128)}) %reduce-scatter.6.cloned.1.call-update) | async-done | bytes 278544 | tf_op jit(solution)/shard_map/reduce_scatter | solution.py:33
  179.8 1.5 collective-permute-start.3
  183.5 3.3 collective-permute-start.4
  187.4 3.3 collective-permute-start.1
  190.8 1.8 collective-permute-start.5
  193.5 2.3 collective-permute-start.2
  196.0 3.0 collective-permute-done.2
  199.8 2.2 collective-permute-start.6
  202.1 3.0 collective-permute-done.6
  205.1 3.1 collective-permute-start.7
  208.2 2.4 collective-permute-done.7
  210.6 1.3 collective-permute-start.8
  211.9 3.1 collective-permute-done.8
  215.8 37.1 %all-gather.6.cloned.1.call-done = bf16[1024,512]{1,0:T(8,128)(2,1)} async-done(((bf16[128,512]{1,0:T(8,128)(2,1)}), bf16[1024,512]{1,0:T(8,128)(2,1)}) %all-gather.6.cloned.1.call-update) | async-done | bytes 1048592 | tf_op jit(solution)/shard_map/all_gather | solution.py:50
  252.9 6.8 %multiply_reduce_fusion = (f32[2048]{0:T(1024)S(1)}, f32[2048,1024]{0,1:T(8,128)}) fusion(bf16[2048,512]{1,0:T(8,128)(2,1)S(1)} %copy-done.3, bf16[1024,512]{1,0:T(8,128)(2,1)} %all-gather.6.cloned.1.call-done), kind=kOutput, calls=%fused_computation.8 | convolution fusion | flops 2151675904 | bytes 11542528 | tf_op jit(solution)/shard_map/dot_general | solution.py:76
  259.7 6.0 %pmax.15 = f32[2048]{0:T(1024)S(1)} all-reduce(f32[2048]{0:T(1024)S(1)} %get-tuple-element.30), channel_id=1, replica_groups=mesh['z'=8,'y'=4,'xh'=2,'xl'=2,'core'=2] {'xl','core'}, use_global_device_ids=true, to_apply=%region_8.9 | all-reduce | flops 2048 | bytes 16384 | tf_op jit(solution)/shard_map/pmax | solution.py:82
  265.8 4.8 %exponential_reduce_fusion = f32[2048]{0:T(1024)S(1)} fusion(f32[2048,1024]{0,1:T(8,128)} %get-tuple-element.31, f32[2048]{0:T(1024)S(1)} %pmax.15), kind=kLoop, calls=%fused_computation.1 | loop fusion | flops 6289408 | bytes 8404992 | tf_op jit(solution)/shard_map/reduce_sum | solution.py:83
  270.5 5.9 %psum.15 = f32[2048]{0:T(1024)S(1)} all-reduce(f32[2048]{0:T(1024)S(1)} %exponential_reduce_fusion), channel_id=1, replica_groups=mesh['z'=8,'y'=4,'xh'=2,'xl'=2,'core'=2] {'xl','core'}, use_global_device_ids=true, to_apply=%region_10.11 | all-reduce | flops 2048 | bytes 16384 | tf_op jit(solution)/shard_map/psum | solution.py:83
  276.5 5.0 %fusion.2 = f32[1024]{0:T(1024)S(1)} fusion(f32[2048,1024]{0,1:T(8,128)} %get-tuple-element.31, f32[2048]{0:T(1024)S(1)} %log_add_fusion), kind=kLoop, calls=%fused_computation.6 | loop fusion | flops 6290432 | bytes 8400896 | tf_op jit(solution)/shard_map/reduce_sum | solution.py:86
  282.2 2.4 fusion.4
  284.6 1.6 select_maximum_fusion
  286.3 41.9 %reduce-scatter.8.cloned.1.call-done = f32[136,512]{1,0:T(8,128)} async-done(((f32[1088,512]{1,0:T(8,128)}), f32[136,512]{1,0:T(8,128)}) %reduce-scatter.8.cloned.1.call-update) | async-done | bytes 278544 | tf_op jit(solution)/shard_map/reduce_scatter | solution.py:33
  329.0 1.5 collective-permute-start.12
  332.7 3.3 collective-permute-start.13
  336.5 2.8 collective-permute-start.10
  339.5 2.4 collective-permute-start.14
  342.4 2.2 collective-permute-start.11
  344.8 3.2 collective-permute-done.11
  348.0 2.2 collective-permute-start.15
  350.2 3.3 collective-permute-done.15
  353.5 2.8 collective-permute-start.16
  356.3 3.0 collective-permute-done.16
  359.3 1.2 collective-permute-start.17
  360.6 3.8 collective-permute-done.17
  365.2 39.7 %all-gather.8.cloned.1.call-done = f32[1024,512]{1,0:T(8,128)} async-done(((f32[128,512]{1,0:T(8,128)}), f32[1024,512]{1,0:T(8,128)}) %all-gather.8.cloned.1.call-update) | async-done | bytes 2097168 | tf_op jit(solution)/shard_map/all_gather | solution.py:50
  404.8 3.1 copy.6
  (71 shorter events, 13.4 us)
Async XLA Ops:
  7.2 1.2 copy-start
  7.2 57.0 %reduce-scatter.4.cloned.1.call-start = ((), (), s32[]{:S(2)}) async-start(), calls=%async_computation.3 | async-start | bytes 5242880 | tf_op jit(solution)/shard_map/reduce_scatter | solution.py:63
  14.9 84.3 %copy-start.4 = (f32[1024,512]{1,0:T(8,128)S(1)}, f32[1024,512]{1,0:T(8,128)}, u32[]{:S(2)}) copy-start(f32[1024,512]{1,0:T(8,128)} %param.9) | copy-start | bytes 6291460
  14.9 84.2 %all-gather.4.cloned.1.call-start = ((), (), s32[]{:S(2)}) async-start(), calls=%async_computation.4 | async-start | bytes 2621440 | tf_op jit(solution)/shard_map/all_gather | solution.py:69
  66.3 112.7 %reduce-scatter.6.cloned.1.call-start = ((), (), s32[]{:S(2)}) async-start(), calls=%async_computation.5 | async-start | bytes 2506752 | tf_op jit(solution)/shard_map/reduce_scatter | solution.py:33
  114.2 15.8 %copy-start.3 = (bf16[2048,512]{1,0:T(8,128)(2,1)S(1)}, bf16[2048,512]{1,0:T(8,128)(2,1)}, u32[]{:S(2)}) copy-start(bf16[2048,512]{1,0:T(8,128)(2,1)} %all-gather.4.cloned.1.call-done) | copy-start | bytes 6291460
  125.0 5.8 %copy-start.1 = (f32[2048,1024]{0,1:T(8,128)S(1)}, f32[2048,1024]{0,1:T(8,128)}, u32[]{:S(2)}) copy-start(f32[2048,1024]{0,1:T(8,128)} %get-tuple-element.29) | copy-start | bytes 25165828
  134.8 118.1 %all-gather.6.cloned.1.call-start = ((), (), s32[]{:S(2)}) async-start(), calls=%async_computation.6 | async-start | bytes 1179648 | tf_op jit(solution)/shard_map/all_gather | solution.py:50
  179.8 3.6 collective-permute-start.3
  182.3 5.1 %collective-permute-start = (f32[64,512]{1,0:T(8,128)S(1)}, f32[64,512]{1,0:T(8,128)S(1)}, u32[]{:S(2)}, u32[]{:S(2)}) collective-permute-start(f32[64,512]{1,0:T(8,128)S(1)} %constant_dynamic-slice_fusion.9), channel_id=1, source_target_pairs={{0,8},{8,0},{16,24},{24,16},{1,9},{9,1},{17,25},{25,17},{2,10},{10... | collective-permute-start | bytes 393224 | tf_op jit(solution)/shard_map/ppermute | solution.py:18
  183.5 7.2 %collective-permute-start.4 = (f32[32]{0:T(128)S(1)}, f32[32]{0:T(128)S(1)}, u32[]{:S(2)}, u32[]{:S(2)}) collective-permute-start(f32[32]{0:T(128)S(1)} %dynamic_slice.95), channel_id=1, source_target_pairs={{0,16},{8,24},{16,0},{24,8},{1,17},{9,25},{17,1},{25,9},{2,18},{10... | collective-permute-start | bytes 392 | tf_op jit(solution)/shard_map/ppermute | solution.py:18
  187.4 6.0 %collective-permute-start.1 = (f32[32,512]{1,0:T(8,128)S(1)}, f32[32,512]{1,0:T(8,128)S(1)}, u32[]{:S(2)}, u32[]{:S(2)}) collective-permute-start(f32[32,512]{1,0:T(8,128)S(1)} %constant_dynamic-slice_fusion.8), channel_id=1, source_target_pairs={{0,16},{8,24},{16,0},{24,8},{1,17},{9,25},{17,1},{25,9},{2,18},{10... | collective-permute-start | bytes 196616 | tf_op jit(solution)/shard_map/ppermute | solution.py:18
  190.8 5.1 %collective-permute-start.5 = (f32[16]{0:T(128)S(1)}, f32[16]{0:T(128)S(1)}, u32[]{:S(2)}, u32[]{:S(2)}) collective-permute-start(f32[16]{0:T(128)S(1)} %dynamic_slice.97), channel_id=1, source_target_pairs={{0,4},{4,0},{1,5},{5,1},{2,6},{6,2},{3,7},{7,3},{8,12},{12,8},{9,1... | collective-permute-start | bytes 200 | tf_op jit(solution)/shard_map/ppermute | solution.py:18
  193.5 5.5 %collective-permute-start.2 = (f32[16,512]{1,0:T(8,128)S(1)}, f32[16,512]{1,0:T(8,128)S(1)}, u32[]{:S(2)}, u32[]{:S(2)}) collective-permute-start(f32[16,512]{1,0:T(8,128)S(1)} %constant_dynamic-slice_fusion.6), channel_id=1, source_target_pairs={{0,4},{4,0},{1,5},{5,1},{2,6},{6,2},{3,7},{7,3},{8,12},{12,8},{9,1... | collective-permute-start | bytes 98312 | tf_op jit(solution)/shard_map/ppermute | solution.py:18
  199.8 5.3 %collective-permute-start.6 = (bf16[16,512]{1,0:T(8,128)(2,1)S(1)}, bf16[16,512]{1,0:T(8,128)(2,1)S(1)}, u32[]{:S(2)}, u32[]{:S(2)}) collective-permute-start(bf16[16,512]{1,0:T(8,128)(2,1)S(1)} %get-tuple-element.26), channel_id=1, source_target_pairs={{0,4},{4,0},{1,5},{5,1},{2,6},{6,2},{3,7},{7,3},{8,12},{12,8},{9,1... | collective-permute-start | bytes 49160 | tf_op jit(solution)/shard_map/ppermute | solution.py:18
  205.1 5.5 %collective-permute-start.7 = (bf16[32,512]{1,0:T(8,128)(2,1)S(1)}, bf16[32,512]{1,0:T(8,128)(2,1)S(1)}, u32[]{:S(2)}, u32[]{:S(2)}) collective-permute-start(bf16[32,512]{1,0:T(8,128)(2,1)S(1)} %maximum_select_fusion.5), channel_id=1, source_target_pairs={{0,16},{8,24},{16,0},{24,8},{1,17},{9,25},{17,1},{25,9},{2,18},{10... | collective-permute-start | bytes 98312 | tf_op jit(solution)/shard_map/ppermute | solution.py:18
  210.6 4.4 %collective-permute-start.8 = (bf16[64,512]{1,0:T(8,128)(2,1)S(1)}, bf16[64,512]{1,0:T(8,128)(2,1)S(1)}, u32[]{:S(2)}, u32[]{:S(2)}) collective-permute-start(bf16[64,512]{1,0:T(8,128)(2,1)S(1)} %maximum_select_fusion.3), channel_id=1, source_target_pairs={{0,8},{8,0},{16,24},{24,16},{1,9},{9,1},{17,25},{25,17},{2,10},{10... | collective-permute-start | bytes 196616 | tf_op jit(solution)/shard_map/ppermute | solution.py:18
  215.7 112.5 %reduce-scatter.8.cloned.1.call-start = ((), (), s32[]{:S(2)}) async-start(), calls=%async_computation.7 | async-start | bytes 2506752 | tf_op jit(solution)/shard_map/reduce_scatter | solution.py:33
  276.4 5.0 %copy-start.5 = (f32[2048]{0:T(1024)}, f32[2048]{0:T(1024)S(1)}, u32[]{:S(2)}) copy-start(f32[2048]{0:T(1024)S(1)} %log_add_fusion) | copy-start | bytes 24580
  276.4 5.8 %copy-start.2 = (f32[2048,1024]{0,1:T(8,128)S(1)}, f32[2048,1024]{0,1:T(8,128)}, u32[]{:S(2)}) copy-start(f32[2048,1024]{0,1:T(8,128)} %get-tuple-element.31) | copy-start | bytes 25165828
  286.2 118.6 %all-gather.8.cloned.1.call-start = ((), (), s32[]{:S(2)}) async-start(), calls=%async_computation.8 | async-start | bytes 2359296 | tf_op jit(solution)/shard_map/all_gather | solution.py:50
  329.0 3.6 collective-permute-start.12
  331.4 5.1 %collective-permute-start.9 = (f32[64,512]{1,0:T(8,128)S(1)}, f32[64,512]{1,0:T(8,128)S(1)}, u32[]{:S(2)}, u32[]{:S(2)}) collective-permute-start(f32[64,512]{1,0:T(8,128)S(1)} %constant_dynamic-slice_fusion.3), channel_id=1, source_target_pairs={{0,8},{8,0},{16,24},{24,16},{1,9},{9,1},{17,25},{25,17},{2,10},{10... | collective-permute-start | bytes 393224 | tf_op jit(solution)/shard_map/ppermute | solution.py:18
  332.7 6.7 %collective-permute-start.13 = (f32[32]{0:T(128)S(1)}, f32[32]{0:T(128)S(1)}, u32[]{:S(2)}, u32[]{:S(2)}) collective-permute-start(f32[32]{0:T(128)S(1)} %dynamic_slice.109), channel_id=1, source_target_pairs={{0,16},{8,24},{16,0},{24,8},{1,17},{9,25},{17,1},{25,9},{2,18},{10... | collective-permute-start | bytes 392 | tf_op jit(solution)/shard_map/ppermute | solution.py:18
  336.5 5.9 %collective-permute-start.10 = (f32[32,512]{1,0:T(8,128)S(1)}, f32[32,512]{1,0:T(8,128)S(1)}, u32[]{:S(2)}, u32[]{:S(2)}) collective-permute-start(f32[32,512]{1,0:T(8,128)S(1)} %constant_dynamic-slice_fusion.2), channel_id=1, source_target_pairs={{0,16},{8,24},{16,0},{24,8},{1,17},{9,25},{17,1},{25,9},{2,18},{10... | collective-permute-start | bytes 196616 | tf_op jit(solution)/shard_map/ppermute | solution.py:18
  339.5 5.2 %collective-permute-start.14 = (f32[16]{0:T(128)S(1)}, f32[16]{0:T(128)S(1)}, u32[]{:S(2)}, u32[]{:S(2)}) collective-permute-start(f32[16]{0:T(128)S(1)} %dynamic_slice.111), channel_id=1, source_target_pairs={{0,4},{4,0},{1,5},{5,1},{2,6},{6,2},{3,7},{7,3},{8,12},{12,8},{9,1... | collective-permute-start | bytes 200 | tf_op jit(solution)/shard_map/ppermute | solution.py:18
  342.4 5.5 %collective-permute-start.11 = (f32[16,512]{1,0:T(8,128)S(1)}, f32[16,512]{1,0:T(8,128)S(1)}, u32[]{:S(2)}, u32[]{:S(2)}) collective-permute-start(f32[16,512]{1,0:T(8,128)S(1)} %constant_dynamic-slice_fusion.1), channel_id=1, source_target_pairs={{0,4},{4,0},{1,5},{5,1},{2,6},{6,2},{3,7},{7,3},{8,12},{12,8},{9,1... | collective-permute-start | bytes 98312 | tf_op jit(solution)/shard_map/ppermute | solution.py:18
  348.0 5.4 %collective-permute-start.15 = (f32[16,512]{1,0:T(8,128)S(1)}, f32[16,512]{1,0:T(8,128)S(1)}, u32[]{:S(2)}, u32[]{:S(2)}) collective-permute-start(f32[16,512]{1,0:T(8,128)S(1)} %add_divide_fusion), channel_id=1, source_target_pairs={{0,4},{4,0},{1,5},{5,1},{2,6},{6,2},{3,7},{7,3},{8,12},{12,8},{9,1... | collective-permute-start | bytes 98312 | tf_op jit(solution)/shard_map/ppermute | solution.py:18
  353.5 5.9 %collective-permute-start.16 = (f32[32,512]{1,0:T(8,128)S(1)}, f32[32,512]{1,0:T(8,128)S(1)}, u32[]{:S(2)}, u32[]{:S(2)}) collective-permute-start(f32[32,512]{1,0:T(8,128)S(1)} %maximum_select_fusion.4), channel_id=1, source_target_pairs={{0,16},{8,24},{16,0},{24,8},{1,17},{9,25},{17,1},{25,9},{2,18},{10... | collective-permute-start | bytes 196616 | tf_op jit(solution)/shard_map/ppermute | solution.py:18
  359.3 5.1 %collective-permute-start.17 = (f32[64,512]{1,0:T(8,128)S(1)}, f32[64,512]{1,0:T(8,128)S(1)}, u32[]{:S(2)}, u32[]{:S(2)}) collective-permute-start(f32[64,512]{1,0:T(8,128)S(1)} %maximum_select_fusion.2), channel_id=1, source_target_pairs={{0,8},{8,0},{16,24},{24,16},{1,9},{9,1},{17,25},{25,17},{2,10},{10... | collective-permute-start | bytes 393224 | tf_op jit(solution)/shard_map/ppermute | solution.py:18
Sparse Core Ops, SparseCore 0:
  15.0 49.1 reduce-scatter.3
  66.6 32.5 all-gather.3
  134.9 44.0 reduce-scatter.5
  215.8 37.0 all-gather.5
  286.4 41.7 reduce-scatter.7
  365.3 39.5 all-gather.7

commit v4 on v3

--- a/solution.py
+++ b/solution.py
@@ -56,17 +56,26 @@
     return lax.axis_index("z") * (count // 8) + (y & 1) * (4 * per) + ((y >> 1) & 1) * (2 * per) + lax.axis_index("xh") * per
 
 
+def _project(embeddings, basis):
+    partial = jnp.dot(embeddings, basis, preferred_element_type=jnp.float32)
+    steps = ((lax.axis_index("core"), "core"), (lax.axis_index("xl"), "xl"))
+    for bit, axis in steps:
+        half = partial.shape[0] // 2
+        keep = lax.dynamic_slice_in_dim(partial, bit * half, half, axis=0)
+        send = lax.dynamic_slice_in_dim(partial, (1 - bit) * half, half, axis=0)
+        partial = keep + lax.ppermute(send, axis, [(0, 1), (1, 0)])
+    block = partial.astype(jnp.bfloat16)
+    for bit, axis in reversed(steps):
+        other = lax.ppermute(block, axis, [(0, 1), (1, 0)])
+        block = jnp.where(bit == 0, jnp.concatenate([block, other]), jnp.concatenate([other, block]))
+    return block
+
+
 def on_device(embeddings, basis, start_centroids):
     row_count = embeddings.shape[0]
     count = start_centroids.shape[0]
     per = count // 64
-    proj_share = lax.psum_scatter(
-        jnp.dot(embeddings, basis, preferred_element_type=jnp.float32),
-        CENT_AXES,
-        scatter_dimension=0,
-        tiled=True,
-    )
-    projected = lax.all_gather(proj_share.astype(jnp.bfloat16), CENT_AXES, axis=0, tiled=True)
+    projected = _project(embeddings, basis)
     start = _row_offset(count)
     block = lax.dynamic_slice_in_dim(start_centroids, start, per, axis=0)
     cent_bf = start_centroids.astype(jnp.bfloat16)

time: 415 us -> 386 us (0.930)
  waiting for transfers between devices: 273 us -> 235 us
    reduce_scatter x1 -> x0, waiting for transfers between devices: 49.2 us -> none  [on_device(): lax.psum_scatter(jnp.dot(embeddings, basis, preferred_element_type=jnp.fl...]
    ppermute x0 -> x4, waiting for transfers between devices: none -> 42.5 us  [the longest x2 28 us: _project(): partial = keep + lax.ppermute(send, axis, [(0, 1), (1, 0)])]
    all_gather x1 -> x0, waiting for transfers between devices: 32.8 us -> none  [on_device(): lax.all_gather(proj_share.astype(jnp.bfloat16), CENT_AXES, axis=0, tiled=...]
    ppermute x0 -> x4, starting transfers between devices: none -> 4.17 us  [the longest x2 2.33 us: _project(): partial = keep + lax.ppermute(send, axis, [(0, 1), (1, 0)])]
  transfers between devices with their start and end apart: 24 -> 26, of which waited for: 21 -> 24; matrix products, arithmetic and copies ran while one was open for 1% -> 1% of each run, Pallas kernels for 0% -> 0%
where the time goes in v4:
time: 386 us; the launch traced here: 385 us
  waiting for transfers between devices  235 us (61%)
  starting transfers between devices  42.1 us (11%)
  other arithmetic  32 us (8%)
  blocking collectives  25.3 us (7%)
  matrix products  24.1 us (6%)
  between operations  14.1 us (4%)
  local copies, waits for them, and re-layouts  12.8 us (3%)
    reduce_scatter x2, waiting for transfers between devices, _reduce_rows(): payload = lax.psum_scatter(payload, 'z', scatter_dimension=0, tiled=True)  86.5 us
    all_gather x2, waiting for transfers between devices, _gather_rows(): return lax.all_gather(block, 'z', axis=0, tiled=True)  76.7 us
    ppermute x18, starting transfers between devices, _swap(): return lax.ppermute(x, axis, [(i, i ^ bit) for i in range(size)])  37.8 us
    ppermute x18, waiting for transfers between devices, _swap(): return lax.ppermute(x, axis, [(i, i ^ bit) for i in range(size)])  28.9 us
    ppermute x2, waiting for transfers between devices, _project(): partial = keep + lax.ppermute(send, axis, [(0, 1), (1, 0)])  28 us
    dot_general x2, matrix products, on_device(): lax.dot_general(projected, cent_bf, (((1,), (1,)), ((), ())), preferred_e...  14.7 us
    ppermute x2, waiting for transfers between devices, _project(): other = lax.ppermute(block, axis, [(0, 1), (1, 0)])  14.5 us
    pmax x2, blocking collectives, on_device(): top = lax.pmax(local_top, CENT_AXES)  13.2 us
  transfers between devices with their start and end apart: 26, of which 24 were waited for; matrix products, arithmetic and copies ran while one was open for 1% of the time, Pallas kernels for 0%

profile of v4, /device:TPU:2, one launch (start us, length us, event | category | flops | bytes accessed | tf_op | source)
XLA Modules:
  0.0 385.1 jit_solution(8818639247940230902)
XLA Ops:
  8.4 4.5 %fusion.24 = f32[2048,512]{1,0:T(8,128)S(1)} fusion(bf16[2048,1024]{1,0:T(8,128)(2,1)} %param.7, bf16[1024,512]{1,0:T(8,128)(2,1)S(1)} %copy-done), kind=kOutput, calls=%fused_computation.65 | convolution fusion | flops 2147483648 | bytes 9437184 | tf_op jit(solution)/shard_map/dot_general | solution.py:60
  12.9 1.9 copy-done.3
  15.2 4.3 %collective-permute-done = f32[1024,512]{1,0:T(8,128)} collective-permute-done((f32[1024,512]{1,0:T(8,128)S(1)}, f32[1024,512]{1,0:T(8,128)}, u32[]{:S(2)}, u32[]{:S(2)}) %collective-permute-start) | collective-permute-done | bytes 2097184 | tf_op jit(solution)/shard_map/ppermute | solution.py:66
  19.4 2.7 dynamic-slice_add_fusion
  23.2 2.2 collective-permute-start.1
  25.4 23.8 %collective-permute-done.1 = f32[512,512]{1,0:T(8,128)} collective-permute-done((f32[512,512]{1,0:T(8,128)}, f32[512,512]{1,0:T(8,128)}, u32[]{:S(2)}, u32[]{:S(2)}) %collective-permute-start.1) | collective-permute-done | bytes 1048608 | tf_op jit(solution)/shard_map/ppermute | solution.py:66
  49.2 2.2 add_convert_fusion
  51.4 1.7 collective-permute-start.2
  53.1 11.9 %collective-permute-done.2 = bf16[512,512]{1,0:T(8,128)(2,1)S(1)} collective-permute-done((bf16[512,512]{1,0:T(8,128)(2,1)}, bf16[512,512]{1,0:T(8,128)(2,1)S(1)}, u32[]{:S(2)}, u32[]{:S(2)}) %collective-permute-start.2) | collective-permute-done | bytes 524320 | tf_op jit(solution)/shard_map/ppermute | solution.py:69
  65.0 1.6 maximum_select_fusion.1
  66.6 2.6 collective-permute-done.3
  69.3 7.6 %multiply_reduce_fusion.1 = (f32[2048]{0:T(1024)S(1)}, f32[2048,1024]{0,1:T(8,128)}) fusion(f32[1024,512]{1,0:T(8,128)} %param.9, bf16[1024,512]{1,0:T(8,128)(2,1)S(1)} %collective-permute-done.3, bf16[1024,512]{1,0:T(8,128)(2,1)S(1)} %maximum_select_fusion.1, pred[]{:T(512)S(6)} %eq.21), kind=kOutput, calls=%fused_computation.9 | convolution fusion | flops 2161637376 | bytes 12591105 | tf_op jit(solution)/shard_map/dot_general | solution.py:85
  76.9 6.9 %pmax.14 = f32[2048]{0:T(1024)S(1)} all-reduce(f32[2048]{0:T(1024)S(1)} %get-tuple-element.28), channel_id=1, replica_groups=mesh['z'=8,'y'=4,'xh'=2,'xl'=2,'core'=2] {'xl','core'}, use_global_device_ids=true, to_apply=%region_1.2 | all-reduce | flops 2048 | bytes 16384 | tf_op jit(solution)/shard_map/pmax | solution.py:91
  83.8 4.8 %exponential_reduce_fusion.1 = f32[2048]{0:T(1024)S(1)} fusion(f32[2048,1024]{0,1:T(8,128)} %get-tuple-element.29, f32[2048]{0:T(1024)S(1)} %pmax.14), kind=kLoop, calls=%fused_computation.3 | loop fusion | flops 6289408 | bytes 8404992 | tf_op jit(solution)/shard_map/reduce_sum | solution.py:92
  88.6 6.3 %psum.14 = f32[2048]{0:T(1024)S(1)} all-reduce(f32[2048]{0:T(1024)S(1)} %exponential_reduce_fusion.1), channel_id=1, replica_groups=mesh['z'=8,'y'=4,'xh'=2,'xl'=2,'core'=2] {'xl','core'}, use_global_device_ids=true, to_apply=%region_3.4 | all-reduce | flops 2048 | bytes 16384 | tf_op jit(solution)/shard_map/psum | solution.py:92
  94.9 5.0 %fusion = f32[1024]{0:T(1024)S(1)} fusion(f32[2048,1024]{0,1:T(8,128)} %get-tuple-element.29, f32[2048]{0:T(1024)S(1)} %log_add_fusion.1), kind=kLoop, calls=%fused_computation.4 | loop fusion | flops 6290432 | bytes 8400896 | tf_op jit(solution)/shard_map/reduce_sum | solution.py:95
  100.6 2.4 fusion.6
  104.7 44.5 %reduce-scatter.3.cloned.1.call-done = f32[136,512]{1,0:T(8,128)} async-done(((f32[1088,512]{1,0:T(8,128)}), f32[136,512]{1,0:T(8,128)}) %reduce-scatter.3.cloned.1.call-update) | async-done | bytes 278544 | tf_op jit(solution)/shard_map/reduce_scatter | solution.py:33
  153.7 3.4 collective-permute-start.8
  157.6 3.1 collective-permute-start.5
  160.8 1.9 collective-permute-start.9
  163.5 2.2 collective-permute-start.6
  165.9 3.0 collective-permute-done.6
  169.8 2.2 collective-permute-start.10
  172.0 3.1 collective-permute-done.10
  175.1 3.1 collective-permute-start.11
  178.2 2.4 collective-permute-done.11
  181.7 3.3 collective-permute-done.12
  185.7 37.3 %all-gather.3.cloned.1.call-done = bf16[1024,512]{1,0:T(8,128)(2,1)} async-done(((bf16[128,512]{1,0:T(8,128)(2,1)}), bf16[1024,512]{1,0:T(8,128)(2,1)}) %all-gather.3.cloned.1.call-update) | async-done | bytes 1048592 | tf_op jit(solution)/shard_map/all_gather | solution.py:50
  223.0 7.2 %multiply_reduce_fusion = (f32[2048]{0:T(1024)S(1)}, f32[2048,1024]{0,1:T(8,128)}) fusion(bf16[1024,512]{1,0:T(8,128)(2,1)} %all-gather.3.cloned.1.call-done, bf16[1024,512]{1,0:T(8,128)(2,1)S(1)} %collective-permute-done.3, bf16[1024,512]{1,0:T(8,128)(2,1)S(1)} %maximum_select_fusion.1, pred[]{:T(512)S(6)} %eq.21), kind=kOutput, calls=%fused_computation.8 | convolution fusion | flops 2161113088 | bytes 11542529 | tf_op jit(solution)/shard_map/dot_general | solution.py:85
  230.2 6.2 %pmax.15 = f32[2048]{0:T(1024)S(1)} all-reduce(f32[2048]{0:T(1024)S(1)} %get-tuple-element.30), channel_id=1, replica_groups=mesh['z'=8,'y'=4,'xh'=2,'xl'=2,'core'=2] {'xl','core'}, use_global_device_ids=true, to_apply=%region_7.8 | all-reduce | flops 2048 | bytes 16384 | tf_op jit(solution)/shard_map/pmax | solution.py:91
  236.4 4.8 %exponential_reduce_fusion = f32[2048]{0:T(1024)S(1)} fusion(f32[2048,1024]{0,1:T(8,128)} %get-tuple-element.31, f32[2048]{0:T(1024)S(1)} %pmax.15), kind=kLoop, calls=%fused_computation.1 | loop fusion | flops 6289408 | bytes 8404992 | tf_op jit(solution)/shard_map/reduce_sum | solution.py:92
  241.2 5.9 %psum.15 = f32[2048]{0:T(1024)S(1)} all-reduce(f32[2048]{0:T(1024)S(1)} %exponential_reduce_fusion), channel_id=1, replica_groups=mesh['z'=8,'y'=4,'xh'=2,'xl'=2,'core'=2] {'xl','core'}, use_global_device_ids=true, to_apply=%region_9.10 | all-reduce | flops 2048 | bytes 16384 | tf_op jit(solution)/shard_map/psum | solution.py:92
  247.1 5.0 %fusion.2 = f32[1024]{0:T(1024)S(1)} fusion(f32[2048,1024]{0,1:T(8,128)} %get-tuple-element.31, f32[2048]{0:T(1024)S(1)} %log_add_fusion), kind=kLoop, calls=%fused_computation.6 | loop fusion | flops 6290432 | bytes 8400896 | tf_op jit(solution)/shard_map/reduce_sum | solution.py:95
  252.9 2.4 fusion.4
  257.0 41.9 %reduce-scatter.5.cloned.1.call-done = f32[136,512]{1,0:T(8,128)} async-done(((f32[1088,512]{1,0:T(8,128)}), f32[136,512]{1,0:T(8,128)}) %reduce-scatter.5.cloned.1.call-update) | async-done | bytes 278544 | tf_op jit(solution)/shard_map/reduce_scatter | solution.py:33
  303.4 3.5 collective-permute-start.17
  307.4 2.9 collective-permute-start.14
  310.4 2.1 collective-permute-start.18
  313.3 2.1 collective-permute-start.15
  315.6 3.2 collective-permute-done.15
  318.9 2.1 collective-permute-start.19
  321.0 3.4 collective-permute-done.19
  324.3 2.9 collective-permute-start.20
  327.2 3.0 collective-permute-done.20
  331.2 4.1 %collective-permute-done.21 = f32[64,512]{1,0:T(8,128)S(1)} collective-permute-done((f32[64,512]{1,0:T(8,128)S(1)}, f32[64,512]{1,0:T(8,128)S(1)}, u32[]{:S(2)}, u32[]{:S(2)}) %collective-permute-start.21) | collective-permute-done | bytes 131104 | tf_op jit(solution)/shard_map/ppermute | solution.py:18
  336.0 39.4 %all-gather.5.cloned.1.call-done = f32[1024,512]{1,0:T(8,128)} async-done(((f32[128,512]{1,0:T(8,128)}), f32[1024,512]{1,0:T(8,128)}) %all-gather.5.cloned.1.call-update) | async-done | bytes 2097168 | tf_op jit(solution)/shard_map/all_gather | solution.py:50
  375.4 3.1 copy.6
  (75 shorter events, 23.9 us)
Async XLA Ops:
  7.2 1.2 copy-start
  7.2 142.1 %reduce-scatter.3.cloned.1.call-start = ((), (), s32[]{:S(2)}) async-start(), calls=%async_computation.2 | async-start | bytes 2506752 | tf_op jit(solution)/shard_map/reduce_scatter | solution.py:33
  12.9 1.9 copy-start.3
  15.1 4.4 %collective-permute-start = (f32[1024,512]{1,0:T(8,128)S(1)}, f32[1024,512]{1,0:T(8,128)}, u32[]{:S(2)}, u32[]{:S(2)}) collective-permute-start(f32[1024,512]{1,0:T(8,128)S(1)} %constant_dynamic-slice_fusion.11), channel_id=1, source_target_pairs={{0,1},{1,0},{2,3},{3,2},{4,5},{5,4},{6,7},{7,6},{8,9},{9,8},{10,11... | collective-permute-start | bytes 6291464 | tf_op jit(solution)/shard_map/ppermute | solution.py:66
  23.2 26.0 %collective-permute-start.1 = (f32[512,512]{1,0:T(8,128)}, f32[512,512]{1,0:T(8,128)}, u32[]{:S(2)}, u32[]{:S(2)}) collective-permute-start(f32[512,512]{1,0:T(8,128)} %constant_dynamic-slice_fusion.10), channel_id=1, source_target_pairs={{0,2},{2,0},{1,3},{3,1},{4,6},{6,4},{5,7},{7,5},{8,10},{10,8},{9,1... | collective-permute-start | bytes 3145736 | tf_op jit(solution)/shard_map/ppermute | solution.py:66
  51.4 13.6 %collective-permute-start.2 = (bf16[512,512]{1,0:T(8,128)(2,1)}, bf16[512,512]{1,0:T(8,128)(2,1)S(1)}, u32[]{:S(2)}, u32[]{:S(2)}) collective-permute-start(bf16[512,512]{1,0:T(8,128)(2,1)} %add_convert_fusion), channel_id=1, source_target_pairs={{0,2},{2,0},{1,3},{3,1},{4,6},{6,4},{5,7},{7,5},{8,10},{10,8},{9,1... | collective-permute-start | bytes 1572872 | tf_op jit(solution)/shard_map/ppermute | solution.py:69
  66.5 2.7 collective-permute-start.3
  94.9 5.8 %copy-start.2 = (f32[2048,1024]{0,1:T(8,128)S(1)}, f32[2048,1024]{0,1:T(8,128)}, u32[]{:S(2)}) copy-start(f32[2048,1024]{0,1:T(8,128)} %get-tuple-element.29) | copy-start | bytes 25165828
  104.6 118.4 %all-gather.3.cloned.1.call-start = ((), (), s32[]{:S(2)}) async-start(), calls=%async_computation.3 | async-start | bytes 1179648 | tf_op jit(solution)/shard_map/all_gather | solution.py:50
  150.0 3.6 collective-permute-start.7
  152.5 5.1 %collective-permute-start.4 = (f32[64,512]{1,0:T(8,128)S(1)}, f32[64,512]{1,0:T(8,128)S(1)}, u32[]{:S(2)}, u32[]{:S(2)}) collective-permute-start(f32[64,512]{1,0:T(8,128)S(1)} %constant_dynamic-slice_fusion.9), channel_id=1, source_target_pairs={{0,8},{8,0},{16,24},{24,16},{1,9},{9,1},{17,25},{25,17},{2,10},{10... | collective-permute-start | bytes 393224 | tf_op jit(solution)/shard_map/ppermute | solution.py:18
  153.7 6.9 %collective-permute-start.8 = (f32[32]{0:T(128)S(1)}, f32[32]{0:T(128)S(1)}, u32[]{:S(2)}, u32[]{:S(2)}) collective-permute-start(f32[32]{0:T(128)S(1)} %dynamic_slice.111), channel_id=1, source_target_pairs={{0,16},{8,24},{16,0},{24,8},{1,17},{9,25},{17,1},{25,9},{2,18},{10... | collective-permute-start | bytes 392 | tf_op jit(solution)/shard_map/ppermute | solution.py:18
  157.6 5.9 %collective-permute-start.5 = (f32[32,512]{1,0:T(8,128)S(1)}, f32[32,512]{1,0:T(8,128)S(1)}, u32[]{:S(2)}, u32[]{:S(2)}) collective-permute-start(f32[32,512]{1,0:T(8,128)S(1)} %constant_dynamic-slice_fusion.8), channel_id=1, source_target_pairs={{0,16},{8,24},{16,0},{24,8},{1,17},{9,25},{17,1},{25,9},{2,18},{10... | collective-permute-start | bytes 196616 | tf_op jit(solution)/shard_map/ppermute | solution.py:18
  160.8 5.1 %collective-permute-start.9 = (f32[16]{0:T(128)S(1)}, f32[16]{0:T(128)S(1)}, u32[]{:S(2)}, u32[]{:S(2)}) collective-permute-start(f32[16]{0:T(128)S(1)} %dynamic_slice.113), channel_id=1, source_target_pairs={{0,4},{4,0},{1,5},{5,1},{2,6},{6,2},{3,7},{7,3},{8,12},{12,8},{9,1... | collective-permute-start | bytes 200 | tf_op jit(solution)/shard_map/ppermute | solution.py:18
  163.5 5.5 %collective-permute-start.6 = (f32[16,512]{1,0:T(8,128)S(1)}, f32[16,512]{1,0:T(8,128)S(1)}, u32[]{:S(2)}, u32[]{:S(2)}) collective-permute-start(f32[16,512]{1,0:T(8,128)S(1)} %constant_dynamic-slice_fusion.6), channel_id=1, source_target_pairs={{0,4},{4,0},{1,5},{5,1},{2,6},{6,2},{3,7},{7,3},{8,12},{12,8},{9,1... | collective-permute-start | bytes 98312 | tf_op jit(solution)/shard_map/ppermute | solution.py:18
  169.8 5.3 %collective-permute-start.10 = (bf16[16,512]{1,0:T(8,128)(2,1)S(1)}, bf16[16,512]{1,0:T(8,128)(2,1)S(1)}, u32[]{:S(2)}, u32[]{:S(2)}) collective-permute-start(bf16[16,512]{1,0:T(8,128)(2,1)S(1)} %get-tuple-element.26), channel_id=1, source_target_pairs={{0,4},{4,0},{1,5},{5,1},{2,6},{6,2},{3,7},{7,3},{8,12},{12,8},{9,1... | collective-permute-start | bytes 49160 | tf_op jit(solution)/shard_map/ppermute | solution.py:18
  175.1 5.5 %collective-permute-start.11 = (bf16[32,512]{1,0:T(8,128)(2,1)S(1)}, bf16[32,512]{1,0:T(8,128)(2,1)S(1)}, u32[]{:S(2)}, u32[]{:S(2)}) collective-permute-start(bf16[32,512]{1,0:T(8,128)(2,1)S(1)} %maximum_select_fusion.7), channel_id=1, source_target_pairs={{0,16},{8,24},{16,0},{24,8},{1,17},{9,25},{17,1},{25,9},{2,18},{10... | collective-permute-start | bytes 98312 | tf_op jit(solution)/shard_map/ppermute | solution.py:18
  180.6 4.4 %collective-permute-start.12 = (bf16[64,512]{1,0:T(8,128)(2,1)S(1)}, bf16[64,512]{1,0:T(8,128)(2,1)S(1)}, u32[]{:S(2)}, u32[]{:S(2)}) collective-permute-start(bf16[64,512]{1,0:T(8,128)(2,1)S(1)} %maximum_select_fusion.5), channel_id=1, source_target_pairs={{0,8},{8,0},{16,24},{24,16},{1,9},{9,1},{17,25},{25,17},{2,10},{10... | collective-permute-start | bytes 196616 | tf_op jit(solution)/shard_map/ppermute | solution.py:18
  185.7 113.2 %reduce-scatter.5.cloned.1.call-start = ((), (), s32[]{:S(2)}) async-start(), calls=%async_computation.4 | async-start | bytes 2506752 | tf_op jit(solution)/shard_map/reduce_scatter | solution.py:33
  247.1 5.0 %copy-start.4 = (f32[2048]{0:T(1024)}, f32[2048]{0:T(1024)S(1)}, u32[]{:S(2)}) copy-start(f32[2048]{0:T(1024)S(1)} %log_add_fusion) | copy-start | bytes 24580
  247.1 5.8 %copy-start.1 = (f32[2048,1024]{0,1:T(8,128)S(1)}, f32[2048,1024]{0,1:T(8,128)}, u32[]{:S(2)}) copy-start(f32[2048,1024]{0,1:T(8,128)} %get-tuple-element.31) | copy-start | bytes 25165828
  256.9 118.5 %all-gather.5.cloned.1.call-start = ((), (), s32[]{:S(2)}) async-start(), calls=%async_computation.5 | async-start | bytes 2359296 | tf_op jit(solution)/shard_map/all_gather | solution.py:50
  299.6 3.6 collective-permute-start.16
  302.1 5.2 %collective-permute-start.13 = (f32[64,512]{1,0:T(8,128)S(1)}, f32[64,512]{1,0:T(8,128)S(1)}, u32[]{:S(2)}, u32[]{:S(2)}) collective-permute-start(f32[64,512]{1,0:T(8,128)S(1)} %constant_dynamic-slice_fusion.3), channel_id=1, source_target_pairs={{0,8},{8,0},{16,24},{24,16},{1,9},{9,1},{17,25},{25,17},{2,10},{10... | collective-permute-start | bytes 393224 | tf_op jit(solution)/shard_map/ppermute | solution.py:18
  303.4 6.9 %collective-permute-start.17 = (f32[32]{0:T(128)S(1)}, f32[32]{0:T(128)S(1)}, u32[]{:S(2)}, u32[]{:S(2)}) collective-permute-start(f32[32]{0:T(128)S(1)} %dynamic_slice.125), channel_id=1, source_target_pairs={{0,16},{8,24},{16,0},{24,8},{1,17},{9,25},{17,1},{25,9},{2,18},{10... | collective-permute-start | bytes 392 | tf_op jit(solution)/shard_map/ppermute | solution.py:18
  307.4 5.9 %collective-permute-start.14 = (f32[32,512]{1,0:T(8,128)S(1)}, f32[32,512]{1,0:T(8,128)S(1)}, u32[]{:S(2)}, u32[]{:S(2)}) collective-permute-start(f32[32,512]{1,0:T(8,128)S(1)} %constant_dynamic-slice_fusion.2), channel_id=1, source_target_pairs={{0,16},{8,24},{16,0},{24,8},{1,17},{9,25},{17,1},{25,9},{2,18},{10... | collective-permute-start | bytes 196616 | tf_op jit(solution)/shard_map/ppermute | solution.py:18
  310.4 5.1 %collective-permute-start.18 = (f32[16]{0:T(128)S(1)}, f32[16]{0:T(128)S(1)}, u32[]{:S(2)}, u32[]{:S(2)}) collective-permute-start(f32[16]{0:T(128)S(1)} %dynamic_slice.127), channel_id=1, source_target_pairs={{0,4},{4,0},{1,5},{5,1},{2,6},{6,2},{3,7},{7,3},{8,12},{12,8},{9,1... | collective-permute-start | bytes 200 | tf_op jit(solution)/shard_map/ppermute | solution.py:18
  313.3 5.5 %collective-permute-start.15 = (f32[16,512]{1,0:T(8,128)S(1)}, f32[16,512]{1,0:T(8,128)S(1)}, u32[]{:S(2)}, u32[]{:S(2)}) collective-permute-start(f32[16,512]{1,0:T(8,128)S(1)} %constant_dynamic-slice_fusion.1), channel_id=1, source_target_pairs={{0,4},{4,0},{1,5},{5,1},{2,6},{6,2},{3,7},{7,3},{8,12},{12,8},{9,1... | collective-permute-start | bytes 98312 | tf_op jit(solution)/shard_map/ppermute | solution.py:18
  318.9 5.4 %collective-permute-start.19 = (f32[16,512]{1,0:T(8,128)S(1)}, f32[16,512]{1,0:T(8,128)S(1)}, u32[]{:S(2)}, u32[]{:S(2)}) collective-permute-start(f32[16,512]{1,0:T(8,128)S(1)} %add_divide_fusion), channel_id=1, source_target_pairs={{0,4},{4,0},{1,5},{5,1},{2,6},{6,2},{3,7},{7,3},{8,12},{12,8},{9,1... | collective-permute-start | bytes 98312 | tf_op jit(solution)/shard_map/ppermute | solution.py:18
  324.3 5.9 %collective-permute-start.20 = (f32[32,512]{1,0:T(8,128)S(1)}, f32[32,512]{1,0:T(8,128)S(1)}, u32[]{:S(2)}, u32[]{:S(2)}) collective-permute-start(f32[32,512]{1,0:T(8,128)S(1)} %maximum_select_fusion.6), channel_id=1, source_target_pairs={{0,16},{8,24},{16,0},{24,8},{1,17},{9,25},{17,1},{25,9},{2,18},{10... | collective-permute-start | bytes 196616 | tf_op jit(solution)/shard_map/ppermute | solution.py:18
  330.2 5.1 %collective-permute-start.21 = (f32[64,512]{1,0:T(8,128)S(1)}, f32[64,512]{1,0:T(8,128)S(1)}, u32[]{:S(2)}, u32[]{:S(2)}) collective-permute-start(f32[64,512]{1,0:T(8,128)S(1)} %maximum_select_fusion.4), channel_id=1, source_target_pairs={{0,8},{8,0},{16,24},{24,16},{1,9},{9,1},{17,25},{25,17},{2,10},{10... | collective-permute-start | bytes 393224 | tf_op jit(solution)/shard_map/ppermute | solution.py:18
Sparse Core Ops, SparseCore 0:
  104.7 44.4 reduce-scatter.2
  185.8 37.1 all-gather.2
  257.0 41.8 reduce-scatter.4
  336.1 39.2 all-gather.4

commit v5 on v4

--- a/solution.py
+++ b/solution.py
@@ -47,7 +47,26 @@
     for bit, axis, mask in reversed(_bits()):
         other = _swap(block, axis, mask)
         block = jnp.where(bit == 0, jnp.concatenate([block, other]), jnp.concatenate([other, block]))
-    return lax.all_gather(block, "z", axis=0, tiled=True)
+    return _ring_gather_z(block)
+
+
+def _ring_gather_z(block):
+    n = 8
+    rows = block.shape[0]
+    up = [(i, (i + 1) % n) for i in range(n)]
+    down = [(i, (i - 1) % n) for i in range(n)]
+    cw, ccw = block, block
+    before, after = [], []
+    for k in range(1, n // 2 + 1):
+        cw = lax.ppermute(cw, "z", up)
+        before.append(cw)
+        if k < n // 2:
+            ccw = lax.ppermute(ccw, "z", down)
+            after.append(ccw)
+    stacked = jnp.concatenate(list(reversed(before)) + [block] + after, axis=0)
+    doubled = jnp.concatenate([stacked, stacked], axis=0)
+    shift = (n // 2 - lax.axis_index("z")) % n
+    return lax.dynamic_slice_in_dim(doubled, shift * rows, n * rows, axis=0)
 
 
 def _row_offset(count):
@@ -78,9 +97,11 @@
     projected = _project(embeddings, basis)
     start = _row_offset(count)
     block = lax.dynamic_slice_in_dim(start_centroids, start, per, axis=0)
-    cent_bf = start_centroids.astype(jnp.bfloat16)
     log_total = jnp.zeros((row_count,), jnp.float32)
-    for step in range(ITERS):
+
+    def one_step(_, carry):
+        block, centroids, log_total = carry
+        cent_bf = centroids.astype(jnp.bfloat16)
         scores = (
             lax.dot_general(
                 projected, cent_bf, (((1,), (1,)), ((), ())), preferred_element_type=jnp.float32
@@ -101,9 +122,9 @@
         )
         numer, mass = _reduce_rows(local_numer, local_mass)
         block = (numer + block) / (mass[:, None] + 1.0)
-        if step + 1 < ITERS:
-            cent_bf = _gather_rows(block.astype(jnp.bfloat16))
-    centroids = _gather_rows(block)
+        return block, _gather_rows(block), log_total
+
+    _, centroids, log_total = lax.fori_loop(0, ITERS, one_step, (block, start_centroids, log_total))
     return (centroids, log_total)
 
 

time: 386 us -> 413 us (1.070)
  waiting for transfers between devices: 235 us -> 208 us
  local copies, waits for them, and re-layouts: 12.8 us -> 34.9 us
  starting transfers between devices: 42.1 us -> 64 us
  matrix products: 24.1 us -> 31.2 us
    all_gather x2 -> x0, waiting for transfers between devices: 76.7 us -> none  [_gather_rows(): return lax.all_gather(block, 'z', axis=0, tiled=True)]
    ppermute x0 -> x14, waiting for transfers between devices: none -> 48.8 us  [the longest x8 48.8 us: _ring_gather_z(): cw = lax.ppermute(cw, 'z', up)]
    ppermute x0 -> x14, starting transfers between devices: none -> 22.3 us  [the longest x6 19.8 us: _ring_gather_z(): ccw = lax.ppermute(ccw, 'z', down)]
    while x0 -> x54, local copies, waits for them, and re-layouts: none -> 19.6 us
    reduce_sum x4, other arithmetic: 19.5 us -> 12.5 us  [the longest x2 9.57 us: one_step(): total = lax.psum(jnp.sum(jnp.exp(scores - top[:, None]), axis=1), CENT_AXES)]
    dot_general x4, matrix products: 19.6 us -> 26.1 us  [the longest x2 14.4 us: one_step(): lax.dot_general(projected, cent_bf, (((1,), (1,)), ((), ())), preferred_e...]
  transfers between devices with their start and end apart: 26 -> 38, of which waited for: 24 -> 30; matrix products, arithmetic and copies ran while one was open for 1% -> 4% of each run, Pallas kernels for 0% -> 0%
where the time goes in v5:
time: 413 us; the launch traced here: 412 us
  waiting for transfers between devices  208 us (50%)
  starting transfers between devices  64 us (15%)
  local copies, waits for them, and re-layouts  34.9 us (8%)
  other arithmetic  33.6 us (8%)
  matrix products  31.2 us (8%)
  blocking collectives  24.7 us (6%)
  between operations  14.1 us (3%)
    reduce_scatter x2, waiting for transfers between devices, _reduce_rows(): payload = lax.psum_scatter(payload, 'z', scatter_dimension=0, tiled=True)  87 us
    ppermute x8, waiting for transfers between devices, _ring_gather_z(): cw = lax.ppermute(cw, 'z', up)  48.8 us
    ppermute x18, starting transfers between devices, _swap(): return lax.ppermute(x, axis, [(i, i ^ bit) for i in range(size)])  37.6 us
    ppermute x18, waiting for transfers between devices, _swap(): return lax.ppermute(x, axis, [(i, i ^ bit) for i in range(size)])  29.9 us
    ppermute x2, waiting for transfers between devices, _project(): partial = keep + lax.ppermute(send, axis, [(0, 1), (1, 0)])  28.3 us
    ppermute x6, starting transfers between devices, _ring_gather_z(): ccw = lax.ppermute(ccw, 'z', down)  19.8 us
    while x54, local copies, waits for them, and re-layouts  19.6 us
    dot_general x2, matrix products, one_step(): lax.dot_general(projected, cent_bf, (((1,), (1,)), ((), ())), preferred_e...  14.4 us
  transfers between devices with their start and end apart: 38, of which 30 were waited for; matrix products, arithmetic and copies ran while one was open for 4% of the time, Pallas kernels for 0%

profile of v5, /device:TPU:2, one launch (start us, length us, event | category | flops | bytes accessed | tf_op | source)
XLA Modules:
  0.0 411.6 jit_solution(6142969600070392172)
XLA Ops:
  9.0 5.1 %fusion.12 = f32[2048,512]{1,0:T(8,128)S(1)} fusion(bf16[2048,1024]{1,0:T(8,128)(2,1)} %param.7, bf16[1024,512]{1,0:T(8,128)(2,1)S(1)} %copy-done), kind=kOutput, calls=%fused_computation.54 | convolution fusion | flops 2147483648 | bytes 9437184 | tf_op jit(solution)/shard_map/dot_general | solution.py:79
  17.6 4.5 %collective-permute-done.16 = f32[1024,512]{1,0:T(8,128)} collective-permute-done((f32[1024,512]{1,0:T(8,128)}, f32[1024,512]{1,0:T(8,128)}, u32[]{:S(2)}, u32[]{:S(2)}) %collective-permute-start.16) | collective-permute-done | bytes 2097184 | tf_op jit(solution)/shard_map/ppermute | solution.py:85
  22.1 2.7 dynamic-slice_add_fusion.3
  29.5 23.8 %collective-permute-done.17 = f32[512,512]{1,0:T(8,128)} collective-permute-done((f32[512,512]{1,0:T(8,128)}, f32[512,512]{1,0:T(8,128)}, u32[]{:S(2)}, u32[]{:S(2)}) %collective-permute-start.17) | collective-permute-done | bytes 1048608 | tf_op jit(solution)/shard_map/ppermute | solution.py:85
  57.5 12.0 %collective-permute-done.18 = bf16[512,512]{1,0:T(8,128)(2,1)} collective-permute-done((bf16[512,512]{1,0:T(8,128)(2,1)}, bf16[512,512]{1,0:T(8,128)(2,1)}, u32[]{:S(2)}, u32[]{:S(2)}) %collective-permute-start.18) | collective-permute-done | bytes 524320 | tf_op jit(solution)/shard_map/ppermute | solution.py:88
  69.5 2.8 maximum_select_fusion.4
  75.3 2.8 maximum_select_fusion.3
  78.1 326.6 %while.17 = (s32[]{:T(128)}, f32[16,512]{1,0:T(8,128)}, f32[1024,512]{1,0:T(8,128)}, f32[2048]{0:T(1024)}, bf16[2048,512]{1,0:T(8,128)(2,1)S(1)}, /*index=5*/s32...) while((s32[]{:T(128)}, f32[16,512]{1,0:T(8,128)}, ...), condition=%wide.region_7.8_spmd, body=%wide.region_0.7_spmd.sunk | while | flops 4320650240 | bytes 116062880 | solution.py:127
  78.4 7.2 %multiply_reduce_fusion.2 = (f32[2048]{0:T(1024)S(1)}, f32[2048,1024]{0,1:T(8,128)}) fusion(bf16[2048,512]{1,0:T(8,128)(2,1)S(1)} %get-tuple-element.170, f32[1024,512]{1,0:T(8,128)} %get-tuple-element.148), kind=kOutput, calls=%fused_computation.4.clone.1 | convolution fusion | flops 2152200192 | bytes 12591104 | tf_op jit(solution)/shard_map/while/body/eval_jaxpr/dot_general | solution.py:106
  85.5 6.9 %pmax.11 = f32[2048]{0:T(1024)S(1)} all-reduce(f32[2048]{0:T(1024)S(1)} %get-tuple-element.125), channel_id=1, replica_groups=mesh['z'=8,'y'=4,'xh'=2,'xl'=2,'core'=2] {'xl','core'}, use_global_device_ids=true, to_apply=%region_2.2 | all-reduce | flops 2048 | bytes 16384 | tf_op jit(solution)/shard_map/while/body/eval_jaxpr/pmax | solution.py:112
  92.5 4.8 %exponential_reduce_fusion.2 = f32[2048]{0:T(1024)S(1)} fusion(f32[2048,1024]{0,1:T(8,128)} %get-tuple-element.124, f32[2048]{0:T(1024)S(1)} %pmax.11), kind=kLoop, calls=%fused_computation.1.clone.1 | loop fusion | flops 6289408 | bytes 8404992 | tf_op jit(solution)/shard_map/while/body/eval_jaxpr/reduce_sum | solution.py:113
  97.3 6.1 %psum.11 = f32[2048]{0:T(1024)S(1)} all-reduce(f32[2048]{0:T(1024)S(1)} %exponential_reduce_fusion.2), channel_id=1, replica_groups=mesh['z'=8,'y'=4,'xh'=2,'xl'=2,'core'=2] {'xl','core'}, use_global_device_ids=true, to_apply=%region_4.4 | all-reduce | flops 2048 | bytes 16384 | tf_op jit(solution)/shard_map/while/body/eval_jaxpr/psum | solution.py:113
  103.4 5.9 %fusion.28 = f32[1024,512]{1,0:T(8,128)S(1)} fusion(bf16[2048,512]{1,0:T(8,128)(2,1)S(1)} %get-tuple-element.170, f32[2048,1024]{0,1:T(8,128)} %get-tuple-element.124, f32[2048]{0:T(1024)S(1)} %log_add_fusion.2), kind=kOutput, calls=%fused_computation.5.clone.1 | convolution fusion | flops 2153775104 | bytes 12591104 | tf_op jit(solution)/shard_map/while/body/eval_jaxpr/dot_general | solution.py:117
  112.4 44.9 %reduce-scatter.2.cloned.1.call-done = f32[136,512]{1,0:T(8,128)} async-done(((f32[1088,512]{1,0:T(8,128)}), f32[136,512]{1,0:T(8,128)}) %reduce-scatter.2.cloned.1.call-update) | async-done | bytes 278544 | tf_op jit(solution)/shard_map/while/body/eval_jaxpr/reduce_scatter | solution.py:33
  161.8 3.0 collective-permute-start.4
  165.3 3.1 collective-permute-start.1
  173.7 3.0 collective-permute-done.2
  180.2 3.5 collective-permute-done.6
  184.6 3.0 collective-permute-start.7
  187.7 2.8 collective-permute-done.7
  191.5 4.1 collective-permute-done.8
  197.9 8.8 %collective-permute-done.9 = f32[128,512]{1,0:T(8,128)S(1)} collective-permute-done((f32[128,512]{1,0:T(8,128)S(1)}, f32[128,512]{1,0:T(8,128)S(1)}, u32[]{:S(2)}, u32[]{:S(2)}) %collective-permute-start.9) | collective-permute-done | bytes 262176 | tf_op jit(solution)/shard_map/while/body/eval_jaxpr/ppermute | solution.py:61
  206.7 3.2 collective-permute-start.13
  209.9 6.8 %collective-permute-done.10 = f32[128,512]{1,0:T(8,128)S(1)} collective-permute-done((f32[128,512]{1,0:T(8,128)S(1)}, f32[128,512]{1,0:T(8,128)S(1)}, u32[]{:S(2)}, u32[]{:S(2)}) %collective-permute-start.10) | collective-permute-done | bytes 262176 | tf_op jit(solution)/shard_map/while/body/eval_jaxpr/ppermute | solution.py:61
  216.7 3.2 collective-permute-start.14
  219.9 4.4 %collective-permute-done.11 = f32[128,512]{1,0:T(8,128)} collective-permute-done((f32[128,512]{1,0:T(8,128)S(1)}, f32[128,512]{1,0:T(8,128)}, u32[]{:S(2)}, u32[]{:S(2)}) %collective-permute-start.11) | collective-permute-done | bytes 262176 | tf_op jit(solution)/shard_map/while/body/eval_jaxpr/ppermute | solution.py:61
  224.4 3.4 collective-permute-start.15
  227.8 4.4 %collective-permute-done.12 = f32[128,512]{1,0:T(8,128)} collective-permute-done((f32[128,512]{1,0:T(8,128)}, f32[128,512]{1,0:T(8,128)}, u32[]{:S(2)}, u32[]{:S(2)}) %collective-permute-start.12) | collective-permute-done | bytes 262176 | tf_op jit(solution)/shard_map/while/body/eval_jaxpr/ppermute | solution.py:61
  243.7 7.2 %multiply_reduce_fusion.2 = (f32[2048]{0:T(1024)S(1)}, f32[2048,1024]{0,1:T(8,128)}) fusion(bf16[2048,512]{1,0:T(8,128)(2,1)S(1)} %get-tuple-element.170, f32[1024,512]{1,0:T(8,128)} %get-tuple-element.148), kind=kOutput, calls=%fused_computation.4.clone.1 | convolution fusion | flops 2152200192 | bytes 12591104 | tf_op jit(solution)/shard_map/while/body/eval_jaxpr/dot_general | solution.py:106
  250.9 5.9 %pmax.11 = f32[2048]{0:T(1024)S(1)} all-reduce(f32[2048]{0:T(1024)S(1)} %get-tuple-element.125), channel_id=1, replica_groups=mesh['z'=8,'y'=4,'xh'=2,'xl'=2,'core'=2] {'xl','core'}, use_global_device_ids=true, to_apply=%region_2.2 | all-reduce | flops 2048 | bytes 16384 | tf_op jit(solution)/shard_map/while/body/eval_jaxpr/pmax | solution.py:112
  256.7 4.8 %exponential_reduce_fusion.2 = f32[2048]{0:T(1024)S(1)} fusion(f32[2048,1024]{0,1:T(8,128)} %get-tuple-element.124, f32[2048]{0:T(1024)S(1)} %pmax.11), kind=kLoop, calls=%fused_computation.1.clone.1 | loop fusion | flops 6289408 | bytes 8404992 | tf_op jit(solution)/shard_map/while/body/eval_jaxpr/reduce_sum | solution.py:113
  261.5 5.9 %psum.11 = f32[2048]{0:T(1024)S(1)} all-reduce(f32[2048]{0:T(1024)S(1)} %exponential_reduce_fusion.2), channel_id=1, replica_groups=mesh['z'=8,'y'=4,'xh'=2,'xl'=2,'core'=2] {'xl','core'}, use_global_device_ids=true, to_apply=%region_4.4 | all-reduce | flops 2048 | bytes 16384 | tf_op jit(solution)/shard_map/while/body/eval_jaxpr/psum | solution.py:113
  267.4 5.9 %fusion.28 = f32[1024,512]{1,0:T(8,128)S(1)} fusion(bf16[2048,512]{1,0:T(8,128)(2,1)S(1)} %get-tuple-element.170, f32[2048,1024]{0,1:T(8,128)} %get-tuple-element.124, f32[2048]{0:T(1024)S(1)} %log_add_fusion.2), kind=kOutput, calls=%fused_computation.5.clone.1 | convolution fusion | flops 2153775104 | bytes 12591104 | tf_op jit(solution)/shard_map/while/body/eval_jaxpr/dot_general | solution.py:117
  276.4 42.1 %reduce-scatter.2.cloned.1.call-done = f32[136,512]{1,0:T(8,128)} async-done(((f32[1088,512]{1,0:T(8,128)}), f32[136,512]{1,0:T(8,128)}) %reduce-scatter.2.cloned.1.call-update) | async-done | bytes 278544 | tf_op jit(solution)/shard_map/while/body/eval_jaxpr/reduce_scatter | solution.py:33
  323.0 2.8 collective-permute-start.4
  326.4 3.1 collective-permute-start.1
  334.8 3.0 collective-permute-done.2
  341.5 3.4 collective-permute-done.6
  345.7 3.1 collective-permute-start.7
  348.8 2.8 collective-permute-done.7
  353.2 3.5 collective-permute-done.8
  359.0 8.7 %collective-permute-done.9 = f32[128,512]{1,0:T(8,128)S(1)} collective-permute-done((f32[128,512]{1,0:T(8,128)S(1)}, f32[128,512]{1,0:T(8,128)S(1)}, u32[]{:S(2)}, u32[]{:S(2)}) %collective-permute-start.9) | collective-permute-done | bytes 262176 | tf_op jit(solution)/shard_map/while/body/eval_jaxpr/ppermute | solution.py:61
  367.7 3.2 collective-permute-start.13
  370.9 6.8 %collective-permute-done.10 = f32[128,512]{1,0:T(8,128)S(1)} collective-permute-done((f32[128,512]{1,0:T(8,128)S(1)}, f32[128,512]{1,0:T(8,128)S(1)}, u32[]{:S(2)}, u32[]{:S(2)}) %collective-permute-start.10) | collective-permute-done | bytes 262176 | tf_op jit(solution)/shard_map/while/body/eval_jaxpr/ppermute | solution.py:61
  377.8 3.2 collective-permute-start.14
  381.0 4.4 %collective-permute-done.11 = f32[128,512]{1,0:T(8,128)} collective-permute-done((f32[128,512]{1,0:T(8,128)S(1)}, f32[128,512]{1,0:T(8,128)}, u32[]{:S(2)}, u32[]{:S(2)}) %collective-permute-start.11) | collective-permute-done | bytes 262176 | tf_op jit(solution)/shard_map/while/body/eval_jaxpr/ppermute | solution.py:61
  385.4 3.4 collective-permute-start.15
  388.9 4.4 %collective-permute-done.12 = f32[128,512]{1,0:T(8,128)} collective-permute-done((f32[128,512]{1,0:T(8,128)}, f32[128,512]{1,0:T(8,128)}, u32[]{:S(2)}, u32[]{:S(2)}) %collective-permute-start.12) | collective-permute-done | bytes 262176 | tf_op jit(solution)/shard_map/while/body/eval_jaxpr/ppermute | solution.py:61
  (157 shorter events, 82.9 us)
Async XLA Ops:
  8.9 63.4 %copy-start.2 = (f32[1024,512]{1,0:T(8,128)}, f32[1024,512]{1,0:T(8,128)S(1)}, u32[]{:S(2)}) copy-start(f32[1024,512]{1,0:T(8,128)S(1)} %copy.33) | copy-start | bytes 6291460
  17.6 4.5 %collective-permute-start.16 = (f32[1024,512]{1,0:T(8,128)}, f32[1024,512]{1,0:T(8,128)}, u32[]{:S(2)}, u32[]{:S(2)}) collective-permute-start(f32[1024,512]{1,0:T(8,128)} %constant_dynamic-slice_fusion.7), channel_id=1, source_target_pairs={{0,1},{1,0},{2,3},{3,2},{4,5},{5,4},{6,7},{7,6},{8,9},{9,8},{10,11... | collective-permute-start | bytes 6291464 | tf_op jit(solution)/shard_map/ppermute | solution.py:85
  27.3 26.0 %collective-permute-start.17 = (f32[512,512]{1,0:T(8,128)}, f32[512,512]{1,0:T(8,128)}, u32[]{:S(2)}, u32[]{:S(2)}) collective-permute-start(f32[512,512]{1,0:T(8,128)} %constant_dynamic-slice_fusion.6), channel_id=1, source_target_pairs={{0,2},{2,0},{1,3},{3,1},{4,6},{6,4},{5,7},{7,5},{8,10},{10,8},{9,1... | collective-permute-start | bytes 3145736 | tf_op jit(solution)/shard_map/ppermute | solution.py:85
  55.8 13.7 %collective-permute-start.18 = (bf16[512,512]{1,0:T(8,128)(2,1)}, bf16[512,512]{1,0:T(8,128)(2,1)}, u32[]{:S(2)}, u32[]{:S(2)}) collective-permute-start(bf16[512,512]{1,0:T(8,128)(2,1)} %add_convert_fusion), channel_id=1, source_target_pairs={{0,2},{2,0},{1,3},{3,1},{4,6},{6,4},{5,7},{7,5},{8,10},{10,8},{9,1... | collective-permute-start | bytes 1572872 | tf_op jit(solution)/shard_map/ppermute | solution.py:88
  72.3 3.0 collective-permute-start.19
  78.3 79.0 %reduce-scatter.2.cloned.1.call-start = ((), (), s32[]{:S(2)}) async-start(), calls=%async_computation.1 | async-start | bytes 2506752 | tf_op jit(solution)/shard_map/while/body/eval_jaxpr/reduce_scatter | solution.py:33
  103.4 5.9 %copy-start.9 = (f32[2048]{0:T(1024)}, f32[2048]{0:T(1024)S(1)}, u32[]{:S(2)}) copy-start(f32[2048]{0:T(1024)S(1)} %log_add_fusion.2) | copy-start | bytes 24580 | tf_op jit(solution)/shard_map/while
  103.4 5.9 %copy-start.1 = (f32[2048,1024]{0,1:T(8,128)S(1)}, f32[2048,1024]{0,1:T(8,128)}, u32[]{:S(2)}) copy-start(f32[2048,1024]{0,1:T(8,128)} %get-tuple-element.124) | copy-start | bytes 25165828 | tf_op jit(solution)/shard_map/while
  158.1 3.6 collective-permute-start.3
  160.2 5.1 %collective-permute-start = (f32[64,512]{1,0:T(8,128)S(1)}, f32[64,512]{1,0:T(8,128)S(1)}, u32[]{:S(2)}, u32[]{:S(2)}) collective-permute-start(f32[64,512]{1,0:T(8,128)S(1)} %constant_dynamic-slice_fusion.13), channel_id=1, source_target_pairs={{0,8},{8,0},{16,24},{24,16},{1,9},{9,1},{17,25},{25,17},{2,10},{10... | collective-permute-start | bytes 393224 | tf_op jit(solution)/shard_map/while/body/eval_jaxpr/ppermute | solution.py:18
  161.8 6.6 %collective-permute-start.4 = (f32[32]{0:T(128)S(1)}, f32[32]{0:T(128)S(1)}, u32[]{:S(2)}, u32[]{:S(2)}) collective-permute-start(f32[32]{0:T(128)S(1)} %dynamic_slice.142), channel_id=1, source_target_pairs={{0,16},{8,24},{16,0},{24,8},{1,17},{9,25},{17,1},{25,9},{2,18},{10... | collective-permute-start | bytes 392 | tf_op jit(solution)/shard_map/while/body/eval_jaxpr/ppermute | solution.py:18
  165.3 5.9 %collective-permute-start.1 = (f32[32,512]{1,0:T(8,128)S(1)}, f32[32,512]{1,0:T(8,128)S(1)}, u32[]{:S(2)}, u32[]{:S(2)}) collective-permute-start(f32[32,512]{1,0:T(8,128)S(1)} %constant_dynamic-slice_fusion.14), channel_id=1, source_target_pairs={{0,16},{8,24},{16,0},{24,8},{1,17},{9,25},{17,1},{25,9},{2,18},{10... | collective-permute-start | bytes 196616 | tf_op jit(solution)/shard_map/while/body/eval_jaxpr/ppermute | solution.py:18
  168.5 5.1 %collective-permute-start.5 = (f32[16]{0:T(128)S(1)}, f32[16]{0:T(128)S(1)}, u32[]{:S(2)}, u32[]{:S(2)}) collective-permute-start(f32[16]{0:T(128)S(1)} %dynamic_slice.143), channel_id=1, source_target_pairs={{0,4},{4,0},{1,5},{5,1},{2,6},{6,2},{3,7},{7,3},{8,12},{12,8},{9,1... | collective-permute-start | bytes 200 | tf_op jit(solution)/shard_map/while/body/eval_jaxpr/ppermute | solution.py:18
  171.2 5.5 %collective-permute-start.2 = (f32[16,512]{1,0:T(8,128)S(1)}, f32[16,512]{1,0:T(8,128)S(1)}, u32[]{:S(2)}, u32[]{:S(2)}) collective-permute-start(f32[16,512]{1,0:T(8,128)S(1)} %constant_dynamic-slice_fusion.15), channel_id=1, source_target_pairs={{0,4},{4,0},{1,5},{5,1},{2,6},{6,2},{3,7},{7,3},{8,12},{12,8},{9,1... | collective-permute-start | bytes 98312 | tf_op jit(solution)/shard_map/while/body/eval_jaxpr/ppermute | solution.py:18
  178.1 5.6 %collective-permute-start.6 = (f32[16,512]{1,0:T(8,128)}, f32[16,512]{1,0:T(8,128)S(1)}, u32[]{:S(2)}, u32[]{:S(2)}) collective-permute-start(f32[16,512]{1,0:T(8,128)} %add_divide_fusion.2), channel_id=1, source_target_pairs={{0,4},{4,0},{1,5},{5,1},{2,6},{6,2},{3,7},{7,3},{8,12},{12,8},{9,1... | collective-permute-start | bytes 98312 | tf_op jit(solution)/shard_map/while/body/eval_jaxpr/ppermute | solution.py:18
  184.6 5.8 %collective-permute-start.7 = (f32[32,512]{1,0:T(8,128)S(1)}, f32[32,512]{1,0:T(8,128)S(1)}, u32[]{:S(2)}, u32[]{:S(2)}) collective-permute-start(f32[32,512]{1,0:T(8,128)S(1)} %maximum_select_fusion.8), channel_id=1, source_target_pairs={{0,16},{8,24},{16,0},{24,8},{1,17},{9,25},{17,1},{25,9},{2,18},{10... | collective-permute-start | bytes 196616 | tf_op jit(solution)/shard_map/while/body/eval_jaxpr/ppermute | solution.py:18
  190.5 5.2 %collective-permute-start.8 = (f32[64,512]{1,0:T(8,128)S(1)}, f32[64,512]{1,0:T(8,128)}, u32[]{:S(2)}, u32[]{:S(2)}) collective-permute-start(f32[64,512]{1,0:T(8,128)S(1)} %maximum_select_fusion.9), channel_id=1, source_target_pairs={{0,8},{8,0},{16,24},{24,16},{1,9},{9,1},{17,25},{25,17},{2,10},{10... | collective-permute-start | bytes 393224 | tf_op jit(solution)/shard_map/while/body/eval_jaxpr/ppermute | solution.py:18
  196.6 10.0 %collective-permute-start.9 = (f32[128,512]{1,0:T(8,128)S(1)}, f32[128,512]{1,0:T(8,128)S(1)}, u32[]{:S(2)}, u32[]{:S(2)}) collective-permute-start(f32[128,512]{1,0:T(8,128)S(1)} %maximum_select_fusion.10), channel_id=1, source_target_pairs={{0,32},{32,64},{64,96},{96,128},{128,160},{160,192},{192,224},{224... | collective-permute-start | bytes 786440 | tf_op jit(solution)/shard_map/while/body/eval_jaxpr/ppermute | solution.py:61
  206.7 10.0 %copy-start.3 = (f32[128,512]{1,0:T(8,128)}, f32[128,512]{1,0:T(8,128)S(1)}, u32[]{:S(2)}) copy-start(f32[128,512]{1,0:T(8,128)S(1)} %collective-permute-done.9) | copy-start | bytes 786436 | tf_op jit(solution)/shard_map/while
  206.7 10.0 %collective-permute-start.10 = (f32[128,512]{1,0:T(8,128)S(1)}, f32[128,512]{1,0:T(8,128)S(1)}, u32[]{:S(2)}, u32[]{:S(2)}) collective-permute-start(f32[128,512]{1,0:T(8,128)S(1)} %collective-permute-done.9), channel_id=1, source_target_pairs={{0,32},{32,64},{64,96},{96,128},{128,160},{160,192},{192,224},{224... | collective-permute-start | bytes 786440 | tf_op jit(solution)/shard_map/while/body/eval_jaxpr/ppermute | solution.py:61
  206.7 10.0 %collective-permute-start.13 = (f32[128,512]{1,0:T(8,128)S(1)}, f32[128,512]{1,0:T(8,128)}, u32[]{:S(2)}, u32[]{:S(2)}) collective-permute-start(f32[128,512]{1,0:T(8,128)S(1)} %maximum_select_fusion.10), channel_id=1, source_target_pairs={{0,224},{32,0},{64,32},{96,64},{128,96},{160,128},{192,160},{224,1... | collective-permute-start | bytes 786440 | tf_op jit(solution)/shard_map/while/body/eval_jaxpr/ppermute | solution.py:64
  216.7 7.7 %collective-permute-start.11 = (f32[128,512]{1,0:T(8,128)S(1)}, f32[128,512]{1,0:T(8,128)}, u32[]{:S(2)}, u32[]{:S(2)}) collective-permute-start(f32[128,512]{1,0:T(8,128)S(1)} %collective-permute-done.10), channel_id=1, source_target_pairs={{0,32},{32,64},{64,96},{96,128},{128,160},{160,192},{192,224},{224... | collective-permute-start | bytes 786440 | tf_op jit(solution)/shard_map/while/body/eval_jaxpr/ppermute | solution.py:61
  216.7 7.7 %collective-permute-start.14 = (f32[128,512]{1,0:T(8,128)}, f32[128,512]{1,0:T(8,128)}, u32[]{:S(2)}, u32[]{:S(2)}) collective-permute-start(f32[128,512]{1,0:T(8,128)} %collective-permute-done.13), channel_id=1, source_target_pairs={{0,224},{32,0},{64,32},{96,64},{128,96},{160,128},{192,160},{224,1... | collective-permute-start | bytes 786440 | tf_op jit(solution)/shard_map/while/body/eval_jaxpr/ppermute | solution.py:64
  224.4 7.9 %collective-permute-start.12 = (f32[128,512]{1,0:T(8,128)}, f32[128,512]{1,0:T(8,128)}, u32[]{:S(2)}, u32[]{:S(2)}) collective-permute-start(f32[128,512]{1,0:T(8,128)} %collective-permute-done.11), channel_id=1, source_target_pairs={{0,32},{32,64},{64,96},{96,128},{128,160},{160,192},{192,224},{224... | collective-permute-start | bytes 786440 | tf_op jit(solution)/shard_map/while/body/eval_jaxpr/ppermute | solution.py:61
  224.4 15.7 %copy-start.6 = (f32[128,512]{1,0:T(8,128)S(1)}, f32[128,512]{1,0:T(8,128)}, u32[]{:S(2)}) copy-start(f32[128,512]{1,0:T(8,128)} %copy-done.5) | copy-start | bytes 786436 | tf_op jit(solution)/shard_map/while
  224.4 15.8 %copy-start.4 = (f32[128,512]{1,0:T(8,128)S(1)}, f32[128,512]{1,0:T(8,128)}, u32[]{:S(2)}) copy-start(f32[128,512]{1,0:T(8,128)} %copy-done.3) | copy-start | bytes 786436 | tf_op jit(solution)/shard_map/while
  224.4 13.8 %collective-permute-start.15 = (f32[128,512]{1,0:T(8,128)}, f32[128,512]{1,0:T(8,128)S(1)}, u32[]{:S(2)}, u32[]{:S(2)}) collective-permute-start(f32[128,512]{1,0:T(8,128)} %collective-permute-done.14), channel_id=1, source_target_pairs={{0,224},{32,0},{64,32},{96,64},{128,96},{160,128},{192,160},{224,1... | collective-permute-start | bytes 786440 | tf_op jit(solution)/shard_map/while/body/eval_jaxpr/ppermute | solution.py:64
  243.7 74.9 %reduce-scatter.2.cloned.1.call-start = ((), (), s32[]{:S(2)}) async-start(), calls=%async_computation.1 | async-start | bytes 2506752 | tf_op jit(solution)/shard_map/while/body/eval_jaxpr/reduce_scatter | solution.py:33
  267.4 5.9 %copy-start.9 = (f32[2048]{0:T(1024)}, f32[2048]{0:T(1024)S(1)}, u32[]{:S(2)}) copy-start(f32[2048]{0:T(1024)S(1)} %log_add_fusion.2) | copy-start | bytes 24580 | tf_op jit(solution)/shard_map/while
  319.3 3.6 collective-permute-start.3
  321.3 5.1 %collective-permute-start = (f32[64,512]{1,0:T(8,128)S(1)}, f32[64,512]{1,0:T(8,128)S(1)}, u32[]{:S(2)}, u32[]{:S(2)}) collective-permute-start(f32[64,512]{1,0:T(8,128)S(1)} %constant_dynamic-slice_fusion.13), channel_id=1, source_target_pairs={{0,8},{8,0},{16,24},{24,16},{1,9},{9,1},{17,25},{25,17},{2,10},{10... | collective-permute-start | bytes 393224 | tf_op jit(solution)/shard_map/while/body/eval_jaxpr/ppermute | solution.py:18
  323.0 6.5 %collective-permute-start.4 = (f32[32]{0:T(128)S(1)}, f32[32]{0:T(128)S(1)}, u32[]{:S(2)}, u32[]{:S(2)}) collective-permute-start(f32[32]{0:T(128)S(1)} %dynamic_slice.142), channel_id=1, source_target_pairs={{0,16},{8,24},{16,0},{24,8},{1,17},{9,25},{17,1},{25,9},{2,18},{10... | collective-permute-start | bytes 392 | tf_op jit(solution)/shard_map/while/body/eval_jaxpr/ppermute | solution.py:18
  326.4 5.9 %collective-permute-start.1 = (f32[32,512]{1,0:T(8,128)S(1)}, f32[32,512]{1,0:T(8,128)S(1)}, u32[]{:S(2)}, u32[]{:S(2)}) collective-permute-start(f32[32,512]{1,0:T(8,128)S(1)} %constant_dynamic-slice_fusion.14), channel_id=1, source_target_pairs={{0,16},{8,24},{16,0},{24,8},{1,17},{9,25},{17,1},{25,9},{2,18},{10... | collective-permute-start | bytes 196616 | tf_op jit(solution)/shard_map/while/body/eval_jaxpr/ppermute | solution.py:18
  329.6 5.1 %collective-permute-start.5 = (f32[16]{0:T(128)S(1)}, f32[16]{0:T(128)S(1)}, u32[]{:S(2)}, u32[]{:S(2)}) collective-permute-start(f32[16]{0:T(128)S(1)} %dynamic_slice.143), channel_id=1, source_target_pairs={{0,4},{4,0},{1,5},{5,1},{2,6},{6,2},{3,7},{7,3},{8,12},{12,8},{9,1... | collective-permute-start | bytes 200 | tf_op jit(solution)/shard_map/while/body/eval_jaxpr/ppermute | solution.py:18
  332.3 5.5 %collective-permute-start.2 = (f32[16,512]{1,0:T(8,128)S(1)}, f32[16,512]{1,0:T(8,128)S(1)}, u32[]{:S(2)}, u32[]{:S(2)}) collective-permute-start(f32[16,512]{1,0:T(8,128)S(1)} %constant_dynamic-slice_fusion.15), channel_id=1, source_target_pairs={{0,4},{4,0},{1,5},{5,1},{2,6},{6,2},{3,7},{7,3},{8,12},{12,8},{9,1... | collective-permute-start | bytes 98312 | tf_op jit(solution)/shard_map/while/body/eval_jaxpr/ppermute | solution.py:18
  339.2 5.6 %collective-permute-start.6 = (f32[16,512]{1,0:T(8,128)}, f32[16,512]{1,0:T(8,128)S(1)}, u32[]{:S(2)}, u32[]{:S(2)}) collective-permute-start(f32[16,512]{1,0:T(8,128)} %add_divide_fusion.2), channel_id=1, source_target_pairs={{0,4},{4,0},{1,5},{5,1},{2,6},{6,2},{3,7},{7,3},{8,12},{12,8},{9,1... | collective-permute-start | bytes 98312 | tf_op jit(solution)/shard_map/while/body/eval_jaxpr/ppermute | solution.py:18
  345.7 5.8 %collective-permute-start.7 = (f32[32,512]{1,0:T(8,128)S(1)}, f32[32,512]{1,0:T(8,128)S(1)}, u32[]{:S(2)}, u32[]{:S(2)}) collective-permute-start(f32[32,512]{1,0:T(8,128)S(1)} %maximum_select_fusion.8), channel_id=1, source_target_pairs={{0,16},{8,24},{16,0},{24,8},{1,17},{9,25},{17,1},{25,9},{2,18},{10... | collective-permute-start | bytes 196616 | tf_op jit(solution)/shard_map/while/body/eval_jaxpr/ppermute | solution.py:18
  351.5 5.2 %collective-permute-start.8 = (f32[64,512]{1,0:T(8,128)S(1)}, f32[64,512]{1,0:T(8,128)}, u32[]{:S(2)}, u32[]{:S(2)}) collective-permute-start(f32[64,512]{1,0:T(8,128)S(1)} %maximum_select_fusion.9), channel_id=1, source_target_pairs={{0,8},{8,0},{16,24},{24,16},{1,9},{9,1},{17,25},{25,17},{2,10},{10... | collective-permute-start | bytes 393224 | tf_op jit(solution)/shard_map/while/body/eval_jaxpr/ppermute | solution.py:18
  357.7 10.0 %collective-permute-start.9 = (f32[128,512]{1,0:T(8,128)S(1)}, f32[128,512]{1,0:T(8,128)S(1)}, u32[]{:S(2)}, u32[]{:S(2)}) collective-permute-start(f32[128,512]{1,0:T(8,128)S(1)} %maximum_select_fusion.10), channel_id=1, source_target_pairs={{0,32},{32,64},{64,96},{96,128},{128,160},{160,192},{192,224},{224... | collective-permute-start | bytes 786440 | tf_op jit(solution)/shard_map/while/body/eval_jaxpr/ppermute | solution.py:61
  367.7 10.0 %copy-start.3 = (f32[128,512]{1,0:T(8,128)}, f32[128,512]{1,0:T(8,128)S(1)}, u32[]{:S(2)}) copy-start(f32[128,512]{1,0:T(8,128)S(1)} %collective-permute-done.9) | copy-start | bytes 786436 | tf_op jit(solution)/shard_map/while
  367.7 10.0 %collective-permute-start.10 = (f32[128,512]{1,0:T(8,128)S(1)}, f32[128,512]{1,0:T(8,128)S(1)}, u32[]{:S(2)}, u32[]{:S(2)}) collective-permute-start(f32[128,512]{1,0:T(8,128)S(1)} %collective-permute-done.9), channel_id=1, source_target_pairs={{0,32},{32,64},{64,96},{96,128},{128,160},{160,192},{192,224},{224... | collective-permute-start | bytes 786440 | tf_op jit(solution)/shard_map/while/body/eval_jaxpr/ppermute | solution.py:61
  367.7 10.0 %collective-permute-start.13 = (f32[128,512]{1,0:T(8,128)S(1)}, f32[128,512]{1,0:T(8,128)}, u32[]{:S(2)}, u32[]{:S(2)}) collective-permute-start(f32[128,512]{1,0:T(8,128)S(1)} %maximum_select_fusion.10), channel_id=1, source_target_pairs={{0,224},{32,0},{64,32},{96,64},{128,96},{160,128},{192,160},{224,1... | collective-permute-start | bytes 786440 | tf_op jit(solution)/shard_map/while/body/eval_jaxpr/ppermute | solution.py:64
  377.7 7.7 %collective-permute-start.11 = (f32[128,512]{1,0:T(8,128)S(1)}, f32[128,512]{1,0:T(8,128)}, u32[]{:S(2)}, u32[]{:S(2)}) collective-permute-start(f32[128,512]{1,0:T(8,128)S(1)} %collective-permute-done.10), channel_id=1, source_target_pairs={{0,32},{32,64},{64,96},{96,128},{128,160},{160,192},{192,224},{224... | collective-permute-start | bytes 786440 | tf_op jit(solution)/shard_map/while/body/eval_jaxpr/ppermute | solution.py:61
  377.8 7.7 %collective-permute-start.14 = (f32[128,512]{1,0:T(8,128)}, f32[128,512]{1,0:T(8,128)}, u32[]{:S(2)}, u32[]{:S(2)}) collective-permute-start(f32[128,512]{1,0:T(8,128)} %collective-permute-done.13), channel_id=1, source_target_pairs={{0,224},{32,0},{64,32},{96,64},{128,96},{160,128},{192,160},{224,1... | collective-permute-start | bytes 786440 | tf_op jit(solution)/shard_map/while/body/eval_jaxpr/ppermute | solution.py:64
  385.4 7.9 %collective-permute-start.12 = (f32[128,512]{1,0:T(8,128)}, f32[128,512]{1,0:T(8,128)}, u32[]{:S(2)}, u32[]{:S(2)}) collective-permute-start(f32[128,512]{1,0:T(8,128)} %collective-permute-done.11), channel_id=1, source_target_pairs={{0,32},{32,64},{64,96},{96,128},{128,160},{160,192},{192,224},{224... | collective-permute-start | bytes 786440 | tf_op jit(solution)/shard_map/while/body/eval_jaxpr/ppermute | solution.py:61
  385.4 15.7 %copy-start.6 = (f32[128,512]{1,0:T(8,128)S(1)}, f32[128,512]{1,0:T(8,128)}, u32[]{:S(2)}) copy-start(f32[128,512]{1,0:T(8,128)} %copy-done.5) | copy-start | bytes 786436 | tf_op jit(solution)/shard_map/while
  385.4 15.8 %copy-start.4 = (f32[128,512]{1,0:T(8,128)S(1)}, f32[128,512]{1,0:T(8,128)}, u32[]{:S(2)}) copy-start(f32[128,512]{1,0:T(8,128)} %copy-done.3) | copy-start | bytes 786436 | tf_op jit(solution)/shard_map/while
  385.4 13.8 %collective-permute-start.15 = (f32[128,512]{1,0:T(8,128)}, f32[128,512]{1,0:T(8,128)S(1)}, u32[]{:S(2)}, u32[]{:S(2)}) collective-permute-start(f32[128,512]{1,0:T(8,128)} %collective-permute-done.14), channel_id=1, source_target_pairs={{0,224},{32,0},{64,32},{96,64},{128,96},{160,128},{192,160},{224,1... | collective-permute-start | bytes 786440 | tf_op jit(solution)/shard_map/while/body/eval_jaxpr/ppermute | solution.py:64
  (6 other events, 17.6 us)
Sparse Core Ops, SparseCore 0:
  112.5 44.7 reduce-scatter.1
  276.5 41.9 reduce-scatter.1

commit v6 on v4

--- a/solution.py
+++ b/solution.py
@@ -13,14 +13,16 @@
 CENT_AXES = ("xl", "core")
 
 
-def _swap(x, axis, bit):
-    size = {"y": 4, "xh": 2}[axis]
-    return lax.ppermute(x, axis, [(i, i ^ bit) for i in range(size)])
+GROUP = ("y", "xh")
+GROUP_SIZE = 8
 
 
-def _bits():
-    y = lax.axis_index("y")
-    return ((y & 1, "y", 1), ((y >> 1) & 1, "y", 2), (lax.axis_index("xh"), "xh", 1))
+def _shift(x, s):
+    return lax.ppermute(x, GROUP, [(i, (i + s) % GROUP_SIZE) for i in range(GROUP_SIZE)])
+
+
+def _group_index():
+    return lax.axis_index("y") * 2 + lax.axis_index("xh")
 
 
 def _reduce_rows(numer, mass):
@@ -32,28 +34,29 @@
     payload = payload.reshape(blocks * (per + 8), width)
     payload = lax.psum_scatter(payload, "z", scatter_dimension=0, tiled=True)
     numer, mass = payload[:per], payload[per, :per]
-    for bit, axis, mask in _bits():
-        half = numer.shape[0] // 2
-        keep = lax.dynamic_slice_in_dim(numer, bit * half, half, axis=0)
-        send = lax.dynamic_slice_in_dim(numer, (1 - bit) * half, half, axis=0)
-        keep_mass = lax.dynamic_slice_in_dim(mass, bit * half, half, axis=0)
-        send_mass = lax.dynamic_slice_in_dim(mass, (1 - bit) * half, half, axis=0)
-        numer = keep + _swap(send, axis, mask)
-        mass = keep_mass + _swap(send_mass, axis, mask)
-    return numer, mass
+    chunk = per // GROUP_SIZE
+    mass_row = jnp.zeros((GROUP_SIZE, 1, width), jnp.float32).at[:, 0, :chunk].set(mass.reshape(GROUP_SIZE, chunk))
+    chunks = jnp.concatenate([numer.reshape(GROUP_SIZE, chunk, width), mass_row], axis=1)
+    g = _group_index()
+    total = lax.dynamic_index_in_dim(chunks, g, axis=0, keepdims=False)
+    for s in range(1, GROUP_SIZE):
+        total = total + _shift(lax.dynamic_index_in_dim(chunks, (g + s) % GROUP_SIZE, axis=0, keepdims=False), s)
+    return total[:chunk], total[chunk, :chunk]
 
 
 def _gather_rows(block):
-    for bit, axis, mask in reversed(_bits()):
-        other = _swap(block, axis, mask)
-        block = jnp.where(bit == 0, jnp.concatenate([block, other]), jnp.concatenate([other, block]))
-    return lax.all_gather(block, "z", axis=0, tiled=True)
+    g = _group_index()
+    got = [block] + [_shift(block, s) for s in range(1, GROUP_SIZE)]
+    stacked = jnp.concatenate(list(reversed(got)), axis=0)
+    doubled = jnp.concatenate([stacked, stacked], axis=0)
+    rows = block.shape[0]
+    start = (GROUP_SIZE - 1 - g) % GROUP_SIZE
+    group_block = lax.dynamic_slice_in_dim(doubled, start * rows, GROUP_SIZE * rows, axis=0)
+    return lax.all_gather(group_block, "z", axis=0, tiled=True)
 
 
 def _row_offset(count):
-    y = lax.axis_index("y")
-    per = count // 64
-    return lax.axis_index("z") * (count // 8) + (y & 1) * (4 * per) + ((y >> 1) & 1) * (2 * per) + lax.axis_index("xh") * per
+    return lax.axis_index("z") * (count // 8) + _group_index() * (count // 64)
 
 
 def _project(embeddings, basis):

time: 386 us -> 411 us (1.065); the launches traced: 385 us -> 404 us
  starting transfers between devices: 42.1 us -> 59.9 us
    ppermute x18 -> x28, starting transfers between devices: 37.8 us -> 55.6 us  [_shift(): lax.ppermute(x, GROUP, [(i, (i + s) % GROUP_SIZE) for i in range(GROUP_SI...]
    ppermute x18 -> x28, waiting for transfers between devices: 28.9 us -> 23.9 us  [_shift(): lax.ppermute(x, GROUP, [(i, (i + s) % GROUP_SIZE) for i in range(GROUP_SI...]
  transfers between devices with their start and end apart: 26 -> 36, of which waited for: 24 -> 16; matrix products, arithmetic and copies ran while one was open for 1% -> 0% of each run, Pallas kernels for 0% -> 0%
where the time goes in v6:
time: 411 us; the launch traced here: 404 us
  waiting for transfers between devices  232 us (56%)
  starting transfers between devices  59.9 us (15%)
  other arithmetic  31 us (8%)
  matrix products  26.3 us (6%)
  blocking collectives  25.1 us (6%)
  between operations  14.8 us (4%)
  local copies, waits for them, and re-layouts  14.1 us (3%)
    reduce_scatter x2, waiting for transfers between devices, _reduce_rows(): payload = lax.psum_scatter(payload, 'z', scatter_dimension=0, tiled=True)  86.8 us
    all_gather x2, waiting for transfers between devices, _gather_rows(): return lax.all_gather(group_block, 'z', axis=0, tiled=True)  78.9 us
    ppermute x28, starting transfers between devices, _shift(): lax.ppermute(x, GROUP, [(i, (i + s) % GROUP_SIZE) for i in range(GROUP_SI...  55.6 us
    ppermute x2, waiting for transfers between devices, _project(): partial = keep + lax.ppermute(send, axis, [(0, 1), (1, 0)])  28 us
    ppermute x28, waiting for transfers between devices, _shift(): lax.ppermute(x, GROUP, [(i, (i + s) % GROUP_SIZE) for i in range(GROUP_SI...  23.9 us
    dot_general x2, matrix products, on_device(): lax.dot_general(projected, cent_bf, (((1,), (1,)), ((), ())), preferred_e...  15.4 us
    ppermute x2, waiting for transfers between devices, _project(): other = lax.ppermute(block, axis, [(0, 1), (1, 0)])  14.5 us
    pmax x2, blocking collectives, on_device(): top = lax.pmax(local_top, CENT_AXES)  13 us
  transfers between devices with their start and end apart: 36, of which 16 were waited for; matrix products, arithmetic and copies ran while one was open for 0% of the time, Pallas kernels for 0%

profile of v6, /device:TPU:2, one launch (start us, length us, event | category | flops | bytes accessed | tf_op | source)
XLA Modules:
  0.0 403.5 jit_solution(12396940160289426540)
XLA Ops:
  8.4 4.5 %fusion.34 = f32[2048,512]{1,0:T(8,128)S(1)} fusion(bf16[2048,1024]{1,0:T(8,128)(2,1)} %param.11, bf16[1024,512]{1,0:T(8,128)(2,1)S(1)} %copy-done), kind=kOutput, calls=%fused_computation.108 | convolution fusion | flops 2147483648 | bytes 9437184 | tf_op jit(solution)/shard_map/dot_general | solution.py:63
  12.9 1.9 copy-done.3
  15.2 4.3 %collective-permute-done = f32[1024,512]{1,0:T(8,128)} collective-permute-done((f32[1024,512]{1,0:T(8,128)S(1)}, f32[1024,512]{1,0:T(8,128)}, u32[]{:S(2)}, u32[]{:S(2)}) %collective-permute-start) | collective-permute-done | bytes 2097184 | tf_op jit(solution)/shard_map/ppermute | solution.py:69
  19.4 2.7 dynamic-slice_add_fusion
  23.2 2.2 collective-permute-start.1
  25.4 23.8 %collective-permute-done.1 = f32[512,512]{1,0:T(8,128)} collective-permute-done((f32[512,512]{1,0:T(8,128)}, f32[512,512]{1,0:T(8,128)}, u32[]{:S(2)}, u32[]{:S(2)}) %collective-permute-start.1) | collective-permute-done | bytes 1048608 | tf_op jit(solution)/shard_map/ppermute | solution.py:69
  49.2 2.2 add_convert_fusion
  53.1 11.9 %collective-permute-done.2 = bf16[512,512]{1,0:T(8,128)(2,1)S(1)} collective-permute-done((bf16[512,512]{1,0:T(8,128)(2,1)}, bf16[512,512]{1,0:T(8,128)(2,1)S(1)}, u32[]{:S(2)}, u32[]{:S(2)}) %collective-permute-start.2) | collective-permute-done | bytes 524320 | tf_op jit(solution)/shard_map/ppermute | solution.py:72
  66.8 2.6 collective-permute-done.3
  69.4 7.9 %multiply_reduce_fusion.1 = (f32[2048]{0:T(1024)S(1)}, f32[2048,1024]{0,1:T(8,128)}) fusion(f32[1024,512]{1,0:T(8,128)} %param.13, bf16[1024,512]{1,0:T(8,128)(2,1)S(1)} %collective-permute-done.3, bf16[1024,512]{1,0:T(8,128)(2,1)S(1)} %maximum_select_fusion.1, pred[]{:T(512)S(6)} %eq.23), kind=kOutput, calls=%fused_computation.9 | convolution fusion | flops 2161637376 | bytes 12591105 | tf_op jit(solution)/shard_map/dot_general | solution.py:88
  77.3 6.9 %pmax.14 = f32[2048]{0:T(1024)S(1)} all-reduce(f32[2048]{0:T(1024)S(1)} %get-tuple-element.64), channel_id=1, replica_groups=mesh['z'=8,'y'=4,'xh'=2,'xl'=2,'core'=2] {'xl','core'}, use_global_device_ids=true, to_apply=%region_1.2 | all-reduce | flops 2048 | bytes 16384 | tf_op jit(solution)/shard_map/pmax | solution.py:94
  84.3 4.8 %exponential_reduce_fusion.1 = f32[2048]{0:T(1024)S(1)} fusion(f32[2048,1024]{0,1:T(8,128)} %get-tuple-element.65, f32[2048]{0:T(1024)S(1)} %pmax.14), kind=kLoop, calls=%fused_computation.3 | loop fusion | flops 6289408 | bytes 8404992 | tf_op jit(solution)/shard_map/reduce_sum | solution.py:95
  89.0 6.2 %psum.14 = f32[2048]{0:T(1024)S(1)} all-reduce(f32[2048]{0:T(1024)S(1)} %exponential_reduce_fusion.1), channel_id=1, replica_groups=mesh['z'=8,'y'=4,'xh'=2,'xl'=2,'core'=2] {'xl','core'}, use_global_device_ids=true, to_apply=%region_3.4 | all-reduce | flops 2048 | bytes 16384 | tf_op jit(solution)/shard_map/psum | solution.py:95
  95.3 5.0 %fusion = f32[1024]{0:T(1024)S(1)} fusion(f32[2048,1024]{0,1:T(8,128)} %get-tuple-element.65, f32[2048]{0:T(1024)S(1)} %log_add_fusion.1), kind=kLoop, calls=%fused_computation.4 | loop fusion | flops 6290432 | bytes 8400896 | tf_op jit(solution)/shard_map/reduce_sum | solution.py:98
  101.1 2.4 fusion.6
  105.2 44.9 %reduce-scatter.3.cloned.1.call-done = f32[136,512]{1,0:T(8,128)} async-done(((f32[1088,512]{1,0:T(8,128)}), f32[136,512]{1,0:T(8,128)}) %reduce-scatter.3.cloned.1.call-update) | async-done | bytes 278544 | tf_op jit(solution)/shard_map/reduce_scatter | solution.py:35
  151.9 2.3 collective-permute-start.4
  154.2 3.5 collective-permute-start.10
  160.3 2.6 collective-permute-start.7
  163.4 2.2 collective-permute-start.5
  165.9 5.0 %collective-permute-done.6 = f32[17,512]{1,0:T(8,128)S(1)} collective-permute-done((f32[17,512]{1,0:T(8,128)S(1)}, f32[17,512]{1,0:T(8,128)S(1)}, u32[]{:S(2)}, u32[]{:S(2)}) %collective-permute-start.6) | collective-permute-done | bytes 34848 | tf_op jit(solution)/shard_map/ppermute | solution.py:21
  173.3 2.1 collective-permute-start.17
  175.4 3.0 collective-permute-start.15
  178.5 3.9 collective-permute-start.14
  183.3 2.8 collective-permute-done.12
  186.1 2.1 collective-permute-start.13
  188.2 4.1 %collective-permute-done.13 = bf16[16,512]{1,0:T(8,128)(2,1)S(1)} collective-permute-done((bf16[16,512]{1,0:T(8,128)(2,1)S(1)}, bf16[16,512]{1,0:T(8,128)(2,1)S(1)}, u32[]{:S(2)}, u32[]{:S(2)}) %collective-permute-start.13) | collective-permute-done | bytes 16416 | tf_op jit(solution)/shard_map/ppermute | solution.py:21
  193.2 38.3 %all-gather.3.cloned.1.call-done = bf16[1024,512]{1,0:T(8,128)(2,1)} async-done(((bf16[128,512]{1,0:T(8,128)(2,1)}), bf16[1024,512]{1,0:T(8,128)(2,1)}) %all-gather.3.cloned.1.call-update) | async-done | bytes 1048592 | tf_op jit(solution)/shard_map/all_gather | solution.py:55
  231.5 7.4 %multiply_reduce_fusion = (f32[2048]{0:T(1024)S(1)}, f32[2048,1024]{0,1:T(8,128)}) fusion(bf16[1024,512]{1,0:T(8,128)(2,1)} %all-gather.3.cloned.1.call-done, bf16[1024,512]{1,0:T(8,128)(2,1)} %copy-done.5, bf16[1024,512]{1,0:T(8,128)(2,1)S(1)} %maximum_select_fusion.1, pred[]{:T(512)S(6)} %eq.23), kind=kOutput, calls=%fused_computation.8 | convolution fusion | flops 2161113088 | bytes 11542529 | tf_op jit(solution)/shard_map/dot_general | solution.py:88
  238.9 6.0 %pmax.15 = f32[2048]{0:T(1024)S(1)} all-reduce(f32[2048]{0:T(1024)S(1)} %get-tuple-element.66), channel_id=1, replica_groups=mesh['z'=8,'y'=4,'xh'=2,'xl'=2,'core'=2] {'xl','core'}, use_global_device_ids=true, to_apply=%region_7.8 | all-reduce | flops 2048 | bytes 16384 | tf_op jit(solution)/shard_map/pmax | solution.py:94
  245.0 4.8 %exponential_reduce_fusion = f32[2048]{0:T(1024)S(1)} fusion(f32[2048,1024]{0,1:T(8,128)} %get-tuple-element.67, f32[2048]{0:T(1024)S(1)} %pmax.15), kind=kLoop, calls=%fused_computation.1 | loop fusion | flops 6289408 | bytes 8404992 | tf_op jit(solution)/shard_map/reduce_sum | solution.py:95
  249.7 5.9 %psum.15 = f32[2048]{0:T(1024)S(1)} all-reduce(f32[2048]{0:T(1024)S(1)} %exponential_reduce_fusion), channel_id=1, replica_groups=mesh['z'=8,'y'=4,'xh'=2,'xl'=2,'core'=2] {'xl','core'}, use_global_device_ids=true, to_apply=%region_9.10 | all-reduce | flops 2048 | bytes 16384 | tf_op jit(solution)/shard_map/psum | solution.py:95
  255.7 5.0 %fusion.2 = f32[1024]{0:T(1024)S(1)} fusion(f32[2048,1024]{0,1:T(8,128)} %get-tuple-element.67, f32[2048]{0:T(1024)S(1)} %log_add_fusion), kind=kLoop, calls=%fused_computation.6 | loop fusion | flops 6290432 | bytes 8400896 | tf_op jit(solution)/shard_map/reduce_sum | solution.py:98
  261.4 4.0 fusion.4
  267.0 42.0 %reduce-scatter.5.cloned.1.call-done = f32[136,512]{1,0:T(8,128)} async-done(((f32[1088,512]{1,0:T(8,128)}), f32[136,512]{1,0:T(8,128)}) %reduce-scatter.5.cloned.1.call-update) | async-done | bytes 278544 | tf_op jit(solution)/shard_map/reduce_scatter | solution.py:35
  310.9 2.5 collective-permute-start.18
  313.4 3.4 collective-permute-start.24
  316.8 1.9 collective-permute-start.23
  320.2 2.3 collective-permute-start.21
  323.1 2.2 collective-permute-start.19
  325.8 4.8 %collective-permute-done.20 = f32[17,512]{1,0:T(8,128)S(1)} collective-permute-done((f32[17,512]{1,0:T(8,128)S(1)}, f32[17,512]{1,0:T(8,128)S(1)}, u32[]{:S(2)}, u32[]{:S(2)}) %collective-permute-start.20) | collective-permute-done | bytes 34848 | tf_op jit(solution)/shard_map/ppermute | solution.py:21
  335.1 2.8 collective-permute-start.29
  338.0 3.7 collective-permute-start.28
  343.1 2.4 collective-permute-done.26
  345.6 2.4 collective-permute-start.27
  348.0 3.9 collective-permute-done.27
  352.8 40.6 %all-gather.5.cloned.1.call-done = f32[1024,512]{1,0:T(8,128)} async-done(((f32[128,512]{1,0:T(8,128)}), f32[1024,512]{1,0:T(8,128)}) %all-gather.5.cloned.1.call-update) | async-done | bytes 2097168 | tf_op jit(solution)/shard_map/all_gather | solution.py:55
  393.5 3.1 copy.40
  (113 shorter events, 31.5 us)
Async XLA Ops:
  7.2 1.2 copy-start
  7.2 142.9 %reduce-scatter.3.cloned.1.call-start = ((), (), s32[]{:S(2)}) async-start(), calls=%async_computation.2 | async-start | bytes 2506752 | tf_op jit(solution)/shard_map/reduce_scatter | solution.py:35
  12.9 2.0 copy-start.3
  15.1 4.4 %collective-permute-start = (f32[1024,512]{1,0:T(8,128)S(1)}, f32[1024,512]{1,0:T(8,128)}, u32[]{:S(2)}, u32[]{:S(2)}) collective-permute-start(f32[1024,512]{1,0:T(8,128)S(1)} %constant_dynamic-slice_fusion.3), channel_id=1, source_target_pairs={{0,1},{1,0},{2,3},{3,2},{4,5},{5,4},{6,7},{7,6},{8,9},{9,8},{10,11... | collective-permute-start | bytes 6291464 | tf_op jit(solution)/shard_map/ppermute | solution.py:69
  23.2 26.0 %collective-permute-start.1 = (f32[512,512]{1,0:T(8,128)}, f32[512,512]{1,0:T(8,128)}, u32[]{:S(2)}, u32[]{:S(2)}) collective-permute-start(f32[512,512]{1,0:T(8,128)} %constant_dynamic-slice_fusion.2), channel_id=1, source_target_pairs={{0,2},{2,0},{1,3},{3,1},{4,6},{6,4},{5,7},{7,5},{8,10},{10,8},{9,1... | collective-permute-start | bytes 3145736 | tf_op jit(solution)/shard_map/ppermute | solution.py:69
  51.4 13.6 %collective-permute-start.2 = (bf16[512,512]{1,0:T(8,128)(2,1)}, bf16[512,512]{1,0:T(8,128)(2,1)S(1)}, u32[]{:S(2)}, u32[]{:S(2)}) collective-permute-start(bf16[512,512]{1,0:T(8,128)(2,1)} %add_convert_fusion), channel_id=1, source_target_pairs={{0,2},{2,0},{1,3},{3,1},{4,6},{6,4},{5,7},{7,5},{8,10},{10,8},{9,1... | collective-permute-start | bytes 1572872 | tf_op jit(solution)/shard_map/ppermute | solution.py:72
  66.7 2.7 collective-permute-start.3
  69.4 30.9 %copy-start.5 = (bf16[1024,512]{1,0:T(8,128)(2,1)}, bf16[1024,512]{1,0:T(8,128)(2,1)S(1)}, u32[]{:S(2)}) copy-start(bf16[1024,512]{1,0:T(8,128)(2,1)S(1)} %collective-permute-done.3) | copy-start | bytes 3145732
  95.3 5.8 %copy-start.2 = (f32[2048,1024]{0,1:T(8,128)S(1)}, f32[2048,1024]{0,1:T(8,128)}, u32[]{:S(2)}) copy-start(f32[2048,1024]{0,1:T(8,128)} %get-tuple-element.65) | copy-start | bytes 25165828
  105.1 126.4 %all-gather.3.cloned.1.call-start = ((), (), s32[]{:S(2)}) async-start(), calls=%async_computation.3 | async-start | bytes 1179648 | tf_op jit(solution)/shard_map/all_gather | solution.py:55
  151.9 11.0 %collective-permute-start.4 = (f32[17,512]{1,0:T(8,128)S(1)}, f32[17,512]{1,0:T(8,128)S(1)}, u32[]{:S(2)}, u32[]{:S(2)}) collective-permute-start(f32[17,512]{1,0:T(8,128)S(1)} %get-tuple-element.57), channel_id=1, source_target_pairs={{0,4},{4,8},{8,12},{12,16},{16,20},{20,24},{24,28},{28,0},{1,5},{5... | collective-permute-start | bytes 104456 | tf_op jit(solution)/shard_map/ppermute | solution.py:21
  154.2 9.2 %collective-permute-start.10 = (f32[17,512]{1,0:T(8,128)S(1)}, f32[17,512]{1,0:T(8,128)S(1)}, u32[]{:S(2)}, u32[]{:S(2)}) collective-permute-start(f32[17,512]{1,0:T(8,128)S(1)} %get-tuple-element.58), channel_id=1, source_target_pairs={{0,28},{4,0},{8,4},{12,8},{16,12},{20,16},{24,20},{28,24},{1,29},{... | collective-permute-start | bytes 104456 | tf_op jit(solution)/shard_map/ppermute | solution.py:21
  157.7 8.0 %collective-permute-start.9 = (f32[17,512]{1,0:T(8,128)S(1)}, f32[17,512]{1,0:T(8,128)S(1)}, u32[]{:S(2)}, u32[]{:S(2)}) collective-permute-start(f32[17,512]{1,0:T(8,128)S(1)} %get-tuple-element.59), channel_id=1, source_target_pairs={{0,24},{4,28},{8,0},{12,4},{16,8},{20,12},{24,16},{28,20},{1,25},{... | collective-permute-start | bytes 104456 | tf_op jit(solution)/shard_map/ppermute | solution.py:21
  158.8 6.9 %collective-permute-start.8 = (f32[17,512]{1,0:T(8,128)S(1)}, f32[17,512]{1,0:T(8,128)S(1)}, u32[]{:S(2)}, u32[]{:S(2)}) collective-permute-start(f32[17,512]{1,0:T(8,128)S(1)} %get-tuple-element.60), channel_id=1, source_target_pairs={{0,20},{4,24},{8,28},{12,0},{16,4},{20,8},{24,12},{28,16},{1,21},{... | collective-permute-start | bytes 104456 | tf_op jit(solution)/shard_map/ppermute | solution.py:21
  160.3 5.6 %collective-permute-start.7 = (f32[17,512]{1,0:T(8,128)S(1)}, f32[17,512]{1,0:T(8,128)S(1)}, u32[]{:S(2)}, u32[]{:S(2)}) collective-permute-start(f32[17,512]{1,0:T(8,128)S(1)} %get-tuple-element.61), channel_id=1, source_target_pairs={{0,16},{4,20},{8,24},{12,28},{16,0},{20,4},{24,8},{28,12},{1,17},{... | collective-permute-start | bytes 104456 | tf_op jit(solution)/shard_map/ppermute | solution.py:21
  162.9 8.1 %collective-permute-start.6 = (f32[17,512]{1,0:T(8,128)S(1)}, f32[17,512]{1,0:T(8,128)S(1)}, u32[]{:S(2)}, u32[]{:S(2)}) collective-permute-start(f32[17,512]{1,0:T(8,128)S(1)} %get-tuple-element.62), channel_id=1, source_target_pairs={{0,12},{4,16},{8,20},{12,24},{16,28},{20,0},{24,4},{28,8},{1,13},{... | collective-permute-start | bytes 104456 | tf_op jit(solution)/shard_map/ppermute | solution.py:21
  163.4 7.5 %collective-permute-start.5 = (f32[17,512]{1,0:T(8,128)S(1)}, f32[17,512]{1,0:T(8,128)S(1)}, u32[]{:S(2)}, u32[]{:S(2)}) collective-permute-start(f32[17,512]{1,0:T(8,128)S(1)} %get-tuple-element.63), channel_id=1, source_target_pairs={{0,8},{4,12},{8,16},{12,20},{16,24},{20,28},{24,0},{28,4},{1,9},{5... | collective-permute-start | bytes 104456 | tf_op jit(solution)/shard_map/ppermute | solution.py:21
  171.9 10.5 %collective-permute-start.11 = (bf16[16,512]{1,0:T(8,128)(2,1)S(1)}, bf16[16,512]{1,0:T(8,128)(2,1)S(1)}, u32[]{:S(2)}, u32[]{:S(2)}) collective-permute-start(bf16[16,512]{1,0:T(8,128)(2,1)S(1)} %fusion.32), channel_id=1, source_target_pairs={{0,28},{4,0},{8,4},{12,8},{16,12},{20,16},{24,20},{28,24},{1,29},{... | collective-permute-start | bytes 49160 | tf_op jit(solution)/shard_map/ppermute | solution.py:21
  173.3 18.9 %collective-permute-start.17 = (bf16[16,512]{1,0:T(8,128)(2,1)S(1)}, bf16[16,512]{1,0:T(8,128)(2,1)S(1)}, u32[]{:S(2)}, u32[]{:S(2)}) collective-permute-start(bf16[16,512]{1,0:T(8,128)(2,1)S(1)} %fusion.32), channel_id=1, source_target_pairs={{0,4},{4,8},{8,12},{12,16},{16,20},{20,24},{24,28},{28,0},{1,5},{5... | collective-permute-start | bytes 49160 | tf_op jit(solution)/shard_map/ppermute | solution.py:21
  175.4 16.8 %collective-permute-start.16 = (bf16[16,512]{1,0:T(8,128)(2,1)S(1)}, bf16[16,512]{1,0:T(8,128)(2,1)S(1)}, u32[]{:S(2)}, u32[]{:S(2)}) collective-permute-start(bf16[16,512]{1,0:T(8,128)(2,1)S(1)} %fusion.32), channel_id=1, source_target_pairs={{0,8},{4,12},{8,16},{12,20},{16,24},{20,28},{24,0},{28,4},{1,9},{5... | collective-permute-start | bytes 49160 | tf_op jit(solution)/shard_map/ppermute | solution.py:21
  175.4 16.8 %collective-permute-start.15 = (bf16[16,512]{1,0:T(8,128)(2,1)S(1)}, bf16[16,512]{1,0:T(8,128)(2,1)S(1)}, u32[]{:S(2)}, u32[]{:S(2)}) collective-permute-start(bf16[16,512]{1,0:T(8,128)(2,1)S(1)} %fusion.32), channel_id=1, source_target_pairs={{0,12},{4,16},{8,20},{12,24},{16,28},{20,0},{24,4},{28,8},{1,13},{... | collective-permute-start | bytes 49160 | tf_op jit(solution)/shard_map/ppermute | solution.py:21
  178.5 13.8 %collective-permute-start.14 = (bf16[16,512]{1,0:T(8,128)(2,1)S(1)}, bf16[16,512]{1,0:T(8,128)(2,1)S(1)}, u32[]{:S(2)}, u32[]{:S(2)}) collective-permute-start(bf16[16,512]{1,0:T(8,128)(2,1)S(1)} %fusion.32), channel_id=1, source_target_pairs={{0,16},{4,20},{8,24},{12,28},{16,0},{20,4},{24,8},{28,12},{1,17},{... | collective-permute-start | bytes 49160 | tf_op jit(solution)/shard_map/ppermute | solution.py:21
  182.4 3.7 collective-permute-start.12
  186.1 6.1 %collective-permute-start.13 = (bf16[16,512]{1,0:T(8,128)(2,1)S(1)}, bf16[16,512]{1,0:T(8,128)(2,1)S(1)}, u32[]{:S(2)}, u32[]{:S(2)}) collective-permute-start(bf16[16,512]{1,0:T(8,128)(2,1)S(1)} %fusion.32), channel_id=1, source_target_pairs={{0,20},{4,24},{8,28},{12,0},{16,4},{20,8},{24,12},{28,16},{1,21},{... | collective-permute-start | bytes 49160 | tf_op jit(solution)/shard_map/ppermute | solution.py:21
  193.1 115.9 %reduce-scatter.5.cloned.1.call-start = ((), (), s32[]{:S(2)}) async-start(), calls=%async_computation.4 | async-start | bytes 2506752 | tf_op jit(solution)/shard_map/reduce_scatter | solution.py:35
  255.6 5.0 %copy-start.4 = (f32[2048]{0:T(1024)}, f32[2048]{0:T(1024)S(1)}, u32[]{:S(2)}) copy-start(f32[2048]{0:T(1024)S(1)} %log_add_fusion) | copy-start | bytes 24580
  255.7 5.8 %copy-start.1 = (f32[2048,1024]{0,1:T(8,128)S(1)}, f32[2048,1024]{0,1:T(8,128)}, u32[]{:S(2)}) copy-start(f32[2048,1024]{0,1:T(8,128)} %get-tuple-element.67) | copy-start | bytes 25165828
  267.0 126.5 %all-gather.5.cloned.1.call-start = ((), (), s32[]{:S(2)}) async-start(), calls=%async_computation.5 | async-start | bytes 2359296 | tf_op jit(solution)/shard_map/all_gather | solution.py:55
  310.9 11.7 %collective-permute-start.18 = (f32[17,512]{1,0:T(8,128)S(1)}, f32[17,512]{1,0:T(8,128)S(1)}, u32[]{:S(2)}, u32[]{:S(2)}) collective-permute-start(f32[17,512]{1,0:T(8,128)S(1)} %get-tuple-element.50), channel_id=1, source_target_pairs={{0,4},{4,8},{8,12},{12,16},{16,20},{20,24},{24,28},{28,0},{1,5},{5... | collective-permute-start | bytes 104456 | tf_op jit(solution)/shard_map/ppermute | solution.py:21
  313.4 9.7 %collective-permute-start.24 = (f32[17,512]{1,0:T(8,128)S(1)}, f32[17,512]{1,0:T(8,128)S(1)}, u32[]{:S(2)}, u32[]{:S(2)}) collective-permute-start(f32[17,512]{1,0:T(8,128)S(1)} %get-tuple-element.51), channel_id=1, source_target_pairs={{0,28},{4,0},{8,4},{12,8},{16,12},{20,16},{24,20},{28,24},{1,29},{... | collective-permute-start | bytes 104456 | tf_op jit(solution)/shard_map/ppermute | solution.py:21
  316.8 8.5 %collective-permute-start.23 = (f32[17,512]{1,0:T(8,128)S(1)}, f32[17,512]{1,0:T(8,128)S(1)}, u32[]{:S(2)}, u32[]{:S(2)}) collective-permute-start(f32[17,512]{1,0:T(8,128)S(1)} %get-tuple-element.52), channel_id=1, source_target_pairs={{0,24},{4,28},{8,0},{12,4},{16,8},{20,12},{24,16},{28,20},{1,25},{... | collective-permute-start | bytes 104456 | tf_op jit(solution)/shard_map/ppermute | solution.py:21
  318.7 6.6 %collective-permute-start.22 = (f32[17,512]{1,0:T(8,128)S(1)}, f32[17,512]{1,0:T(8,128)S(1)}, u32[]{:S(2)}, u32[]{:S(2)}) collective-permute-start(f32[17,512]{1,0:T(8,128)S(1)} %get-tuple-element.53), channel_id=1, source_target_pairs={{0,20},{4,24},{8,28},{12,0},{16,4},{20,8},{24,12},{28,16},{1,21},{... | collective-permute-start | bytes 104456 | tf_op jit(solution)/shard_map/ppermute | solution.py:21
  320.2 5.6 %collective-permute-start.21 = (f32[17,512]{1,0:T(8,128)S(1)}, f32[17,512]{1,0:T(8,128)S(1)}, u32[]{:S(2)}, u32[]{:S(2)}) collective-permute-start(f32[17,512]{1,0:T(8,128)S(1)} %get-tuple-element.54), channel_id=1, source_target_pairs={{0,16},{4,20},{8,24},{12,28},{16,0},{20,4},{24,8},{28,12},{1,17},{... | collective-permute-start | bytes 104456 | tf_op jit(solution)/shard_map/ppermute | solution.py:21
  322.6 8.1 %collective-permute-start.20 = (f32[17,512]{1,0:T(8,128)S(1)}, f32[17,512]{1,0:T(8,128)S(1)}, u32[]{:S(2)}, u32[]{:S(2)}) collective-permute-start(f32[17,512]{1,0:T(8,128)S(1)} %get-tuple-element.55), channel_id=1, source_target_pairs={{0,12},{4,16},{8,20},{12,24},{16,28},{20,0},{24,4},{28,8},{1,13},{... | collective-permute-start | bytes 104456 | tf_op jit(solution)/shard_map/ppermute | solution.py:21
  323.1 7.5 %collective-permute-start.19 = (f32[17,512]{1,0:T(8,128)S(1)}, f32[17,512]{1,0:T(8,128)S(1)}, u32[]{:S(2)}, u32[]{:S(2)}) collective-permute-start(f32[17,512]{1,0:T(8,128)S(1)} %get-tuple-element.56), channel_id=1, source_target_pairs={{0,8},{4,12},{8,16},{12,20},{16,24},{20,28},{24,0},{28,4},{1,9},{5... | collective-permute-start | bytes 104456 | tf_op jit(solution)/shard_map/ppermute | solution.py:21
  331.5 10.1 %collective-permute-start.25 = (f32[16,512]{1,0:T(8,128)S(1)}, f32[16,512]{1,0:T(8,128)S(1)}, u32[]{:S(2)}, u32[]{:S(2)}) collective-permute-start(f32[16,512]{1,0:T(8,128)S(1)} %fusion.26), channel_id=1, source_target_pairs={{0,28},{4,0},{8,4},{12,8},{16,12},{20,16},{24,20},{28,24},{1,29},{... | collective-permute-start | bytes 98312 | tf_op jit(solution)/shard_map/ppermute | solution.py:21
  333.4 18.6 %collective-permute-start.31 = (f32[16,512]{1,0:T(8,128)S(1)}, f32[16,512]{1,0:T(8,128)S(1)}, u32[]{:S(2)}, u32[]{:S(2)}) collective-permute-start(f32[16,512]{1,0:T(8,128)S(1)} %fusion.26), channel_id=1, source_target_pairs={{0,4},{4,8},{8,12},{12,16},{16,20},{20,24},{24,28},{28,0},{1,5},{5... | collective-permute-start | bytes 98312 | tf_op jit(solution)/shard_map/ppermute | solution.py:21
  335.1 16.8 %collective-permute-start.30 = (f32[16,512]{1,0:T(8,128)S(1)}, f32[16,512]{1,0:T(8,128)S(1)}, u32[]{:S(2)}, u32[]{:S(2)}) collective-permute-start(f32[16,512]{1,0:T(8,128)S(1)} %fusion.26), channel_id=1, source_target_pairs={{0,8},{4,12},{8,16},{12,20},{16,24},{20,28},{24,0},{28,4},{1,9},{5... | collective-permute-start | bytes 98312 | tf_op jit(solution)/shard_map/ppermute | solution.py:21
  335.1 16.8 %collective-permute-start.29 = (f32[16,512]{1,0:T(8,128)S(1)}, f32[16,512]{1,0:T(8,128)S(1)}, u32[]{:S(2)}, u32[]{:S(2)}) collective-permute-start(f32[16,512]{1,0:T(8,128)S(1)} %fusion.26), channel_id=1, source_target_pairs={{0,12},{4,16},{8,20},{12,24},{16,28},{20,0},{24,4},{28,8},{1,13},{... | collective-permute-start | bytes 98312 | tf_op jit(solution)/shard_map/ppermute | solution.py:21
  338.0 13.9 %collective-permute-start.28 = (f32[16,512]{1,0:T(8,128)S(1)}, f32[16,512]{1,0:T(8,128)S(1)}, u32[]{:S(2)}, u32[]{:S(2)}) collective-permute-start(f32[16,512]{1,0:T(8,128)S(1)} %fusion.26), channel_id=1, source_target_pairs={{0,16},{4,20},{8,24},{12,28},{16,0},{20,4},{24,8},{28,12},{1,17},{... | collective-permute-start | bytes 98312 | tf_op jit(solution)/shard_map/ppermute | solution.py:21
  341.6 3.9 collective-permute-start.26
  345.6 6.3 %collective-permute-start.27 = (f32[16,512]{1,0:T(8,128)S(1)}, f32[16,512]{1,0:T(8,128)S(1)}, u32[]{:S(2)}, u32[]{:S(2)}) collective-permute-start(f32[16,512]{1,0:T(8,128)S(1)} %fusion.26), channel_id=1, source_target_pairs={{0,20},{4,24},{8,28},{12,0},{16,4},{20,8},{24,12},{28,16},{1,21},{... | collective-permute-start | bytes 98312 | tf_op jit(solution)/shard_map/ppermute | solution.py:21
Sparse Core Ops, SparseCore 0:
  105.2 44.8 reduce-scatter.2
  193.2 38.1 all-gather.2
  267.1 41.8 reduce-scatter.4
  353.0 40.4 all-gather.4

commit v7 on v4

--- a/solution.py
+++ b/solution.py
@@ -71,6 +71,21 @@
     return block
 
 
+def _merge(a, b):
+    top = jnp.maximum(a[0], b[0])
+    return jnp.stack([top, a[1] * jnp.exp(a[0] - top) + b[1] * jnp.exp(b[0] - top)])
+
+
+def _log_total(scores):
+    local_top = jnp.max(scores, axis=1)
+    pair = jnp.stack([local_top, jnp.sum(jnp.exp(scores - local_top[:, None]), axis=1)])
+    for axis in ("core", "xl"):
+        other = lax.ppermute(pair, axis, [(0, 1), (1, 0)])
+        low = lax.axis_index(axis) == 0
+        pair = _merge(jnp.where(low, pair, other), jnp.where(low, other, pair))
+    return pair[0] + jnp.log(pair[1])
+
+
 def on_device(embeddings, basis, start_centroids):
     row_count = embeddings.shape[0]
     count = start_centroids.shape[0]
@@ -87,10 +102,7 @@
             )
             / TEMPER
         )
-        local_top = jnp.max(scores, axis=1)
-        top = lax.pmax(local_top, CENT_AXES)
-        total = lax.psum(jnp.sum(jnp.exp(scores - top[:, None]), axis=1), CENT_AXES)
-        log_total = top + jnp.log(total)
+        log_total = _log_total(scores)
         weights = jnp.exp(scores - log_total[:, None])
         local_mass = jnp.sum(weights, axis=0)
         local_numer = lax.dot_general(

time: 386 us -> 349 us (0.904)
  blocking collectives: 25.3 us -> 0 us
  other arithmetic: 32 us -> 18.4 us
  waiting for transfers between devices: 235 us -> 245 us
  matrix products: 24.1 us -> 16.9 us
    pmax x2 -> x0, blocking collectives: 13.2 us -> none  [on_device(): top = lax.pmax(local_top, CENT_AXES)]
    psum x2 -> x0, blocking collectives: 12.1 us -> none  [on_device(): total = lax.psum(jnp.sum(jnp.exp(scores - top[:, None]), axis=1), CENT_AXES)]
    ppermute x0 -> x4, waiting for transfers between devices: none -> 7.67 us  [_log_total(): other = lax.ppermute(pair, axis, [(0, 1), (1, 0)])]
    dot_general x2, matrix products: 14.7 us -> 7.58 us  [on_device(): lax.dot_general(projected, cent_bf, (((1,), (1,)), ((), ())), preferred_e...]
    reduce_sum x2, other arithmetic: 9.97 us -> 2.89 us  [on_device(): local_mass = jnp.sum(weights, axis=0)]
    reduce_sum x2, other arithmetic: 9.57 us -> 2.81 us  [_log_total(): jnp.sum(jnp.exp(scores - local_top[:, None]), axis=1)]
    unnamed x11 -> x7, local copies, waits for them, and re-layouts: 7.73 us -> 6.21 us
  transfers between devices with their start and end apart: 26 -> 30, of which waited for: 24 -> 27; matrix products, arithmetic and copies ran while one was open for 1% -> 1% of each run, Pallas kernels for 0% -> 0%
where the time goes in v7:
time: 349 us; the launch traced here: 348 us
  waiting for transfers between devices  245 us (70%)
  starting transfers between devices  42.1 us (12%)
  other arithmetic  18.4 us (5%)
  matrix products  16.9 us (5%)
  between operations  14.1 us (4%)
  local copies, waits for them, and re-layouts  11.3 us (3%)
    reduce_scatter x2, waiting for transfers between devices, _reduce_rows(): payload = lax.psum_scatter(payload, 'z', scatter_dimension=0, tiled=True)  86.8 us
    all_gather x2, waiting for transfers between devices, _gather_rows(): return lax.all_gather(block, 'z', axis=0, tiled=True)  76.2 us
    ppermute x18, starting transfers between devices, _swap(): return lax.ppermute(x, axis, [(i, i ^ bit) for i in range(size)])  34.9 us
    ppermute x18, waiting for transfers between devices, _swap(): return lax.ppermute(x, axis, [(i, i ^ bit) for i in range(size)])  31.9 us
    ppermute x2, waiting for transfers between devices, _project(): partial = keep + lax.ppermute(send, axis, [(0, 1), (1, 0)])  28 us
    ppermute x2, waiting for transfers between devices, _project(): other = lax.ppermute(block, axis, [(0, 1), (1, 0)])  14.5 us
    ppermute x4, waiting for transfers between devices, _log_total(): other = lax.ppermute(pair, axis, [(0, 1), (1, 0)])  7.67 us
    dot_general x2, matrix products, on_device(): lax.dot_general(projected, cent_bf, (((1,), (1,)), ((), ())), preferred_e...  7.58 us
  transfers between devices with their start and end apart: 30, of which 27 were waited for; matrix products, arithmetic and copies ran while one was open for 1% of the time, Pallas kernels for 0%

profile of v7, /device:TPU:2, one launch (start us, length us, event | category | flops | bytes accessed | tf_op | source)
XLA Modules:
  0.0 348.0 jit_solution(13008515234022563669)
XLA Ops:
  8.4 4.5 %fusion.34 = f32[2048,512]{1,0:T(8,128)S(1)} fusion(bf16[2048,1024]{1,0:T(8,128)(2,1)} %param.7, bf16[1024,512]{1,0:T(8,128)(2,1)S(1)} %copy-done), kind=kOutput, calls=%fused_computation.95 | convolution fusion | flops 2147483648 | bytes 9437184 | tf_op jit(solution)/shard_map/dot_general | solution.py:60
  12.9 1.9 copy-done.1
  15.2 4.3 %collective-permute-done = f32[1024,512]{1,0:T(8,128)} collective-permute-done((f32[1024,512]{1,0:T(8,128)S(1)}, f32[1024,512]{1,0:T(8,128)}, u32[]{:S(2)}, u32[]{:S(2)}) %collective-permute-start) | collective-permute-done | bytes 2097184 | tf_op jit(solution)/shard_map/ppermute | solution.py:66
  19.4 2.7 dynamic-slice_add_fusion
  23.2 2.2 collective-permute-start.1
  25.4 23.8 %collective-permute-done.1 = f32[512,512]{1,0:T(8,128)} collective-permute-done((f32[512,512]{1,0:T(8,128)}, f32[512,512]{1,0:T(8,128)}, u32[]{:S(2)}, u32[]{:S(2)}) %collective-permute-start.1) | collective-permute-done | bytes 1048608 | tf_op jit(solution)/shard_map/ppermute | solution.py:66
  49.2 2.2 add_convert_fusion
  51.4 1.7 collective-permute-start.2
  53.1 11.9 %collective-permute-done.2 = bf16[512,512]{1,0:T(8,128)(2,1)S(1)} collective-permute-done((bf16[512,512]{1,0:T(8,128)(2,1)}, bf16[512,512]{1,0:T(8,128)(2,1)S(1)}, u32[]{:S(2)}, u32[]{:S(2)}) %collective-permute-start.2) | collective-permute-done | bytes 524320 | tf_op jit(solution)/shard_map/ppermute | solution.py:69
  65.0 1.6 maximum_select_fusion.1
  66.7 2.6 collective-permute-done.3
  69.3 4.0 %multiply_reduce_fusion.1 = (f32[2048]{0:T(1024)S(1)}, f32[2048,1024]{0,1:T(8,128)S(1)}) fusion(f32[1024,512]{1,0:T(8,128)} %param.9, bf16[1024,512]{1,0:T(8,128)(2,1)S(1)} %collective-permute-done.3, bf16[1024,512]{1,0:T(8,128)(2,1)S(1)} %maximum_select_fusion.1, pred[]{:T(512)S(6)} %eq.25), kind=kOutput, calls=%fused_computation.9 | convolution fusion | flops 2161637376 | bytes 12591105 | tf_op jit(solution)/shard_map/dot_general | solution.py:100
  76.1 1.7 collective-permute-start.5
  77.8 2.3 collective-permute-done.5
  81.6 2.4 fusion.6
  84.0 1.6 select_maximum_fusion.1
  85.7 45.1 %reduce-scatter.3.cloned.1.call-done = f32[136,512]{1,0:T(8,128)} async-done(((f32[1088,512]{1,0:T(8,128)}), f32[136,512]{1,0:T(8,128)}) %reduce-scatter.3.cloned.1.call-update) | async-done | bytes 278544 | tf_op jit(solution)/shard_map/reduce_scatter | solution.py:33
  131.6 1.5 collective-permute-start.9
  135.3 3.3 collective-permute-start.10
  139.2 2.9 collective-permute-start.7
  142.2 2.0 collective-permute-start.11
  145.0 2.3 collective-permute-start.8
  147.4 3.1 collective-permute-done.8
  151.4 2.2 collective-permute-start.12
  153.6 3.1 collective-permute-done.12
  156.7 2.9 collective-permute-start.13
  159.6 2.6 collective-permute-done.13
  163.5 3.0 collective-permute-done.14
  167.5 37.0 %all-gather.3.cloned.1.call-done = bf16[1024,512]{1,0:T(8,128)(2,1)} async-done(((bf16[128,512]{1,0:T(8,128)(2,1)}), bf16[1024,512]{1,0:T(8,128)(2,1)}) %all-gather.3.cloned.1.call-update) | async-done | bytes 1048592 | tf_op jit(solution)/shard_map/all_gather | solution.py:50
  204.6 3.6 %multiply_reduce_fusion = (f32[2048]{0:T(1024)S(1)}, f32[2048,1024]{0,1:T(8,128)S(1)}) fusion(bf16[1024,512]{1,0:T(8,128)(2,1)} %all-gather.3.cloned.1.call-done, bf16[1024,512]{1,0:T(8,128)(2,1)S(1)} %collective-permute-done.3, bf16[1024,512]{1,0:T(8,128)(2,1)S(1)} %maximum_select_fusion.1, pred[]{:T(512)S(6)} %eq.25), kind=kOutput, calls=%fused_computation.8 | convolution fusion | flops 2161113088 | bytes 11542529 | tf_op jit(solution)/shard_map/dot_general | solution.py:100
  211.6 3.2 collective-permute-done.16
  214.9 1.5 fusion.2
  216.4 2.4 fusion.4
  218.8 1.6 select_maximum_fusion
  220.5 41.6 %reduce-scatter.5.cloned.1.call-done = f32[136,512]{1,0:T(8,128)} async-done(((f32[1088,512]{1,0:T(8,128)}), f32[136,512]{1,0:T(8,128)}) %reduce-scatter.5.cloned.1.call-update) | async-done | bytes 278544 | tf_op jit(solution)/shard_map/reduce_scatter | solution.py:33
  262.8 1.7 collective-permute-start.20
  266.6 2.7 collective-permute-start.21
  270.6 2.7 collective-permute-start.18
  273.5 1.7 collective-permute-start.22
  276.5 1.6 collective-permute-start.19
  278.6 3.4 collective-permute-done.19
  282.1 1.6 collective-permute-start.23
  283.7 3.9 %collective-permute-done.23 = f32[16,512]{1,0:T(8,128)S(1)} collective-permute-done((f32[16,512]{1,0:T(8,128)S(1)}, f32[16,512]{1,0:T(8,128)S(1)}, u32[]{:S(2)}, u32[]{:S(2)}) %collective-permute-start.23) | collective-permute-done | bytes 32800 | tf_op jit(solution)/shard_map/ppermute | solution.py:18
  287.6 2.7 collective-permute-start.24
  290.2 3.2 collective-permute-done.24
  294.2 4.3 %collective-permute-done.25 = f32[64,512]{1,0:T(8,128)S(1)} collective-permute-done((f32[64,512]{1,0:T(8,128)S(1)}, f32[64,512]{1,0:T(8,128)S(1)}, u32[]{:S(2)}, u32[]{:S(2)}) %collective-permute-start.25) | collective-permute-done | bytes 131104 | tf_op jit(solution)/shard_map/ppermute | solution.py:18
  299.2 39.2 %all-gather.5.cloned.1.call-done = f32[1024,512]{1,0:T(8,128)} async-done(((f32[128,512]{1,0:T(8,128)}), f32[1024,512]{1,0:T(8,128)}) %all-gather.5.cloned.1.call-update) | async-done | bytes 2097168 | tf_op jit(solution)/shard_map/all_gather | solution.py:50
  338.4 3.1 copy.6
  (88 shorter events, 25.8 us)
Async XLA Ops:
  7.2 1.2 copy-start
  7.2 123.7 %reduce-scatter.3.cloned.1.call-start = ((), (), s32[]{:S(2)}) async-start(), calls=%async_computation.2 | async-start | bytes 2506752 | tf_op jit(solution)/shard_map/reduce_scatter | solution.py:33
  12.9 2.0 copy-start.1
  15.1 4.4 %collective-permute-start = (f32[1024,512]{1,0:T(8,128)S(1)}, f32[1024,512]{1,0:T(8,128)}, u32[]{:S(2)}, u32[]{:S(2)}) collective-permute-start(f32[1024,512]{1,0:T(8,128)S(1)} %constant_dynamic-slice_fusion.11), channel_id=1, source_target_pairs={{0,1},{1,0},{2,3},{3,2},{4,5},{5,4},{6,7},{7,6},{8,9},{9,8},{10,11... | collective-permute-start | bytes 6291464 | tf_op jit(solution)/shard_map/ppermute | solution.py:66
  23.2 26.0 %collective-permute-start.1 = (f32[512,512]{1,0:T(8,128)}, f32[512,512]{1,0:T(8,128)}, u32[]{:S(2)}, u32[]{:S(2)}) collective-permute-start(f32[512,512]{1,0:T(8,128)} %constant_dynamic-slice_fusion.10), channel_id=1, source_target_pairs={{0,2},{2,0},{1,3},{3,1},{4,6},{6,4},{5,7},{7,5},{8,10},{10,8},{9,1... | collective-permute-start | bytes 3145736 | tf_op jit(solution)/shard_map/ppermute | solution.py:66
  51.4 13.6 %collective-permute-start.2 = (bf16[512,512]{1,0:T(8,128)(2,1)}, bf16[512,512]{1,0:T(8,128)(2,1)S(1)}, u32[]{:S(2)}, u32[]{:S(2)}) collective-permute-start(bf16[512,512]{1,0:T(8,128)(2,1)} %add_convert_fusion), channel_id=1, source_target_pairs={{0,2},{2,0},{1,3},{3,1},{4,6},{6,4},{5,7},{7,5},{8,10},{10,8},{9,1... | collective-permute-start | bytes 1572872 | tf_op jit(solution)/shard_map/ppermute | solution.py:69
  66.6 2.7 collective-permute-start.3
  74.7 1.3 collective-permute-start.4
  76.1 4.0 %collective-permute-start.5 = (f32[2,2048]{1,0:T(2,128)S(1)}, f32[2,2048]{1,0:T(2,128)S(1)}, u32[]{:S(2)}, u32[]{:S(2)}) collective-permute-start(f32[2,2048]{1,0:T(2,128)S(1)} %pad_maximum_fusion.1), channel_id=1, source_target_pairs={{0,2},{2,0},{1,3},{3,1},{4,6},{6,4},{5,7},{7,5},{8,10},{10,8},{9,1... | collective-permute-start | bytes 49160 | tf_op jit(solution)/shard_map/ppermute | solution.py:83
  85.6 118.9 %all-gather.3.cloned.1.call-start = ((), (), s32[]{:S(2)}) async-start(), calls=%async_computation.3 | async-start | bytes 1179648 | tf_op jit(solution)/shard_map/all_gather | solution.py:50
  131.6 3.6 %collective-permute-start.9 = (f32[64]{0:T(128)S(1)}, f32[64]{0:T(128)S(1)}, u32[]{:S(2)}, u32[]{:S(2)}) collective-permute-start(f32[64]{0:T(128)S(1)} %fusion.23), channel_id=1, source_target_pairs={{0,8},{8,0},{16,24},{24,16},{1,9},{9,1},{17,25},{25,17},{2,10},{10... | collective-permute-start | bytes 776 | tf_op jit(solution)/shard_map/ppermute | solution.py:18
  134.1 5.1 %collective-permute-start.6 = (f32[64,512]{1,0:T(8,128)S(1)}, f32[64,512]{1,0:T(8,128)S(1)}, u32[]{:S(2)}, u32[]{:S(2)}) collective-permute-start(f32[64,512]{1,0:T(8,128)S(1)} %constant_dynamic-slice_fusion.9), channel_id=1, source_target_pairs={{0,8},{8,0},{16,24},{24,16},{1,9},{9,1},{17,25},{25,17},{2,10},{10... | collective-permute-start | bytes 393224 | tf_op jit(solution)/shard_map/ppermute | solution.py:18
  135.3 6.8 %collective-permute-start.10 = (f32[32]{0:T(128)S(1)}, f32[32]{0:T(128)S(1)}, u32[]{:S(2)}, u32[]{:S(2)}) collective-permute-start(f32[32]{0:T(128)S(1)} %dynamic_slice.111), channel_id=1, source_target_pairs={{0,16},{8,24},{16,0},{24,8},{1,17},{9,25},{17,1},{25,9},{2,18},{10... | collective-permute-start | bytes 392 | tf_op jit(solution)/shard_map/ppermute | solution.py:18
  139.2 5.9 %collective-permute-start.7 = (f32[32,512]{1,0:T(8,128)S(1)}, f32[32,512]{1,0:T(8,128)S(1)}, u32[]{:S(2)}, u32[]{:S(2)}) collective-permute-start(f32[32,512]{1,0:T(8,128)S(1)} %constant_dynamic-slice_fusion.8), channel_id=1, source_target_pairs={{0,16},{8,24},{16,0},{24,8},{1,17},{9,25},{17,1},{25,9},{2,18},{10... | collective-permute-start | bytes 196616 | tf_op jit(solution)/shard_map/ppermute | solution.py:18
  142.2 5.1 %collective-permute-start.11 = (f32[16]{0:T(128)S(1)}, f32[16]{0:T(128)S(1)}, u32[]{:S(2)}, u32[]{:S(2)}) collective-permute-start(f32[16]{0:T(128)S(1)} %dynamic_slice.113), channel_id=1, source_target_pairs={{0,4},{4,0},{1,5},{5,1},{2,6},{6,2},{3,7},{7,3},{8,12},{12,8},{9,1... | collective-permute-start | bytes 200 | tf_op jit(solution)/shard_map/ppermute | solution.py:18
  145.0 5.5 %collective-permute-start.8 = (f32[16,512]{1,0:T(8,128)S(1)}, f32[16,512]{1,0:T(8,128)S(1)}, u32[]{:S(2)}, u32[]{:S(2)}) collective-permute-start(f32[16,512]{1,0:T(8,128)S(1)} %constant_dynamic-slice_fusion.6), channel_id=1, source_target_pairs={{0,4},{4,0},{1,5},{5,1},{2,6},{6,2},{3,7},{7,3},{8,12},{12,8},{9,1... | collective-permute-start | bytes 98312 | tf_op jit(solution)/shard_map/ppermute | solution.py:18
  151.4 5.3 %collective-permute-start.12 = (bf16[16,512]{1,0:T(8,128)(2,1)S(1)}, bf16[16,512]{1,0:T(8,128)(2,1)S(1)}, u32[]{:S(2)}, u32[]{:S(2)}) collective-permute-start(bf16[16,512]{1,0:T(8,128)(2,1)S(1)} %get-tuple-element.28), channel_id=1, source_target_pairs={{0,4},{4,0},{1,5},{5,1},{2,6},{6,2},{3,7},{7,3},{8,12},{12,8},{9,1... | collective-permute-start | bytes 49160 | tf_op jit(solution)/shard_map/ppermute | solution.py:18
  156.7 5.5 %collective-permute-start.13 = (bf16[32,512]{1,0:T(8,128)(2,1)S(1)}, bf16[32,512]{1,0:T(8,128)(2,1)S(1)}, u32[]{:S(2)}, u32[]{:S(2)}) collective-permute-start(bf16[32,512]{1,0:T(8,128)(2,1)S(1)} %maximum_select_fusion.7), channel_id=1, source_target_pairs={{0,16},{8,24},{16,0},{24,8},{1,17},{9,25},{17,1},{25,9},{2,18},{10... | collective-permute-start | bytes 98312 | tf_op jit(solution)/shard_map/ppermute | solution.py:18
  162.2 4.4 %collective-permute-start.14 = (bf16[64,512]{1,0:T(8,128)(2,1)S(1)}, bf16[64,512]{1,0:T(8,128)(2,1)S(1)}, u32[]{:S(2)}, u32[]{:S(2)}) collective-permute-start(bf16[64,512]{1,0:T(8,128)(2,1)S(1)} %maximum_select_fusion.5), channel_id=1, source_target_pairs={{0,8},{8,0},{16,24},{24,16},{1,9},{9,1},{17,25},{25,17},{2,10},{10... | collective-permute-start | bytes 196616 | tf_op jit(solution)/shard_map/ppermute | solution.py:18
  167.3 94.8 %reduce-scatter.5.cloned.1.call-start = ((), (), s32[]{:S(2)}) async-start(), calls=%async_computation.4 | async-start | bytes 2506752 | tf_op jit(solution)/shard_map/reduce_scatter | solution.py:33
  209.6 1.3 collective-permute-start.15
  211.0 3.8 %collective-permute-start.16 = (f32[2,2048]{1,0:T(2,128)S(1)}, f32[2,2048]{1,0:T(2,128)S(1)}, u32[]{:S(2)}, u32[]{:S(2)}) collective-permute-start(f32[2,2048]{1,0:T(2,128)S(1)} %pad_maximum_fusion.3), channel_id=1, source_target_pairs={{0,2},{2,0},{1,3},{3,1},{4,6},{6,4},{5,7},{7,5},{8,10},{10,8},{9,1... | collective-permute-start | bytes 49160 | tf_op jit(solution)/shard_map/ppermute | solution.py:83
  214.9 1.5 copy-start.2
  220.4 118.0 %all-gather.5.cloned.1.call-start = ((), (), s32[]{:S(2)}) async-start(), calls=%async_computation.5 | async-start | bytes 2359296 | tf_op jit(solution)/shard_map/all_gather | solution.py:50
  262.8 3.6 %collective-permute-start.20 = (f32[64]{0:T(128)S(1)}, f32[64]{0:T(128)S(1)}, u32[]{:S(2)}, u32[]{:S(2)}) collective-permute-start(f32[64]{0:T(128)S(1)} %fusion.20), channel_id=1, source_target_pairs={{0,8},{8,0},{16,24},{24,16},{1,9},{9,1},{17,25},{25,17},{2,10},{10... | collective-permute-start | bytes 776 | tf_op jit(solution)/shard_map/ppermute | solution.py:18
  265.5 5.1 %collective-permute-start.17 = (f32[64,512]{1,0:T(8,128)S(1)}, f32[64,512]{1,0:T(8,128)S(1)}, u32[]{:S(2)}, u32[]{:S(2)}) collective-permute-start(f32[64,512]{1,0:T(8,128)S(1)} %constant_dynamic-slice_fusion.3), channel_id=1, source_target_pairs={{0,8},{8,0},{16,24},{24,16},{1,9},{9,1},{17,25},{25,17},{2,10},{10... | collective-permute-start | bytes 393224 | tf_op jit(solution)/shard_map/ppermute | solution.py:18
  266.6 6.8 %collective-permute-start.21 = (f32[32]{0:T(128)S(1)}, f32[32]{0:T(128)S(1)}, u32[]{:S(2)}, u32[]{:S(2)}) collective-permute-start(f32[32]{0:T(128)S(1)} %dynamic_slice.125), channel_id=1, source_target_pairs={{0,16},{8,24},{16,0},{24,8},{1,17},{9,25},{17,1},{25,9},{2,18},{10... | collective-permute-start | bytes 392 | tf_op jit(solution)/shard_map/ppermute | solution.py:18
  270.6 5.9 %collective-permute-start.18 = (f32[32,512]{1,0:T(8,128)S(1)}, f32[32,512]{1,0:T(8,128)S(1)}, u32[]{:S(2)}, u32[]{:S(2)}) collective-permute-start(f32[32,512]{1,0:T(8,128)S(1)} %constant_dynamic-slice_fusion.2), channel_id=1, source_target_pairs={{0,16},{8,24},{16,0},{24,8},{1,17},{9,25},{17,1},{25,9},{2,18},{10... | collective-permute-start | bytes 196616 | tf_op jit(solution)/shard_map/ppermute | solution.py:18
  273.5 5.1 %collective-permute-start.22 = (f32[16]{0:T(128)S(1)}, f32[16]{0:T(128)S(1)}, u32[]{:S(2)}, u32[]{:S(2)}) collective-permute-start(f32[16]{0:T(128)S(1)} %dynamic_slice.127), channel_id=1, source_target_pairs={{0,4},{4,0},{1,5},{5,1},{2,6},{6,2},{3,7},{7,3},{8,12},{12,8},{9,1... | collective-permute-start | bytes 200 | tf_op jit(solution)/shard_map/ppermute | solution.py:18
  276.5 5.5 %collective-permute-start.19 = (f32[16,512]{1,0:T(8,128)S(1)}, f32[16,512]{1,0:T(8,128)S(1)}, u32[]{:S(2)}, u32[]{:S(2)}) collective-permute-start(f32[16,512]{1,0:T(8,128)S(1)} %constant_dynamic-slice_fusion.1), channel_id=1, source_target_pairs={{0,4},{4,0},{1,5},{5,1},{2,6},{6,2},{3,7},{7,3},{8,12},{12,8},{9,1... | collective-permute-start | bytes 98312 | tf_op jit(solution)/shard_map/ppermute | solution.py:18
  282.1 5.4 %collective-permute-start.23 = (f32[16,512]{1,0:T(8,128)S(1)}, f32[16,512]{1,0:T(8,128)S(1)}, u32[]{:S(2)}, u32[]{:S(2)}) collective-permute-start(f32[16,512]{1,0:T(8,128)S(1)} %add_divide_fusion), channel_id=1, source_target_pairs={{0,4},{4,0},{1,5},{5,1},{2,6},{6,2},{3,7},{7,3},{8,12},{12,8},{9,1... | collective-permute-start | bytes 98312 | tf_op jit(solution)/shard_map/ppermute | solution.py:18
  287.6 5.9 %collective-permute-start.24 = (f32[32,512]{1,0:T(8,128)S(1)}, f32[32,512]{1,0:T(8,128)S(1)}, u32[]{:S(2)}, u32[]{:S(2)}) collective-permute-start(f32[32,512]{1,0:T(8,128)S(1)} %maximum_select_fusion.6), channel_id=1, source_target_pairs={{0,16},{8,24},{16,0},{24,8},{1,17},{9,25},{17,1},{25,9},{2,18},{10... | collective-permute-start | bytes 196616 | tf_op jit(solution)/shard_map/ppermute | solution.py:18
  293.4 5.1 %collective-permute-start.25 = (f32[64,512]{1,0:T(8,128)S(1)}, f32[64,512]{1,0:T(8,128)S(1)}, u32[]{:S(2)}, u32[]{:S(2)}) collective-permute-start(f32[64,512]{1,0:T(8,128)S(1)} %maximum_select_fusion.4), channel_id=1, source_target_pairs={{0,8},{8,0},{16,24},{24,16},{1,9},{9,1},{17,25},{25,17},{2,10},{10... | collective-permute-start | bytes 393224 | tf_op jit(solution)/shard_map/ppermute | solution.py:18
Sparse Core Ops, SparseCore 0:
  85.7 45.0 reduce-scatter.2
  167.4 37.1 all-gather.2
  220.5 41.5 reduce-scatter.4
  299.4 39.0 all-gather.4

commit v8 on v7

--- a/solution.py
+++ b/solution.py
@@ -27,20 +27,27 @@
     count, width = numer.shape
     blocks = 8
     per = count // blocks
-    mass_rows = jnp.zeros((blocks, 8, width), jnp.float32).at[:, 0, :per].set(mass.reshape(blocks, per))
+    subs = 8
+    sub = per // subs
+    mass_rows = jnp.zeros((blocks, subs, width), jnp.float32).at[:, :, :sub].set(mass.reshape(blocks, subs, sub))
     payload = jnp.concatenate([numer.reshape(blocks, per, width), mass_rows], axis=1)
-    payload = payload.reshape(blocks * (per + 8), width)
-    payload = lax.psum_scatter(payload, "z", scatter_dimension=0, tiled=True)
-    numer, mass = payload[:per], payload[per, :per]
+    payload = payload.reshape(blocks * (per + subs), width)
+    state = lax.psum_scatter(payload, "z", scatter_dimension=0, tiled=True)
+    rows, extra = per, subs
     for bit, axis, mask in _bits():
-        half = numer.shape[0] // 2
-        keep = lax.dynamic_slice_in_dim(numer, bit * half, half, axis=0)
-        send = lax.dynamic_slice_in_dim(numer, (1 - bit) * half, half, axis=0)
-        keep_mass = lax.dynamic_slice_in_dim(mass, bit * half, half, axis=0)
-        send_mass = lax.dynamic_slice_in_dim(mass, (1 - bit) * half, half, axis=0)
-        numer = keep + _swap(send, axis, mask)
-        mass = keep_mass + _swap(send_mass, axis, mask)
-    return numer, mass
+        rows, extra = rows // 2, extra // 2
+        numer_part, mass_part = state[: 2 * rows], state[2 * rows :]
+
+        def half(which):
+            return jnp.concatenate(
+                [
+                    lax.dynamic_slice_in_dim(numer_part, which * rows, rows, axis=0),
+                    lax.dynamic_slice_in_dim(mass_part, which * extra, extra, axis=0),
+                ]
+            )
+
+        state = half(bit) + _swap(half(1 - bit), axis, mask)
+    return state[:rows], state[rows, :rows]
 
 
 def _gather_rows(block):

time: 349 us -> 358 us (1.026)
  waiting for transfers between devices: 245 us -> 256 us
  starting transfers between devices: 42.1 us -> 32.1 us
  matrix products: 16.9 us -> 24.7 us
    ppermute x18 -> x12, waiting for transfers between devices: 31.9 us -> 42.4 us  [_swap(): return lax.ppermute(x, axis, [(i, i ^ bit) for i in range(size)])]
    ppermute x18 -> x12, starting transfers between devices: 34.9 us -> 24.8 us  [_swap(): return lax.ppermute(x, axis, [(i, i ^ bit) for i in range(size)])]
    dot_general x2, matrix products: 4.83 us -> 11.6 us  [on_device(): lax.dot_general(weights.astype(jnp.bfloat16), projected, (((0,), (0,)), (...]
  transfers between devices with their start and end apart: 30 -> 24, of which waited for: 27 -> 24; matrix products, arithmetic and copies ran while one was open for 1% -> 0% of each run, Pallas kernels for 0% -> 0%
where the time goes in v8:
time: 358 us; the launch traced here: 357 us
  waiting for transfers between devices  256 us (72%)
  starting transfers between devices  32.1 us (9%)
  matrix products  24.7 us (7%)
  other arithmetic  18.9 us (5%)
  between operations  14.3 us (4%)
  local copies, waits for them, and re-layouts  11.3 us (3%)
    reduce_scatter x2, waiting for transfers between devices, _reduce_rows(): state = lax.psum_scatter(payload, 'z', scatter_dimension=0, tiled=True)  86.8 us
    all_gather x2, waiting for transfers between devices, _gather_rows(): return lax.all_gather(block, 'z', axis=0, tiled=True)  76.6 us
    ppermute x12, waiting for transfers between devices, _swap(): return lax.ppermute(x, axis, [(i, i ^ bit) for i in range(size)])  42.4 us
    ppermute x2, waiting for transfers between devices, _project(): partial = keep + lax.ppermute(send, axis, [(0, 1), (1, 0)])  28 us
    ppermute x12, starting transfers between devices, _swap(): return lax.ppermute(x, axis, [(i, i ^ bit) for i in range(size)])  24.8 us
    ppermute x2, waiting for transfers between devices, _project(): other = lax.ppermute(block, axis, [(0, 1), (1, 0)])  14.5 us
    dot_general x2, matrix products, on_device(): lax.dot_general(weights.astype(jnp.bfloat16), projected, (((0,), (0,)), (...  11.6 us
    dot_general x2, matrix products, on_device(): lax.dot_general(projected, cent_bf, (((1,), (1,)), ((), ())), preferred_e...  8.62 us
  transfers between devices with their start and end apart: 24, of which 24 were waited for; matrix products, arithmetic and copies ran while one was open for 0% of the time, Pallas kernels for 0%

profile of v8, /device:TPU:2, one launch (start us, length us, event | category | flops | bytes accessed | tf_op | source)
XLA Modules:
  0.0 357.3 jit_solution(16653980036859322819)
XLA Ops:
  8.4 4.5 %fusion.32 = f32[2048,512]{1,0:T(8,128)S(1)} fusion(bf16[2048,1024]{1,0:T(8,128)(2,1)} %param.7, bf16[1024,512]{1,0:T(8,128)(2,1)S(1)} %copy-done), kind=kOutput, calls=%fused_computation.113 | convolution fusion | flops 2147483648 | bytes 9437184 | tf_op jit(solution)/shard_map/dot_general | solution.py:67
  12.9 2.0 copy-done.3
  15.2 4.3 %collective-permute-done = f32[1024,512]{1,0:T(8,128)} collective-permute-done((f32[1024,512]{1,0:T(8,128)S(1)}, f32[1024,512]{1,0:T(8,128)}, u32[]{:S(2)}, u32[]{:S(2)}) %collective-permute-start) | collective-permute-done | bytes 2097184 | tf_op jit(solution)/shard_map/ppermute | solution.py:73
  19.5 2.7 dynamic-slice_add_fusion
  23.2 2.2 collective-permute-start.1
  25.4 23.8 %collective-permute-done.1 = f32[512,512]{1,0:T(8,128)} collective-permute-done((f32[512,512]{1,0:T(8,128)}, f32[512,512]{1,0:T(8,128)}, u32[]{:S(2)}, u32[]{:S(2)}) %collective-permute-start.1) | collective-permute-done | bytes 1048608 | tf_op jit(solution)/shard_map/ppermute | solution.py:73
  49.2 2.2 add_convert_fusion
  51.4 1.7 collective-permute-start.2
  53.1 11.9 %collective-permute-done.2 = bf16[512,512]{1,0:T(8,128)(2,1)S(1)} collective-permute-done((bf16[512,512]{1,0:T(8,128)(2,1)}, bf16[512,512]{1,0:T(8,128)(2,1)S(1)}, u32[]{:S(2)}, u32[]{:S(2)}) %collective-permute-start.2) | collective-permute-done | bytes 524320 | tf_op jit(solution)/shard_map/ppermute | solution.py:76
  65.0 1.6 maximum_select_fusion.1
  66.7 2.6 collective-permute-done.3
  69.3 4.4 %multiply_reduce_fusion.1 = (f32[2048]{0:T(1024)S(1)}, f32[2048,1024]{0,1:T(8,128)S(1)}) fusion(f32[1024,512]{1,0:T(8,128)} %param.9, bf16[1024,512]{1,0:T(8,128)(2,1)S(1)} %collective-permute-done.3, bf16[1024,512]{1,0:T(8,128)(2,1)S(1)} %maximum_select_fusion.1, pred[]{:T(512)S(6)} %eq.25), kind=kOutput, calls=%fused_computation.9 | convolution fusion | flops 2161637376 | bytes 12591105 | tf_op jit(solution)/shard_map/dot_general | solution.py:107
  76.5 1.7 collective-permute-start.5
  78.2 2.3 collective-permute-done.5
  80.6 1.5 fusion
  82.1 5.8 %fusion.6 = f32[1024,512]{1,0:T(8,128)S(1)} fusion(f32[2048,1024]{0,1:T(8,128)} %copy-done.2, f32[2048]{0:T(1024)S(1)} %log_add_fusion.1, bf16[1024,512]{1,0:T(8,128)(2,1)S(1)} %collective-permute-done.3, bf16[1024,512]{1,0:T(8,128)(2,1)S(1)} %maximum_select_fusion.1, pred[]{:T(512)S(6)} %eq.25), kind=kOutput, calls=%fused_computation.11 | convolution fusion | flops 2163212288 | bytes 12591105 | tf_op jit(solution)/shard_map/dot_general | solution.py:115
  88.0 1.6 select_maximum_fusion.1
  89.6 45.1 %reduce-scatter.3.cloned.1.call-done = f32[136,512]{1,0:T(8,128)} async-done(((f32[1088,512]{1,0:T(8,128)}), f32[136,512]{1,0:T(8,128)}) %reduce-scatter.3.cloned.1.call-update) | async-done | bytes 278544 | tf_op jit(solution)/shard_map/reduce_scatter | solution.py:35
  136.5 1.7 collective-permute-start.6
  138.2 4.4 %collective-permute-done.6 = f32[68,512]{1,0:T(8,128)S(1)} collective-permute-done((f32[68,512]{1,0:T(8,128)S(1)}, f32[68,512]{1,0:T(8,128)S(1)}, u32[]{:S(2)}, u32[]{:S(2)}) %collective-permute-start.6) | collective-permute-done | bytes 139296 | tf_op jit(solution)/shard_map/ppermute | solution.py:18
  142.7 2.7 collective-permute-start.7
  145.4 3.4 collective-permute-done.7
  148.8 2.2 collective-permute-start.8
  151.1 3.5 collective-permute-done.8
  155.4 2.2 collective-permute-start.9
  157.6 3.1 collective-permute-done.9
  160.7 2.7 collective-permute-start.10
  163.3 2.8 collective-permute-done.10
  166.2 1.7 collective-permute-start.11
  167.9 2.7 collective-permute-done.11
  171.3 37.3 %all-gather.3.cloned.1.call-done = bf16[1024,512]{1,0:T(8,128)(2,1)} async-done(((bf16[128,512]{1,0:T(8,128)(2,1)}), bf16[1024,512]{1,0:T(8,128)(2,1)}) %all-gather.3.cloned.1.call-update) | async-done | bytes 1048592 | tf_op jit(solution)/shard_map/all_gather | solution.py:57
  208.6 4.2 %multiply_reduce_fusion = (f32[2048]{0:T(1024)S(1)}, f32[2048,1024]{0,1:T(8,128)S(1)}) fusion(bf16[1024,512]{1,0:T(8,128)(2,1)} %all-gather.3.cloned.1.call-done, bf16[1024,512]{1,0:T(8,128)(2,1)} %copy-done.5, bf16[1024,512]{1,0:T(8,128)(2,1)S(1)} %maximum_select_fusion.1, pred[]{:T(512)S(6)} %eq.25), kind=kOutput, calls=%fused_computation.8 | convolution fusion | flops 2161113088 | bytes 11542529 | tf_op jit(solution)/shard_map/dot_general | solution.py:107
  216.6 3.2 collective-permute-done.13
  221.4 5.8 %fusion.4 = f32[1024,512]{1,0:T(8,128)S(1)} fusion(f32[2048,1024]{0,1:T(8,128)} %copy-done.1, f32[2048]{0:T(1024)S(1)} %log_add_fusion, bf16[1024,512]{1,0:T(8,128)(2,1)S(1)} %copy-done.6, bf16[1024,512]{1,0:T(8,128)(2,1)S(1)} %maximum_select_fusion.1, pred[]{:T(512)S(6)} %eq.25), kind=kOutput, calls=%fused_computation.10 | convolution fusion | flops 2163212288 | bytes 12591105 | tf_op jit(solution)/shard_map/dot_general | solution.py:115
  227.2 1.6 select_maximum_fusion
  228.9 41.7 %reduce-scatter.5.cloned.1.call-done = f32[136,512]{1,0:T(8,128)} async-done(((f32[1088,512]{1,0:T(8,128)}), f32[136,512]{1,0:T(8,128)}) %reduce-scatter.5.cloned.1.call-update) | async-done | bytes 278544 | tf_op jit(solution)/shard_map/reduce_scatter | solution.py:35
  273.7 4.7 %collective-permute-done.14 = f32[68,512]{1,0:T(8,128)S(1)} collective-permute-done((f32[68,512]{1,0:T(8,128)S(1)}, f32[68,512]{1,0:T(8,128)S(1)}, u32[]{:S(2)}, u32[]{:S(2)}) %collective-permute-start.14) | collective-permute-done | bytes 139296 | tf_op jit(solution)/shard_map/ppermute | solution.py:18
  278.5 2.5 collective-permute-start.15
  281.0 3.6 %collective-permute-done.15 = f32[34,512]{1,0:T(8,128)S(1)} collective-permute-done((f32[34,512]{1,0:T(8,128)S(1)}, f32[34,512]{1,0:T(8,128)S(1)}, u32[]{:S(2)}, u32[]{:S(2)}) %collective-permute-start.15) | collective-permute-done | bytes 69664 | tf_op jit(solution)/shard_map/ppermute | solution.py:18
  284.6 2.0 collective-permute-start.16
  286.6 3.7 %collective-permute-done.16 = f32[17,512]{1,0:T(8,128)S(1)} collective-permute-done((f32[17,512]{1,0:T(8,128)S(1)}, f32[17,512]{1,0:T(8,128)S(1)}, u32[]{:S(2)}, u32[]{:S(2)}) %collective-permute-start.16) | collective-permute-done | bytes 34848 | tf_op jit(solution)/shard_map/ppermute | solution.py:18
  291.2 2.0 collective-permute-start.17
  293.2 3.5 collective-permute-done.17
  296.7 2.5 collective-permute-start.18
  299.2 3.4 collective-permute-done.18
  304.0 3.6 %collective-permute-done.19 = f32[64,512]{1,0:T(8,128)S(1)} collective-permute-done((f32[64,512]{1,0:T(8,128)S(1)}, f32[64,512]{1,0:T(8,128)S(1)}, u32[]{:S(2)}, u32[]{:S(2)}) %collective-permute-start.19) | collective-permute-done | bytes 131104 | tf_op jit(solution)/shard_map/ppermute | solution.py:18
  308.4 39.3 %all-gather.5.cloned.1.call-done = f32[1024,512]{1,0:T(8,128)} async-done(((f32[128,512]{1,0:T(8,128)}), f32[1024,512]{1,0:T(8,128)}) %all-gather.5.cloned.1.call-update) | async-done | bytes 2097168 | tf_op jit(solution)/shard_map/all_gather | solution.py:57
  347.7 3.1 copy.6
  (98 shorter events, 20.7 us)
Async XLA Ops:
  7.2 1.2 copy-start
  7.2 127.5 %reduce-scatter.3.cloned.1.call-start = ((), (), s32[]{:S(2)}) async-start(), calls=%async_computation.2 | async-start | bytes 2506752 | tf_op jit(solution)/shard_map/reduce_scatter | solution.py:35
  12.9 2.0 copy-start.3
  15.1 4.4 %collective-permute-start = (f32[1024,512]{1,0:T(8,128)S(1)}, f32[1024,512]{1,0:T(8,128)}, u32[]{:S(2)}, u32[]{:S(2)}) collective-permute-start(f32[1024,512]{1,0:T(8,128)S(1)} %constant_dynamic-slice_fusion.25), channel_id=1, source_target_pairs={{0,1},{1,0},{2,3},{3,2},{4,5},{5,4},{6,7},{7,6},{8,9},{9,8},{10,11... | collective-permute-start | bytes 6291464 | tf_op jit(solution)/shard_map/ppermute | solution.py:73
  23.2 26.0 %collective-permute-start.1 = (f32[512,512]{1,0:T(8,128)}, f32[512,512]{1,0:T(8,128)}, u32[]{:S(2)}, u32[]{:S(2)}) collective-permute-start(f32[512,512]{1,0:T(8,128)} %constant_dynamic-slice_fusion.24), channel_id=1, source_target_pairs={{0,2},{2,0},{1,3},{3,1},{4,6},{6,4},{5,7},{7,5},{8,10},{10,8},{9,1... | collective-permute-start | bytes 3145736 | tf_op jit(solution)/shard_map/ppermute | solution.py:73
  51.4 13.6 %collective-permute-start.2 = (bf16[512,512]{1,0:T(8,128)(2,1)}, bf16[512,512]{1,0:T(8,128)(2,1)S(1)}, u32[]{:S(2)}, u32[]{:S(2)}) collective-permute-start(bf16[512,512]{1,0:T(8,128)(2,1)} %add_convert_fusion), channel_id=1, source_target_pairs={{0,2},{2,0},{1,3},{3,1},{4,6},{6,4},{5,7},{7,5},{8,10},{10,8},{9,1... | collective-permute-start | bytes 1572872 | tf_op jit(solution)/shard_map/ppermute | solution.py:76
  66.6 2.7 collective-permute-start.3
  69.3 12.8 %copy-start.5 = (bf16[1024,512]{1,0:T(8,128)(2,1)}, bf16[1024,512]{1,0:T(8,128)(2,1)S(1)}, u32[]{:S(2)}) copy-start(bf16[1024,512]{1,0:T(8,128)(2,1)S(1)} %collective-permute-done.3) | copy-start | bytes 3145732
  73.7 6.9 %copy-start.2 = (f32[2048,1024]{0,1:T(8,128)}, f32[2048,1024]{0,1:T(8,128)S(1)}, u32[]{:S(2)}) copy-start(f32[2048,1024]{0,1:T(8,128)S(1)} %get-tuple-element.71) | copy-start | bytes 25165828
  75.1 1.3 collective-permute-start.4
  76.5 4.0 %collective-permute-start.5 = (f32[2,2048]{1,0:T(2,128)S(1)}, f32[2,2048]{1,0:T(2,128)S(1)}, u32[]{:S(2)}, u32[]{:S(2)}) collective-permute-start(f32[2,2048]{1,0:T(2,128)S(1)} %pad_maximum_fusion.7), channel_id=1, source_target_pairs={{0,2},{2,0},{1,3},{3,1},{4,6},{6,4},{5,7},{7,5},{8,10},{10,8},{9,1... | collective-permute-start | bytes 49160 | tf_op jit(solution)/shard_map/ppermute | solution.py:90
  89.5 119.1 %all-gather.3.cloned.1.call-start = ((), (), s32[]{:S(2)}) async-start(), calls=%async_computation.3 | async-start | bytes 1179648 | tf_op jit(solution)/shard_map/all_gather | solution.py:57
  136.5 6.1 %collective-permute-start.6 = (f32[68,512]{1,0:T(8,128)S(1)}, f32[68,512]{1,0:T(8,128)S(1)}, u32[]{:S(2)}, u32[]{:S(2)}) collective-permute-start(f32[68,512]{1,0:T(8,128)S(1)} %pad_maximum_fusion), channel_id=1, source_target_pairs={{0,8},{8,0},{16,24},{24,16},{1,9},{9,1},{17,25},{25,17},{2,10},{10... | collective-permute-start | bytes 417800 | tf_op jit(solution)/shard_map/ppermute | solution.py:18
  142.7 6.0 %collective-permute-start.7 = (f32[34,512]{1,0:T(8,128)S(1)}, f32[34,512]{1,0:T(8,128)S(1)}, u32[]{:S(2)}, u32[]{:S(2)}) collective-permute-start(f32[34,512]{1,0:T(8,128)S(1)} %pad_maximum_fusion.2), channel_id=1, source_target_pairs={{0,16},{8,24},{16,0},{24,8},{1,17},{9,25},{17,1},{25,9},{2,18},{10... | collective-permute-start | bytes 208904 | tf_op jit(solution)/shard_map/ppermute | solution.py:18
  148.8 5.7 %collective-permute-start.8 = (f32[17,512]{1,0:T(8,128)S(1)}, f32[17,512]{1,0:T(8,128)S(1)}, u32[]{:S(2)}, u32[]{:S(2)}) collective-permute-start(f32[17,512]{1,0:T(8,128)S(1)} %pad_maximum_fusion.4), channel_id=1, source_target_pairs={{0,4},{4,0},{1,5},{5,1},{2,6},{6,2},{3,7},{7,3},{8,12},{12,8},{9,1... | collective-permute-start | bytes 104456 | tf_op jit(solution)/shard_map/ppermute | solution.py:18
  155.4 5.3 %collective-permute-start.9 = (bf16[16,512]{1,0:T(8,128)(2,1)S(1)}, bf16[16,512]{1,0:T(8,128)(2,1)S(1)}, u32[]{:S(2)}, u32[]{:S(2)}) collective-permute-start(bf16[16,512]{1,0:T(8,128)(2,1)S(1)} %fusion.26), channel_id=1, source_target_pairs={{0,4},{4,0},{1,5},{5,1},{2,6},{6,2},{3,7},{7,3},{8,12},{12,8},{9,1... | collective-permute-start | bytes 49160 | tf_op jit(solution)/shard_map/ppermute | solution.py:18
  160.7 5.5 %collective-permute-start.10 = (bf16[32,512]{1,0:T(8,128)(2,1)S(1)}, bf16[32,512]{1,0:T(8,128)(2,1)S(1)}, u32[]{:S(2)}, u32[]{:S(2)}) collective-permute-start(bf16[32,512]{1,0:T(8,128)(2,1)S(1)} %maximum_select_fusion.7), channel_id=1, source_target_pairs={{0,16},{8,24},{16,0},{24,8},{1,17},{9,25},{17,1},{25,9},{2,18},{10... | collective-permute-start | bytes 98312 | tf_op jit(solution)/shard_map/ppermute | solution.py:18
  166.2 4.4 %collective-permute-start.11 = (bf16[64,512]{1,0:T(8,128)(2,1)S(1)}, bf16[64,512]{1,0:T(8,128)(2,1)S(1)}, u32[]{:S(2)}, u32[]{:S(2)}) collective-permute-start(bf16[64,512]{1,0:T(8,128)(2,1)S(1)} %maximum_select_fusion.5), channel_id=1, source_target_pairs={{0,8},{8,0},{16,24},{24,16},{1,9},{9,1},{17,25},{25,17},{2,10},{10... | collective-permute-start | bytes 196616 | tf_op jit(solution)/shard_map/ppermute | solution.py:18
  171.3 99.3 %reduce-scatter.5.cloned.1.call-start = ((), (), s32[]{:S(2)}) async-start(), calls=%async_computation.4 | async-start | bytes 2506752 | tf_op jit(solution)/shard_map/reduce_scatter | solution.py:35
  212.9 7.0 %copy-start.1 = (f32[2048,1024]{0,1:T(8,128)}, f32[2048,1024]{0,1:T(8,128)S(1)}, u32[]{:S(2)}) copy-start(f32[2048,1024]{0,1:T(8,128)S(1)} %get-tuple-element.73) | copy-start | bytes 25165828
  214.3 1.5 collective-permute-start.12
  215.9 3.8 %collective-permute-start.13 = (f32[2,2048]{1,0:T(2,128)S(1)}, f32[2,2048]{1,0:T(2,128)S(1)}, u32[]{:S(2)}, u32[]{:S(2)}) collective-permute-start(f32[2,2048]{1,0:T(2,128)S(1)} %pad_maximum_fusion.9), channel_id=1, source_target_pairs={{0,2},{2,0},{1,3},{3,1},{4,6},{6,4},{5,7},{7,5},{8,10},{10,8},{9,1... | collective-permute-start | bytes 49160 | tf_op jit(solution)/shard_map/ppermute | solution.py:90
  219.8 1.6 copy-start.4
  219.9 1.6 copy-start.6
  228.8 118.9 %all-gather.5.cloned.1.call-start = ((), (), s32[]{:S(2)}) async-start(), calls=%async_computation.5 | async-start | bytes 2359296 | tf_op jit(solution)/shard_map/all_gather | solution.py:57
  272.3 6.1 %collective-permute-start.14 = (f32[68,512]{1,0:T(8,128)S(1)}, f32[68,512]{1,0:T(8,128)S(1)}, u32[]{:S(2)}, u32[]{:S(2)}) collective-permute-start(f32[68,512]{1,0:T(8,128)S(1)} %pad_maximum_fusion.1), channel_id=1, source_target_pairs={{0,8},{8,0},{16,24},{24,16},{1,9},{9,1},{17,25},{25,17},{2,10},{10... | collective-permute-start | bytes 417800 | tf_op jit(solution)/shard_map/ppermute | solution.py:18
  278.5 6.0 %collective-permute-start.15 = (f32[34,512]{1,0:T(8,128)S(1)}, f32[34,512]{1,0:T(8,128)S(1)}, u32[]{:S(2)}, u32[]{:S(2)}) collective-permute-start(f32[34,512]{1,0:T(8,128)S(1)} %pad_maximum_fusion.3), channel_id=1, source_target_pairs={{0,16},{8,24},{16,0},{24,8},{1,17},{9,25},{17,1},{25,9},{2,18},{10... | collective-permute-start | bytes 208904 | tf_op jit(solution)/shard_map/ppermute | solution.py:18
  284.6 5.7 %collective-permute-start.16 = (f32[17,512]{1,0:T(8,128)S(1)}, f32[17,512]{1,0:T(8,128)S(1)}, u32[]{:S(2)}, u32[]{:S(2)}) collective-permute-start(f32[17,512]{1,0:T(8,128)S(1)} %pad_maximum_fusion.5), channel_id=1, source_target_pairs={{0,4},{4,0},{1,5},{5,1},{2,6},{6,2},{3,7},{7,3},{8,12},{12,8},{9,1... | collective-permute-start | bytes 104456 | tf_op jit(solution)/shard_map/ppermute | solution.py:18
  291.2 5.5 %collective-permute-start.17 = (f32[16,512]{1,0:T(8,128)S(1)}, f32[16,512]{1,0:T(8,128)S(1)}, u32[]{:S(2)}, u32[]{:S(2)}) collective-permute-start(f32[16,512]{1,0:T(8,128)S(1)} %fusion.14), channel_id=1, source_target_pairs={{0,4},{4,0},{1,5},{5,1},{2,6},{6,2},{3,7},{7,3},{8,12},{12,8},{9,1... | collective-permute-start | bytes 98312 | tf_op jit(solution)/shard_map/ppermute | solution.py:18
  296.7 5.9 %collective-permute-start.18 = (f32[32,512]{1,0:T(8,128)S(1)}, f32[32,512]{1,0:T(8,128)S(1)}, u32[]{:S(2)}, u32[]{:S(2)}) collective-permute-start(f32[32,512]{1,0:T(8,128)S(1)} %maximum_select_fusion.6), channel_id=1, source_target_pairs={{0,16},{8,24},{16,0},{24,8},{1,17},{9,25},{17,1},{25,9},{2,18},{10... | collective-permute-start | bytes 196616 | tf_op jit(solution)/shard_map/ppermute | solution.py:18
  302.6 5.1 %collective-permute-start.19 = (f32[64,512]{1,0:T(8,128)S(1)}, f32[64,512]{1,0:T(8,128)S(1)}, u32[]{:S(2)}, u32[]{:S(2)}) collective-permute-start(f32[64,512]{1,0:T(8,128)S(1)} %maximum_select_fusion.4), channel_id=1, source_target_pairs={{0,8},{8,0},{16,24},{24,16},{1,9},{9,1},{17,25},{25,17},{2,10},{10... | collective-permute-start | bytes 393224 | tf_op jit(solution)/shard_map/ppermute | solution.py:18
Sparse Core Ops, SparseCore 0:
  89.7 45.0 reduce-scatter.2
  171.4 37.2 all-gather.2
  228.9 41.5 reduce-scatter.4
  308.5 39.1 all-gather.4

commit v9 on v7

--- a/solution.py
+++ b/solution.py
@@ -20,7 +20,7 @@
 
 def _bits():
     y = lax.axis_index("y")
-    return ((y & 1, "y", 1), ((y >> 1) & 1, "y", 2), (lax.axis_index("xh"), "xh", 1))
+    return (((y >> 1) & 1, "y", 2), (y & 1, "y", 1), (lax.axis_index("xh"), "xh", 1))
 
 
 def _reduce_rows(numer, mass):
@@ -44,16 +44,15 @@
 
 
 def _gather_rows(block):
-    for bit, axis, mask in reversed(_bits()):
-        other = _swap(block, axis, mask)
-        block = jnp.where(bit == 0, jnp.concatenate([block, other]), jnp.concatenate([other, block]))
-    return lax.all_gather(block, "z", axis=0, tiled=True)
+    bit, axis, mask = _bits()[-1]
+    other = _swap(block, axis, mask)
+    block = jnp.where(bit == 0, jnp.concatenate([block, other]), jnp.concatenate([other, block]))
+    return lax.all_gather(block, ("z", "y"), axis=0, tiled=True)
 
 
 def _row_offset(count):
-    y = lax.axis_index("y")
     per = count // 64
-    return lax.axis_index("z") * (count // 8) + (y & 1) * (4 * per) + ((y >> 1) & 1) * (2 * per) + lax.axis_index("xh") * per
+    return (lax.axis_index("z") * 4 + lax.axis_index("y")) * (2 * per) + lax.axis_index("xh") * per
 
 
 def _project(embeddings, basis):

time: 349 us -> 403 us (1.15)
  waiting for transfers between devices: 245 us -> 312 us
  starting transfers between devices: 42.1 us -> 29.9 us
    all_gather x2, waiting for transfers between devices: 76.2 us -> 150 us  [_gather_rows(): return lax.all_gather(block, ('z', 'y'), axis=0, tiled=True)]
    ppermute x18 -> x14, starting transfers between devices: 34.9 us -> 22.6 us  [_swap(): return lax.ppermute(x, axis, [(i, i ^ bit) for i in range(size)])]
    ppermute x18 -> x14, waiting for transfers between devices: 31.9 us -> 26.4 us  [_swap(): return lax.ppermute(x, axis, [(i, i ^ bit) for i in range(size)])]
  transfers between devices with their start and end apart: 30 -> 26, of which waited for: 27 -> 22; matrix products, arithmetic and copies ran while one was open for 1% -> 1% of each run, Pallas kernels for 0% -> 0%
where the time goes in v9:
time: 403 us
  waiting for transfers between devices  312 us (77%)
  starting transfers between devices  29.9 us (7%)
  other arithmetic  18.3 us (5%)
  matrix products  16.9 us (4%)
  between operations  14.1 us (3%)
  local copies, waits for them, and re-layouts  11.3 us (3%)
    all_gather x2, waiting for transfers between devices, _gather_rows(): return lax.all_gather(block, ('z', 'y'), axis=0, tiled=True)  150 us
    reduce_scatter x2, waiting for transfers between devices, _reduce_rows(): payload = lax.psum_scatter(payload, 'z', scatter_dimension=0, tiled=True)  85.8 us
    ppermute x2, waiting for transfers between devices, _project(): partial = keep + lax.ppermute(send, axis, [(0, 1), (1, 0)])  28 us
    ppermute x14, waiting for transfers between devices, _swap(): return lax.ppermute(x, axis, [(i, i ^ bit) for i in range(size)])  26.4 us
    ppermute x14, starting transfers between devices, _swap(): return lax.ppermute(x, axis, [(i, i ^ bit) for i in range(size)])  22.6 us
    ppermute x2, waiting for transfers between devices, _project(): other = lax.ppermute(block, axis, [(0, 1), (1, 0)])  14.5 us
  transfers between devices with their start and end apart: 26, of which 22 were waited for; matrix products, arithmetic and copies ran while one was open for 1% of the time, Pallas kernels for 0%

profile of v9, /device:TPU:2, one launch (start us, length us, event | category | flops | bytes accessed | tf_op | source)
XLA Modules:
  0.0 402.8 jit_solution(114333943985074098)
XLA Ops:
  8.4 4.5 %fusion.34 = f32[2048,512]{1,0:T(8,128)S(1)} fusion(bf16[2048,1024]{1,0:T(8,128)(2,1)} %param.7, bf16[1024,512]{1,0:T(8,128)(2,1)S(1)} %copy-done), kind=kOutput, calls=%fused_computation.91 | convolution fusion | flops 2147483648 | bytes 9437184 | tf_op jit(solution)/shard_map/dot_general | solution.py:59
  12.9 1.9 copy-done.1
  15.2 4.3 %collective-permute-done = f32[1024,512]{1,0:T(8,128)} collective-permute-done((f32[1024,512]{1,0:T(8,128)S(1)}, f32[1024,512]{1,0:T(8,128)}, u32[]{:S(2)}, u32[]{:S(2)}) %collective-permute-start) | collective-permute-done | bytes 2097184 | tf_op jit(solution)/shard_map/ppermute | solution.py:65
  19.4 2.7 dynamic-slice_add_fusion
  23.2 2.2 collective-permute-start.1
  25.4 23.8 %collective-permute-done.1 = f32[512,512]{1,0:T(8,128)} collective-permute-done((f32[512,512]{1,0:T(8,128)}, f32[512,512]{1,0:T(8,128)}, u32[]{:S(2)}, u32[]{:S(2)}) %collective-permute-start.1) | collective-permute-done | bytes 1048608 | tf_op jit(solution)/shard_map/ppermute | solution.py:65
  49.2 2.2 add_convert_fusion
  51.4 1.7 collective-permute-start.2
  53.1 11.9 %collective-permute-done.2 = bf16[512,512]{1,0:T(8,128)(2,1)S(1)} collective-permute-done((bf16[512,512]{1,0:T(8,128)(2,1)}, bf16[512,512]{1,0:T(8,128)(2,1)S(1)}, u32[]{:S(2)}, u32[]{:S(2)}) %collective-permute-start.2) | collective-permute-done | bytes 524320 | tf_op jit(solution)/shard_map/ppermute | solution.py:68
  65.0 1.6 maximum_select_fusion.1
  66.6 2.6 collective-permute-done.3
  69.3 4.0 multiply_reduce_fusion.1
  73.3 1.4 exponential_reduce_fusion.1
  76.1 1.7 collective-permute-start.5
  77.8 2.3 collective-permute-done.5
  80.2 1.4 fusion
  81.6 2.4 fusion.6
  84.0 1.6 select_maximum_fusion.1
  85.7 45.1 %reduce-scatter.3.cloned.1.call-done = f32[136,512]{1,0:T(8,128)} async-done(((f32[1088,512]{1,0:T(8,128)}), f32[136,512]{1,0:T(8,128)}) %reduce-scatter.3.cloned.1.call-update) | async-done | bytes 278544 | tf_op jit(solution)/shard_map/reduce_scatter | solution.py:33
  131.6 3.3 collective-permute-start.9
  136.8 1.5 collective-permute-start.10
  138.3 4.1 %collective-permute-done.6 = f32[64,512]{1,0:T(8,128)S(1)} collective-permute-done((f32[64,512]{1,0:T(8,128)S(1)}, f32[64,512]{1,0:T(8,128)S(1)}, u32[]{:S(2)}, u32[]{:S(2)}) %collective-permute-start.6) | collective-permute-done | bytes 131104 | tf_op jit(solution)/shard_map/ppermute | solution.py:18
  143.1 2.0 collective-permute-start.11
  145.2 1.6 collective-permute-done.7
  146.8 1.9 collective-permute-start.8
  148.8 3.5 collective-permute-done.8
  153.2 1.9 collective-permute-start.12
  155.0 3.4 collective-permute-done.12
  159.2 74.1 %all-gather.3.cloned.1.call-done = bf16[1024,512]{1,0:T(8,128)(2,1)} async-done(((bf16[32,512]{1,0:T(8,128)(2,1)}), bf16[1024,512]{1,0:T(8,128)(2,1)}) %all-gather.3.cloned.1.call-update) | async-done | bytes 1048592 | tf_op jit(solution)/shard_map/all_gather | solution.py:50
  233.2 3.6 multiply_reduce_fusion
  236.8 1.4 exponential_reduce_fusion
  238.6 1.2 collective-permute-done.13
  240.5 3.2 collective-permute-done.14
  243.8 1.5 fusion.2
  245.3 2.4 fusion.4
  247.7 1.6 select_maximum_fusion
  249.3 40.7 %reduce-scatter.5.cloned.1.call-done = f32[136,512]{1,0:T(8,128)} async-done(((f32[1088,512]{1,0:T(8,128)}), f32[136,512]{1,0:T(8,128)}) %reduce-scatter.5.cloned.1.call-update) | async-done | bytes 278544 | tf_op jit(solution)/shard_map/reduce_scatter | solution.py:33
  290.8 3.0 collective-permute-start.18
  296.0 1.2 collective-permute-start.19
  297.2 4.2 %collective-permute-done.15 = f32[64,512]{1,0:T(8,128)S(1)} collective-permute-done((f32[64,512]{1,0:T(8,128)S(1)}, f32[64,512]{1,0:T(8,128)S(1)}, u32[]{:S(2)}, u32[]{:S(2)}) %collective-permute-start.15) | collective-permute-done | bytes 131104 | tf_op jit(solution)/shard_map/ppermute | solution.py:18
  301.9 2.1 collective-permute-start.20
  304.0 1.8 collective-permute-done.16
  305.8 2.0 collective-permute-start.17
  307.9 3.4 collective-permute-done.17
  311.4 2.0 collective-permute-start.21
  313.3 3.5 collective-permute-done.21
  317.5 75.8 %all-gather.5.cloned.1.call-done = f32[1024,512]{1,0:T(8,128)} async-done(((f32[32,512]{1,0:T(8,128)}), f32[1024,512]{1,0:T(8,128)}) %all-gather.5.cloned.1.call-update) | async-done | bytes 2097168 | tf_op jit(solution)/shard_map/all_gather | solution.py:50
  393.2 3.1 copy.6
  (76 shorter events, 14.6 us)
Async XLA Ops:
  7.2 1.2 copy-start
  7.2 123.6 %reduce-scatter.3.cloned.1.call-start = ((), (), s32[]{:S(2)}) async-start(), calls=%async_computation.2 | async-start | bytes 2506752 | tf_op jit(solution)/shard_map/reduce_scatter | solution.py:33
  12.9 1.9 copy-start.1
  15.0 4.4 %collective-permute-start = (f32[1024,512]{1,0:T(8,128)S(1)}, f32[1024,512]{1,0:T(8,128)}, u32[]{:S(2)}, u32[]{:S(2)}) collective-permute-start(f32[1024,512]{1,0:T(8,128)S(1)} %constant_dynamic-slice_fusion.11), channel_id=1, source_target_pairs={{0,1},{1,0},{2,3},{3,2},{4,5},{5,4},{6,7},{7,6},{8,9},{9,8},{10,11... | collective-permute-start | bytes 6291464 | tf_op jit(solution)/shard_map/ppermute | solution.py:65
  23.2 26.0 %collective-permute-start.1 = (f32[512,512]{1,0:T(8,128)}, f32[512,512]{1,0:T(8,128)}, u32[]{:S(2)}, u32[]{:S(2)}) collective-permute-start(f32[512,512]{1,0:T(8,128)} %constant_dynamic-slice_fusion.10), channel_id=1, source_target_pairs={{0,2},{2,0},{1,3},{3,1},{4,6},{6,4},{5,7},{7,5},{8,10},{10,8},{9,1... | collective-permute-start | bytes 3145736 | tf_op jit(solution)/shard_map/ppermute | solution.py:65
  51.4 13.6 %collective-permute-start.2 = (bf16[512,512]{1,0:T(8,128)(2,1)}, bf16[512,512]{1,0:T(8,128)(2,1)S(1)}, u32[]{:S(2)}, u32[]{:S(2)}) collective-permute-start(bf16[512,512]{1,0:T(8,128)(2,1)} %add_convert_fusion), channel_id=1, source_target_pairs={{0,2},{2,0},{1,3},{3,1},{4,6},{6,4},{5,7},{7,5},{8,10},{10,8},{9,1... | collective-permute-start | bytes 1572872 | tf_op jit(solution)/shard_map/ppermute | solution.py:68
  66.5 2.7 collective-permute-start.3
  74.7 1.3 collective-permute-start.4
  76.1 4.0 collective-permute-start.5
  85.6 147.6 %all-gather.3.cloned.1.call-start = ((), (), s32[]{:S(2)}) async-start(), calls=%async_computation.3 | async-start | bytes 1081344 | tf_op jit(solution)/shard_map/all_gather | solution.py:50
  131.6 5.1 %collective-permute-start.9 = (f32[64]{0:T(128)S(1)}, f32[64]{0:T(128)S(1)}, u32[]{:S(2)}, u32[]{:S(2)}) collective-permute-start(f32[64]{0:T(128)S(1)} %fusion.23), channel_id=1, source_target_pairs={{0,16},{8,24},{16,0},{24,8},{1,17},{9,25},{17,1},{25,9},{2,18},{10... | collective-permute-start | bytes 776 | tf_op jit(solution)/shard_map/ppermute | solution.py:18
  135.8 6.6 %collective-permute-start.6 = (f32[64,512]{1,0:T(8,128)S(1)}, f32[64,512]{1,0:T(8,128)S(1)}, u32[]{:S(2)}, u32[]{:S(2)}) collective-permute-start(f32[64,512]{1,0:T(8,128)S(1)} %constant_dynamic-slice_fusion.9), channel_id=1, source_target_pairs={{0,16},{8,24},{16,0},{24,8},{1,17},{9,25},{17,1},{25,9},{2,18},{10... | collective-permute-start | bytes 393224 | tf_op jit(solution)/shard_map/ppermute | solution.py:18
  136.8 6.2 %collective-permute-start.10 = (f32[32]{0:T(128)S(1)}, f32[32]{0:T(128)S(1)}, u32[]{:S(2)}, u32[]{:S(2)}) collective-permute-start(f32[32]{0:T(128)S(1)} %dynamic_slice.111), channel_id=1, source_target_pairs={{0,8},{8,0},{16,24},{24,16},{1,9},{9,1},{17,25},{25,17},{2,10},{10... | collective-permute-start | bytes 392 | tf_op jit(solution)/shard_map/ppermute | solution.py:18
  142.4 4.4 %collective-permute-start.7 = (f32[32,512]{1,0:T(8,128)S(1)}, f32[32,512]{1,0:T(8,128)S(1)}, u32[]{:S(2)}, u32[]{:S(2)}) collective-permute-start(f32[32,512]{1,0:T(8,128)S(1)} %constant_dynamic-slice_fusion.8), channel_id=1, source_target_pairs={{0,8},{8,0},{16,24},{24,16},{1,9},{9,1},{17,25},{25,17},{2,10},{10... | collective-permute-start | bytes 196616 | tf_op jit(solution)/shard_map/ppermute | solution.py:18
  143.1 5.6 %collective-permute-start.11 = (f32[16]{0:T(128)S(1)}, f32[16]{0:T(128)S(1)}, u32[]{:S(2)}, u32[]{:S(2)}) collective-permute-start(f32[16]{0:T(128)S(1)} %dynamic_slice.113), channel_id=1, source_target_pairs={{0,4},{4,0},{1,5},{5,1},{2,6},{6,2},{3,7},{7,3},{8,12},{12,8},{9,1... | collective-permute-start | bytes 200 | tf_op jit(solution)/shard_map/ppermute | solution.py:18
  146.8 5.5 %collective-permute-start.8 = (f32[16,512]{1,0:T(8,128)S(1)}, f32[16,512]{1,0:T(8,128)S(1)}, u32[]{:S(2)}, u32[]{:S(2)}) collective-permute-start(f32[16,512]{1,0:T(8,128)S(1)} %constant_dynamic-slice_fusion.6), channel_id=1, source_target_pairs={{0,4},{4,0},{1,5},{5,1},{2,6},{6,2},{3,7},{7,3},{8,12},{12,8},{9,1... | collective-permute-start | bytes 98312 | tf_op jit(solution)/shard_map/ppermute | solution.py:18
  153.2 5.3 %collective-permute-start.12 = (bf16[16,512]{1,0:T(8,128)(2,1)S(1)}, bf16[16,512]{1,0:T(8,128)(2,1)S(1)}, u32[]{:S(2)}, u32[]{:S(2)}) collective-permute-start(bf16[16,512]{1,0:T(8,128)(2,1)S(1)} %get-tuple-element.28), channel_id=1, source_target_pairs={{0,4},{4,0},{1,5},{5,1},{2,6},{6,2},{3,7},{7,3},{8,12},{12,8},{9,1... | collective-permute-start | bytes 49160 | tf_op jit(solution)/shard_map/ppermute | solution.py:18
  159.1 130.9 %reduce-scatter.5.cloned.1.call-start = ((), (), s32[]{:S(2)}) async-start(), calls=%async_computation.4 | async-start | bytes 2506752 | tf_op jit(solution)/shard_map/reduce_scatter | solution.py:33
  238.3 1.5 collective-permute-start.13
  239.9 3.8 collective-permute-start.14
  243.8 1.5 copy-start.2
  249.3 144.0 %all-gather.5.cloned.1.call-start = ((), (), s32[]{:S(2)}) async-start(), calls=%async_computation.5 | async-start | bytes 2162688 | tf_op jit(solution)/shard_map/all_gather | solution.py:50
  290.8 5.1 %collective-permute-start.18 = (f32[64]{0:T(128)S(1)}, f32[64]{0:T(128)S(1)}, u32[]{:S(2)}, u32[]{:S(2)}) collective-permute-start(f32[64]{0:T(128)S(1)} %fusion.20), channel_id=1, source_target_pairs={{0,16},{8,24},{16,0},{24,8},{1,17},{9,25},{17,1},{25,9},{2,18},{10... | collective-permute-start | bytes 776 | tf_op jit(solution)/shard_map/ppermute | solution.py:18
  294.8 6.6 %collective-permute-start.15 = (f32[64,512]{1,0:T(8,128)S(1)}, f32[64,512]{1,0:T(8,128)S(1)}, u32[]{:S(2)}, u32[]{:S(2)}) collective-permute-start(f32[64,512]{1,0:T(8,128)S(1)} %constant_dynamic-slice_fusion.3), channel_id=1, source_target_pairs={{0,16},{8,24},{16,0},{24,8},{1,17},{9,25},{17,1},{25,9},{2,18},{10... | collective-permute-start | bytes 393224 | tf_op jit(solution)/shard_map/ppermute | solution.py:18
  296.0 5.7 %collective-permute-start.19 = (f32[32]{0:T(128)S(1)}, f32[32]{0:T(128)S(1)}, u32[]{:S(2)}, u32[]{:S(2)}) collective-permute-start(f32[32]{0:T(128)S(1)} %dynamic_slice.125), channel_id=1, source_target_pairs={{0,8},{8,0},{16,24},{24,16},{1,9},{9,1},{17,25},{25,17},{2,10},{10... | collective-permute-start | bytes 392 | tf_op jit(solution)/shard_map/ppermute | solution.py:18
  301.4 4.4 %collective-permute-start.16 = (f32[32,512]{1,0:T(8,128)S(1)}, f32[32,512]{1,0:T(8,128)S(1)}, u32[]{:S(2)}, u32[]{:S(2)}) collective-permute-start(f32[32,512]{1,0:T(8,128)S(1)} %constant_dynamic-slice_fusion.2), channel_id=1, source_target_pairs={{0,8},{8,0},{16,24},{24,16},{1,9},{9,1},{17,25},{25,17},{2,10},{10... | collective-permute-start | bytes 196616 | tf_op jit(solution)/shard_map/ppermute | solution.py:18
  301.9 5.9 %collective-permute-start.20 = (f32[16]{0:T(128)S(1)}, f32[16]{0:T(128)S(1)}, u32[]{:S(2)}, u32[]{:S(2)}) collective-permute-start(f32[16]{0:T(128)S(1)} %dynamic_slice.127), channel_id=1, source_target_pairs={{0,4},{4,0},{1,5},{5,1},{2,6},{6,2},{3,7},{7,3},{8,12},{12,8},{9,1... | collective-permute-start | bytes 200 | tf_op jit(solution)/shard_map/ppermute | solution.py:18
  305.8 5.5 %collective-permute-start.17 = (f32[16,512]{1,0:T(8,128)S(1)}, f32[16,512]{1,0:T(8,128)S(1)}, u32[]{:S(2)}, u32[]{:S(2)}) collective-permute-start(f32[16,512]{1,0:T(8,128)S(1)} %constant_dynamic-slice_fusion.1), channel_id=1, source_target_pairs={{0,4},{4,0},{1,5},{5,1},{2,6},{6,2},{3,7},{7,3},{8,12},{12,8},{9,1... | collective-permute-start | bytes 98312 | tf_op jit(solution)/shard_map/ppermute | solution.py:18
  311.4 5.4 %collective-permute-start.21 = (f32[16,512]{1,0:T(8,128)S(1)}, f32[16,512]{1,0:T(8,128)S(1)}, u32[]{:S(2)}, u32[]{:S(2)}) collective-permute-start(f32[16,512]{1,0:T(8,128)S(1)} %add_divide_fusion), channel_id=1, source_target_pairs={{0,4},{4,0},{1,5},{5,1},{2,6},{6,2},{3,7},{7,3},{8,12},{12,8},{9,1... | collective-permute-start | bytes 98312 | tf_op jit(solution)/shard_map/ppermute | solution.py:18
Sparse Core Ops, SparseCore 0:
  85.7 45.0 reduce-scatter.2
  159.2 73.9 all-gather.2
  249.4 40.5 reduce-scatter.4
  317.6 75.5 all-gather.4

commit v10 on v7

--- a/solution.py
+++ b/solution.py
@@ -93,9 +93,11 @@
     projected = _project(embeddings, basis)
     start = _row_offset(count)
     block = lax.dynamic_slice_in_dim(start_centroids, start, per, axis=0)
-    cent_bf = start_centroids.astype(jnp.bfloat16)
     log_total = jnp.zeros((row_count,), jnp.float32)
-    for step in range(ITERS):
+
+    def one_step(_, carry):
+        block, centroids, log_total = carry
+        cent_bf = centroids.astype(jnp.bfloat16)
         scores = (
             lax.dot_general(
                 projected, cent_bf, (((1,), (1,)), ((), ())), preferred_element_type=jnp.float32
@@ -113,9 +115,9 @@
         )
         numer, mass = _reduce_rows(local_numer, local_mass)
         block = (numer + block) / (mass[:, None] + 1.0)
-        if step + 1 < ITERS:
-            cent_bf = _gather_rows(block.astype(jnp.bfloat16))
-    centroids = _gather_rows(block)
+        return block, _gather_rows(block), log_total
+
+    _, centroids, log_total = lax.fori_loop(0, ITERS, one_step, (block, start_centroids, log_total))
     return (centroids, log_total)
 
 

time: 349 us -> 374 us (1.072)
  other arithmetic: 18.4 us -> 27.4 us
  matrix products: 16.9 us -> 23.9 us
  local copies, waits for them, and re-layouts: 11.3 us -> 17.8 us
    dot_general x4, matrix products: 12.4 us -> 19.4 us  [the longest x2 11.4 us: one_step(): lax.dot_general(weights.astype(jnp.bfloat16), projected, (((0,), (0,)), (...]
    reduce_sum x2, other arithmetic: 2.89 us -> 9.63 us  [one_step(): local_mass = jnp.sum(weights, axis=0)]
    unnamed x7 -> x8, local copies, waits for them, and re-layouts: 6.21 us -> 8.27 us
where the time goes in v10:
time: 374 us
  waiting for transfers between devices  248 us (66%)
  starting transfers between devices  42.1 us (11%)
  other arithmetic  27.4 us (7%)
  matrix products  23.9 us (6%)
  local copies, waits for them, and re-layouts  17.8 us (5%)
  between operations  13.8 us (4%)
    reduce_scatter x2, waiting for transfers between devices, _reduce_rows(): payload = lax.psum_scatter(payload, 'z', scatter_dimension=0, tiled=True)  87.1 us
    all_gather x2, waiting for transfers between devices, _gather_rows(): return lax.all_gather(block, 'z', axis=0, tiled=True)  78.7 us
    ppermute x18, starting transfers between devices, _swap(): return lax.ppermute(x, axis, [(i, i ^ bit) for i in range(size)])  35.3 us
    ppermute x18, waiting for transfers between devices, _swap(): return lax.ppermute(x, axis, [(i, i ^ bit) for i in range(size)])  32.7 us
    ppermute x2, waiting for transfers between devices, _project(): partial = keep + lax.ppermute(send, axis, [(0, 1), (1, 0)])  28 us
    ppermute x2, waiting for transfers between devices, _project(): other = lax.ppermute(block, axis, [(0, 1), (1, 0)])  13.8 us
    dot_general x2, matrix products, one_step(): lax.dot_general(weights.astype(jnp.bfloat16), projected, (((0,), (0,)), (...  11.4 us
    reduce_sum x2, other arithmetic, one_step(): local_mass = jnp.sum(weights, axis=0)  9.63 us
  transfers between devices with their start and end apart: 30, of which 27 were waited for; matrix products, arithmetic and copies ran while one was open for 1% of the time, Pallas kernels for 0%

profile of v10, /device:TPU:2, one launch (start us, length us, event | category | flops | bytes accessed | tf_op | source)
XLA Modules:
  0.0 373.6 jit_solution(15011631649027141460)
XLA Ops:
  7.2 3.2 copy.19
  10.4 4.5 %fusion.17 = f32[2048,512]{1,0:T(8,128)S(1)} fusion(bf16[2048,1024]{1,0:T(8,128)(2,1)} %param.7, bf16[1024,512]{1,0:T(8,128)(2,1)S(1)} %copy-done), kind=kOutput, calls=%fused_computation.52 | convolution fusion | flops 2147483648 | bytes 9437184 | tf_op jit(solution)/shard_map/dot_general | solution.py:60
  14.9 1.9 copy-done.3
  17.2 4.3 %collective-permute-done.11 = f32[1024,512]{1,0:T(8,128)} collective-permute-done((f32[1024,512]{1,0:T(8,128)S(1)}, f32[1024,512]{1,0:T(8,128)}, u32[]{:S(2)}, u32[]{:S(2)}) %collective-permute-start.11) | collective-permute-done | bytes 2097184 | tf_op jit(solution)/shard_map/ppermute | solution.py:66
  21.4 2.7 dynamic-slice_add_fusion.3
  25.2 2.2 collective-permute-start.12
  27.4 23.8 %collective-permute-done.12 = f32[512,512]{1,0:T(8,128)} collective-permute-done((f32[512,512]{1,0:T(8,128)}, f32[512,512]{1,0:T(8,128)}, u32[]{:S(2)}, u32[]{:S(2)}) %collective-permute-start.12) | collective-permute-done | bytes 1048608 | tf_op jit(solution)/shard_map/ppermute | solution.py:66
  51.2 2.2 add_convert_fusion
  55.1 11.9 %collective-permute-done.13 = bf16[512,512]{1,0:T(8,128)(2,1)S(1)} collective-permute-done((bf16[512,512]{1,0:T(8,128)(2,1)}, bf16[512,512]{1,0:T(8,128)(2,1)S(1)}, u32[]{:S(2)}, u32[]{:S(2)}) %collective-permute-start.13) | collective-permute-done | bytes 524320 | tf_op jit(solution)/shard_map/ppermute | solution.py:69
  69.5 1.9 collective-permute-done.14
  71.4 2.9 maximum_select_fusion.3
  74.3 289.6 %while.17 = (s32[]{:T(128)}, f32[16,512]{1,0:T(8,128)S(1)}, f32[1024,512]{1,0:T(8,128)}, f32[2048]{0:T(1024)}, bf16[2048,512]{1,0:T(8,128)(2,1)S(1)}, /*index=5*...) while((s32[]{:T(128)}, f32[16,512]{1,0:T(8,128)S(1)}, ...), condition=%wide.region_5.6_spmd, body=%wide.region_0.5_spmd.sunk | while | flops 4320703488 | bytes 99449056 | solution.py:120
  74.6 4.0 %multiply_reduce_fusion.2 = (f32[2048]{0:T(1024)S(1)}, f32[2048,1024]{0,1:T(8,128)S(1)}) fusion(bf16[2048,512]{1,0:T(8,128)(2,1)S(1)} %get-tuple-element.188, f32[1024,512]{1,0:T(8,128)} %get-tuple-element.172), kind=kOutput, calls=%fused_computation.4.clone.1 | convolution fusion | flops 2152200192 | bytes 12591104 | tf_op jit(solution)/shard_map/while/body/eval_jaxpr/dot_general | solution.py:102
  80.0 1.8 copy-done.1
  84.7 2.3 collective-permute-done.1
  87.1 5.7 %fusion.37 = f32[1024,512]{1,0:T(8,128)S(1)} fusion(bf16[2048,512]{1,0:T(8,128)(2,1)S(1)} %get-tuple-element.188, f32[2048,1024]{0,1:T(8,128)} %copy-done.1, f32[2048]{0:T(1024)S(1)} %log_add_fusion.2), kind=kOutput, calls=%fused_computation.5.clone.1 | convolution fusion | flops 2153775104 | bytes 12591104 | tf_op jit(solution)/shard_map/while/body/eval_jaxpr/dot_general | solution.py:110
  92.9 4.8 %fusion.36 = f32[1024]{0:T(1024)S(1)} fusion(f32[2048,1024]{0,1:T(8,128)} %copy-done.1, f32[2048]{0:T(1024)S(1)} %log_add_fusion.2), kind=kLoop, calls=%fused_computation.2.clone.1 | loop fusion | flops 6290432 | bytes 8400896 | tf_op jit(solution)/shard_map/while/body/eval_jaxpr/reduce_sum | solution.py:109
  99.4 45.1 %reduce-scatter.2.cloned.1.call-done = f32[136,512]{1,0:T(8,128)} async-done(((f32[1088,512]{1,0:T(8,128)}), f32[136,512]{1,0:T(8,128)}) %reduce-scatter.2.cloned.1.call-update) | async-done | bytes 278544 | tf_op jit(solution)/shard_map/while/body/eval_jaxpr/reduce_scatter | solution.py:33
  145.3 1.8 collective-permute-start.5
  149.0 3.0 collective-permute-start.6
  153.1 2.6 collective-permute-start.3
  155.8 2.5 collective-permute-start.7
  159.0 1.9 collective-permute-start.4
  161.0 3.5 collective-permute-done.4
  164.6 1.8 collective-permute-start.8
  166.4 3.6 collective-permute-done.8
  170.0 2.6 collective-permute-start.9
  172.6 3.3 collective-permute-done.9
  177.0 4.0 %collective-permute-done.10 = f32[64,512]{1,0:T(8,128)S(1)} collective-permute-done((f32[64,512]{1,0:T(8,128)S(1)}, f32[64,512]{1,0:T(8,128)S(1)}, u32[]{:S(2)}, u32[]{:S(2)}) %collective-permute-start.10) | collective-permute-done | bytes 131104 | tf_op jit(solution)/shard_map/while/body/eval_jaxpr/ppermute | solution.py:18
  181.7 39.4 %all-gather.2.cloned.1.call-done = f32[1024,512]{1,0:T(8,128)} async-done(((f32[128,512]{1,0:T(8,128)}), f32[1024,512]{1,0:T(8,128)}) %all-gather.2.cloned.1.call-update) | async-done | bytes 2097168 | tf_op jit(solution)/shard_map/while/body/eval_jaxpr/all_gather | solution.py:50
  221.1 4.0 %multiply_reduce_fusion.2 = (f32[2048]{0:T(1024)S(1)}, f32[2048,1024]{0,1:T(8,128)S(1)}) fusion(bf16[2048,512]{1,0:T(8,128)(2,1)S(1)} %get-tuple-element.188, f32[1024,512]{1,0:T(8,128)} %get-tuple-element.172), kind=kOutput, calls=%fused_computation.4.clone.1 | convolution fusion | flops 2152200192 | bytes 12591104 | tf_op jit(solution)/shard_map/while/body/eval_jaxpr/dot_general | solution.py:102
  226.5 1.8 copy-done.1
  230.3 3.2 collective-permute-done.1
  233.6 5.7 %fusion.37 = f32[1024,512]{1,0:T(8,128)S(1)} fusion(bf16[2048,512]{1,0:T(8,128)(2,1)S(1)} %get-tuple-element.188, f32[2048,1024]{0,1:T(8,128)} %copy-done.1, f32[2048]{0:T(1024)S(1)} %log_add_fusion.2), kind=kOutput, calls=%fused_computation.5.clone.1 | convolution fusion | flops 2153775104 | bytes 12591104 | tf_op jit(solution)/shard_map/while/body/eval_jaxpr/dot_general | solution.py:110
  239.3 4.8 %fusion.36 = f32[1024]{0:T(1024)S(1)} fusion(f32[2048,1024]{0,1:T(8,128)} %copy-done.1, f32[2048]{0:T(1024)S(1)} %log_add_fusion.2), kind=kLoop, calls=%fused_computation.2.clone.1 | loop fusion | flops 6290432 | bytes 8400896 | tf_op jit(solution)/shard_map/while/body/eval_jaxpr/reduce_sum | solution.py:109
  245.8 41.9 %reduce-scatter.2.cloned.1.call-done = f32[136,512]{1,0:T(8,128)} async-done(((f32[1088,512]{1,0:T(8,128)}), f32[136,512]{1,0:T(8,128)}) %reduce-scatter.2.cloned.1.call-update) | async-done | bytes 278544 | tf_op jit(solution)/shard_map/while/body/eval_jaxpr/reduce_scatter | solution.py:33
  292.2 2.9 collective-permute-start.6
  296.0 2.6 collective-permute-start.3
  298.8 2.5 collective-permute-start.7
  301.9 1.9 collective-permute-start.4
  303.9 3.5 collective-permute-done.4
  307.5 1.8 collective-permute-start.8
  309.3 3.6 collective-permute-done.8
  313.0 2.6 collective-permute-start.9
  315.5 3.3 collective-permute-done.9
  320.2 3.7 collective-permute-done.10
  324.7 39.3 %all-gather.2.cloned.1.call-done = f32[1024,512]{1,0:T(8,128)} async-done(((f32[128,512]{1,0:T(8,128)}), f32[1024,512]{1,0:T(8,128)}) %all-gather.2.cloned.1.call-update) | async-done | bytes 2097168 | tf_op jit(solution)/shard_map/while/body/eval_jaxpr/all_gather | solution.py:50
  364.0 3.1 copy.20
  (100 shorter events, 31.9 us)
Async XLA Ops:
  7.2 3.2 copy-start
  14.9 1.9 copy-start.3
  17.0 4.4 %collective-permute-start.11 = (f32[1024,512]{1,0:T(8,128)S(1)}, f32[1024,512]{1,0:T(8,128)}, u32[]{:S(2)}, u32[]{:S(2)}) collective-permute-start(f32[1024,512]{1,0:T(8,128)S(1)} %constant_dynamic-slice_fusion.6), channel_id=1, source_target_pairs={{0,1},{1,0},{2,3},{3,2},{4,5},{5,4},{6,7},{7,6},{8,9},{9,8},{10,11... | collective-permute-start | bytes 6291464 | tf_op jit(solution)/shard_map/ppermute | solution.py:66
  25.2 26.0 %collective-permute-start.12 = (f32[512,512]{1,0:T(8,128)}, f32[512,512]{1,0:T(8,128)}, u32[]{:S(2)}, u32[]{:S(2)}) collective-permute-start(f32[512,512]{1,0:T(8,128)} %constant_dynamic-slice_fusion.5), channel_id=1, source_target_pairs={{0,2},{2,0},{1,3},{3,1},{4,6},{6,4},{5,7},{7,5},{8,10},{10,8},{9,1... | collective-permute-start | bytes 3145736 | tf_op jit(solution)/shard_map/ppermute | solution.py:66
  53.4 13.6 %collective-permute-start.13 = (bf16[512,512]{1,0:T(8,128)(2,1)}, bf16[512,512]{1,0:T(8,128)(2,1)S(1)}, u32[]{:S(2)}, u32[]{:S(2)}) collective-permute-start(bf16[512,512]{1,0:T(8,128)(2,1)} %add_convert_fusion), channel_id=1, source_target_pairs={{0,2},{2,0},{1,3},{3,1},{4,6},{6,4},{5,7},{7,5},{8,10},{10,8},{9,1... | collective-permute-start | bytes 1572872 | tf_op jit(solution)/shard_map/ppermute | solution.py:69
  68.5 1.0 copy-start.2
  68.5 2.9 collective-permute-start.14
  74.5 70.0 %reduce-scatter.2.cloned.1.call-start = ((), (), s32[]{:S(2)}) async-start(), calls=%async_computation.1 | async-start | bytes 2506752 | tf_op jit(solution)/shard_map/while/body/eval_jaxpr/reduce_scatter | solution.py:33
  78.6 3.2 copy-start.1
  81.8 1.3 collective-permute-start
  83.2 3.8 %collective-permute-start.1 = (f32[2,2048]{1,0:T(2,128)S(1)}, f32[2,2048]{1,0:T(2,128)S(1)}, u32[]{:S(2)}, u32[]{:S(2)}) collective-permute-start(f32[2,2048]{1,0:T(2,128)S(1)} %pad_maximum_fusion.5), channel_id=1, source_target_pairs={{0,2},{2,0},{1,3},{3,1},{4,6},{6,4},{5,7},{7,5},{8,10},{10,8},{9,1... | collective-permute-start | bytes 49160 | tf_op jit(solution)/shard_map/while/body/eval_jaxpr/ppermute | solution.py:83
  87.1 5.7 %copy-start.4 = (f32[2048]{0:T(1024)}, f32[2048]{0:T(1024)S(1)}, u32[]{:S(2)}) copy-start(f32[2048]{0:T(1024)S(1)} %log_add_fusion.2) | copy-start | bytes 24580 | tf_op jit(solution)/shard_map/while
  99.3 121.8 %all-gather.2.cloned.1.call-start = ((), (), s32[]{:S(2)}) async-start(), calls=%async_computation.2 | async-start | bytes 2359296 | tf_op jit(solution)/shard_map/while/body/eval_jaxpr/all_gather | solution.py:50
  145.3 3.6 collective-permute-start.5
  148.0 5.1 %collective-permute-start.2 = (f32[64,512]{1,0:T(8,128)S(1)}, f32[64,512]{1,0:T(8,128)S(1)}, u32[]{:S(2)}, u32[]{:S(2)}) collective-permute-start(f32[64,512]{1,0:T(8,128)S(1)} %constant_dynamic-slice_fusion.11), channel_id=1, source_target_pairs={{0,8},{8,0},{16,24},{24,16},{1,9},{9,1},{17,25},{25,17},{2,10},{10... | collective-permute-start | bytes 393224 | tf_op jit(solution)/shard_map/while/body/eval_jaxpr/ppermute | solution.py:18
  149.0 6.7 %collective-permute-start.6 = (f32[32]{0:T(128)S(1)}, f32[32]{0:T(128)S(1)}, u32[]{:S(2)}, u32[]{:S(2)}) collective-permute-start(f32[32]{0:T(128)S(1)} %dynamic_slice.133), channel_id=1, source_target_pairs={{0,16},{8,24},{16,0},{24,8},{1,17},{9,25},{17,1},{25,9},{2,18},{10... | collective-permute-start | bytes 392 | tf_op jit(solution)/shard_map/while/body/eval_jaxpr/ppermute | solution.py:18
  153.1 5.9 %collective-permute-start.3 = (f32[32,512]{1,0:T(8,128)S(1)}, f32[32,512]{1,0:T(8,128)S(1)}, u32[]{:S(2)}, u32[]{:S(2)}) collective-permute-start(f32[32,512]{1,0:T(8,128)S(1)} %constant_dynamic-slice_fusion.12), channel_id=1, source_target_pairs={{0,16},{8,24},{16,0},{24,8},{1,17},{9,25},{17,1},{25,9},{2,18},{10... | collective-permute-start | bytes 196616 | tf_op jit(solution)/shard_map/while/body/eval_jaxpr/ppermute | solution.py:18
  155.8 5.1 %collective-permute-start.7 = (f32[16]{0:T(128)S(1)}, f32[16]{0:T(128)S(1)}, u32[]{:S(2)}, u32[]{:S(2)}) collective-permute-start(f32[16]{0:T(128)S(1)} %dynamic_slice.134), channel_id=1, source_target_pairs={{0,4},{4,0},{1,5},{5,1},{2,6},{6,2},{3,7},{7,3},{8,12},{12,8},{9,1... | collective-permute-start | bytes 200 | tf_op jit(solution)/shard_map/while/body/eval_jaxpr/ppermute | solution.py:18
  159.0 5.5 %collective-permute-start.4 = (f32[16,512]{1,0:T(8,128)S(1)}, f32[16,512]{1,0:T(8,128)S(1)}, u32[]{:S(2)}, u32[]{:S(2)}) collective-permute-start(f32[16,512]{1,0:T(8,128)S(1)} %constant_dynamic-slice_fusion.13), channel_id=1, source_target_pairs={{0,4},{4,0},{1,5},{5,1},{2,6},{6,2},{3,7},{7,3},{8,12},{12,8},{9,1... | collective-permute-start | bytes 98312 | tf_op jit(solution)/shard_map/while/body/eval_jaxpr/ppermute | solution.py:18
  164.6 5.4 %collective-permute-start.8 = (f32[16,512]{1,0:T(8,128)S(1)}, f32[16,512]{1,0:T(8,128)S(1)}, u32[]{:S(2)}, u32[]{:S(2)}) collective-permute-start(f32[16,512]{1,0:T(8,128)S(1)} %add_divide_fusion.2), channel_id=1, source_target_pairs={{0,4},{4,0},{1,5},{5,1},{2,6},{6,2},{3,7},{7,3},{8,12},{12,8},{9,1... | collective-permute-start | bytes 98312 | tf_op jit(solution)/shard_map/while/body/eval_jaxpr/ppermute | solution.py:18
  170.0 5.9 %collective-permute-start.9 = (f32[32,512]{1,0:T(8,128)S(1)}, f32[32,512]{1,0:T(8,128)S(1)}, u32[]{:S(2)}, u32[]{:S(2)}) collective-permute-start(f32[32,512]{1,0:T(8,128)S(1)} %maximum_select_fusion.8), channel_id=1, source_target_pairs={{0,16},{8,24},{16,0},{24,8},{1,17},{9,25},{17,1},{25,9},{2,18},{10... | collective-permute-start | bytes 196616 | tf_op jit(solution)/shard_map/while/body/eval_jaxpr/ppermute | solution.py:18
  175.9 5.1 %collective-permute-start.10 = (f32[64,512]{1,0:T(8,128)S(1)}, f32[64,512]{1,0:T(8,128)S(1)}, u32[]{:S(2)}, u32[]{:S(2)}) collective-permute-start(f32[64,512]{1,0:T(8,128)S(1)} %maximum_select_fusion.9), channel_id=1, source_target_pairs={{0,8},{8,0},{16,24},{24,16},{1,9},{9,1},{17,25},{25,17},{2,10},{10... | collective-permute-start | bytes 393224 | tf_op jit(solution)/shard_map/while/body/eval_jaxpr/ppermute | solution.py:18
  221.1 66.7 %reduce-scatter.2.cloned.1.call-start = ((), (), s32[]{:S(2)}) async-start(), calls=%async_computation.1 | async-start | bytes 2506752 | tf_op jit(solution)/shard_map/while/body/eval_jaxpr/reduce_scatter | solution.py:33
  225.1 3.2 copy-start.1
  228.3 1.3 collective-permute-start
  229.7 3.8 %collective-permute-start.1 = (f32[2,2048]{1,0:T(2,128)S(1)}, f32[2,2048]{1,0:T(2,128)S(1)}, u32[]{:S(2)}, u32[]{:S(2)}) collective-permute-start(f32[2,2048]{1,0:T(2,128)S(1)} %pad_maximum_fusion.5), channel_id=1, source_target_pairs={{0,2},{2,0},{1,3},{3,1},{4,6},{6,4},{5,7},{7,5},{8,10},{10,8},{9,1... | collective-permute-start | bytes 49160 | tf_op jit(solution)/shard_map/while/body/eval_jaxpr/ppermute | solution.py:83
  233.6 5.7 %copy-start.4 = (f32[2048]{0:T(1024)}, f32[2048]{0:T(1024)S(1)}, u32[]{:S(2)}) copy-start(f32[2048]{0:T(1024)S(1)} %log_add_fusion.2) | copy-start | bytes 24580 | tf_op jit(solution)/shard_map/while
  245.8 118.2 %all-gather.2.cloned.1.call-start = ((), (), s32[]{:S(2)}) async-start(), calls=%async_computation.2 | async-start | bytes 2359296 | tf_op jit(solution)/shard_map/while/body/eval_jaxpr/all_gather | solution.py:50
  288.5 3.6 collective-permute-start.5
  290.9 5.1 %collective-permute-start.2 = (f32[64,512]{1,0:T(8,128)S(1)}, f32[64,512]{1,0:T(8,128)S(1)}, u32[]{:S(2)}, u32[]{:S(2)}) collective-permute-start(f32[64,512]{1,0:T(8,128)S(1)} %constant_dynamic-slice_fusion.11), channel_id=1, source_target_pairs={{0,8},{8,0},{16,24},{24,16},{1,9},{9,1},{17,25},{25,17},{2,10},{10... | collective-permute-start | bytes 393224 | tf_op jit(solution)/shard_map/while/body/eval_jaxpr/ppermute | solution.py:18
  292.2 6.4 %collective-permute-start.6 = (f32[32]{0:T(128)S(1)}, f32[32]{0:T(128)S(1)}, u32[]{:S(2)}, u32[]{:S(2)}) collective-permute-start(f32[32]{0:T(128)S(1)} %dynamic_slice.133), channel_id=1, source_target_pairs={{0,16},{8,24},{16,0},{24,8},{1,17},{9,25},{17,1},{25,9},{2,18},{10... | collective-permute-start | bytes 392 | tf_op jit(solution)/shard_map/while/body/eval_jaxpr/ppermute | solution.py:18
  296.0 5.9 %collective-permute-start.3 = (f32[32,512]{1,0:T(8,128)S(1)}, f32[32,512]{1,0:T(8,128)S(1)}, u32[]{:S(2)}, u32[]{:S(2)}) collective-permute-start(f32[32,512]{1,0:T(8,128)S(1)} %constant_dynamic-slice_fusion.12), channel_id=1, source_target_pairs={{0,16},{8,24},{16,0},{24,8},{1,17},{9,25},{17,1},{25,9},{2,18},{10... | collective-permute-start | bytes 196616 | tf_op jit(solution)/shard_map/while/body/eval_jaxpr/ppermute | solution.py:18
  298.8 5.1 %collective-permute-start.7 = (f32[16]{0:T(128)S(1)}, f32[16]{0:T(128)S(1)}, u32[]{:S(2)}, u32[]{:S(2)}) collective-permute-start(f32[16]{0:T(128)S(1)} %dynamic_slice.134), channel_id=1, source_target_pairs={{0,4},{4,0},{1,5},{5,1},{2,6},{6,2},{3,7},{7,3},{8,12},{12,8},{9,1... | collective-permute-start | bytes 200 | tf_op jit(solution)/shard_map/while/body/eval_jaxpr/ppermute | solution.py:18
  301.9 5.5 %collective-permute-start.4 = (f32[16,512]{1,0:T(8,128)S(1)}, f32[16,512]{1,0:T(8,128)S(1)}, u32[]{:S(2)}, u32[]{:S(2)}) collective-permute-start(f32[16,512]{1,0:T(8,128)S(1)} %constant_dynamic-slice_fusion.13), channel_id=1, source_target_pairs={{0,4},{4,0},{1,5},{5,1},{2,6},{6,2},{3,7},{7,3},{8,12},{12,8},{9,1... | collective-permute-start | bytes 98312 | tf_op jit(solution)/shard_map/while/body/eval_jaxpr/ppermute | solution.py:18
  307.5 5.4 %collective-permute-start.8 = (f32[16,512]{1,0:T(8,128)S(1)}, f32[16,512]{1,0:T(8,128)S(1)}, u32[]{:S(2)}, u32[]{:S(2)}) collective-permute-start(f32[16,512]{1,0:T(8,128)S(1)} %add_divide_fusion.2), channel_id=1, source_target_pairs={{0,4},{4,0},{1,5},{5,1},{2,6},{6,2},{3,7},{7,3},{8,12},{12,8},{9,1... | collective-permute-start | bytes 98312 | tf_op jit(solution)/shard_map/while/body/eval_jaxpr/ppermute | solution.py:18
  313.0 5.9 %collective-permute-start.9 = (f32[32,512]{1,0:T(8,128)S(1)}, f32[32,512]{1,0:T(8,128)S(1)}, u32[]{:S(2)}, u32[]{:S(2)}) collective-permute-start(f32[32,512]{1,0:T(8,128)S(1)} %maximum_select_fusion.8), channel_id=1, source_target_pairs={{0,16},{8,24},{16,0},{24,8},{1,17},{9,25},{17,1},{25,9},{2,18},{10... | collective-permute-start | bytes 196616 | tf_op jit(solution)/shard_map/while/body/eval_jaxpr/ppermute | solution.py:18
  318.8 5.1 %collective-permute-start.10 = (f32[64,512]{1,0:T(8,128)S(1)}, f32[64,512]{1,0:T(8,128)S(1)}, u32[]{:S(2)}, u32[]{:S(2)}) collective-permute-start(f32[64,512]{1,0:T(8,128)S(1)} %maximum_select_fusion.9), channel_id=1, source_target_pairs={{0,8},{8,0},{16,24},{24,16},{1,9},{9,1},{17,25},{25,17},{2,10},{10... | collective-permute-start | bytes 393224 | tf_op jit(solution)/shard_map/while/body/eval_jaxpr/ppermute | solution.py:18
Sparse Core Ops, SparseCore 0:
  99.4 45.0 reduce-scatter.1
  181.8 39.1 all-gather.1
  245.9 41.8 reduce-scatter.1
  324.8 39.1 all-gather.1
